TPU v7x, 512 devices: a whole 4x8x8 slice. The times are simulated.
512 devices in a mesh: kv: 16 (over z, core), ep: 32 (over x, y).
Axes of the slice: x: 4, y: 8, z: 8, core: 2. Of those that a mesh axis runs over, the one named last changes fastest.
Arguments:
- queries: bfloat16 [32, 64, 2048], P('ep'), may hold values from -12 to 12
- new_keys: bfloat16 [32, 64, 512], P('ep'), may hold values from -12 to 12
- new_values: bfloat16 [32, 64, 512], P('ep'), may hold values from -6 to 6
- cache_keys: bfloat16 [32, 64, 128, 512], P('ep', 'kv'), may hold values from -12 to 12
- cache_values: bfloat16 [32, 64, 128, 512], P('ep', 'kv'), may hold values from -10 to 10
- page_table: int32 [32, 64], P('ep'), may hold values from 0 to 63, each once within a row
- cached_len: int32 [32], P('ep'), may hold values from 1 to 8192, 65536 in all
- moe_rows: bfloat16 [1024, 4096], P('ep'), may hold values from -6 to 6
- expert_ids: int32 [1024, 2], P('ep'), may hold values from 0 to 7, all different within a row; in each aligned block of 32 rows (0 to 31, 32 to 63, ...) at most 16 rows name the same one
- gate_probs: float32 [1024, 2], P('ep'), may hold values from 0.1 to 0.9
- w_gate: bfloat16 [32, 4096, 2048], P('ep', None, 'kv'), may hold values from -0.09375 to 0.09375
- w_up: bfloat16 [32, 4096, 2048], P('ep', None, 'kv'), may hold values from -0.09375 to 0.09375
- w_down: bfloat16 [32, 2048, 4096], P('ep', 'kv'), may hold values from -0.09375 to 0.09375
Outputs:
- attn_out: bfloat16 [32, 64, 2048], P('ep')
- moe_out: bfloat16 [1024, 4096], P('ep', 'kv')
Inputs may be any that keep to these rules, and one draw needn't show every extreme that they name: `page_table`: each row is a permutation of the 64 slots of its request. `cached_len`: cached positions at or past a request's length hold no data. `expert_ids`: each row names 2 different experts; among the 32 rows of one ep index no expert is named more than 16 times, and this bound is reached.
All inputs are finite; a program needn't handle non-finite values. No bound on the sum of `cached_len` on one device may be relied on, other than what follows from the above.
Results may differ from a plain program's by a relative error of at most 0.0085.
Values may be sent and summed in bfloat16 or wider, within the bound.
No kernel may reach another device: no remote copies, remote signals or barrier semaphores. Data moves between devices by JAX's collectives and lax.ppermute only.
A program may use at most 128 MiB of HBM per device.

v0:
```python
import math

import jax
import jax.numpy as jnp
from jax import lax
from jax.sharding import PartitionSpec as P

HD = 128
EXPERTS = 8
TOP = 2
HQ = 16
KVH = 4
PAGE = 128
POOL_DEV = 4
CAP = 16


ROPE_BASE = 10000.0
MASKED = -1e30


def merged(part, axis, combine):
    gathered = jax.tree.map(lambda a: lax.all_gather(a, axis), part)

    def take(source):
        return jax.tree.map(lambda a: lax.dynamic_index_in_dim(a, source, 0, False), gathered)

    return lax.fori_loop(
        1, lax.axis_size(axis), lambda source, state: combine(state, take(source)), take(0)
    )


def rotary(values, positions):
    half_width = values.shape[-1] // 2
    indices = jnp.arange(half_width, dtype=jnp.float32)
    frequency = jnp.power(ROPE_BASE, -2.0 * indices / values.shape[-1])
    angles = positions.astype(jnp.float32)[:, None] * frequency[None, :]
    cosine = jnp.cos(angles)[:, None, :]
    sine_part = jnp.sin(angles)[:, None, :]
    lower_half = values[..., :half_width]
    upper_half = values[..., half_width:]
    return jnp.concatenate(
        [
            lower_half * cosine - upper_half * sine_part,
            upper_half * cosine + lower_half * sine_part,
        ],
        axis=-1,
    )


def combine_parts(first, second):
    high_first, total_first, blend_first = first
    high_second, total_second, blend_second = second
    highest = jnp.maximum(high_first, high_second)
    factor_first = jnp.exp(high_first - highest)
    factor_second = jnp.exp(high_second - highest)
    row_count, head_count = highest.shape
    blended = (
        blend_first.reshape(row_count, head_count, -1) * factor_first[..., None]
        + blend_second.reshape(row_count, head_count, -1) * factor_second[..., None]
    )
    return (
        highest,
        total_first * factor_first + total_second * factor_second,
        blended.reshape(blend_first.shape),
    )


def on_device(
    queries,
    new_keys,
    new_values,
    cache_keys,
    cache_values,
    page_table,
    cached_len,
    moe_rows,
    expert_ids,
    gate_probs,
    w_gate,
    w_up,
    w_down,
):
    kv_index = lax.axis_index("kv")
    kv_count = lax.axis_size("kv")
    all_rows = queries.shape[1]
    block_rows = all_rows // kv_count
    length = cached_len[0]
    group_size = HQ // KVH
    score_scale = 1.0 / math.sqrt(HD)
    slot_ids = kv_index * POOL_DEV + jnp.arange(POOL_DEV, dtype=jnp.int32)
    matches = (page_table[0][:, None] == slot_ids[None, :]).astype(jnp.int32)
    page_index = jnp.sum(
        matches * jnp.arange(page_table.shape[1], dtype=jnp.int32)[:, None], axis=0
    )
    cached_pos = (page_index[:, None] * PAGE + jnp.arange(PAGE, dtype=jnp.int32)[None, :]).reshape(
        -1
    )
    block_start = kv_index * block_rows
    own_pos = length + block_start + jnp.arange(block_rows, dtype=jnp.int32)
    key_block = lax.dynamic_slice_in_dim(new_keys[0], block_start, block_rows, 0)
    value_block = lax.dynamic_slice_in_dim(new_values[0], block_start, block_rows, 0)
    own_keys = rotary(key_block.astype(jnp.float32).reshape(block_rows, KVH, HD), own_pos).astype(
        jnp.bfloat16
    )
    local_keys = jnp.concatenate([cache_keys[0].reshape(-1, KVH, HD), own_keys], axis=0)
    local_values = jnp.concatenate(
        [cache_values[0].reshape(-1, KVH, HD), value_block.reshape(block_rows, KVH, HD)], axis=0
    )
    key_pos = jnp.concatenate([cached_pos, own_pos])
    live_keys = jnp.concatenate([cached_pos < length, jnp.ones((block_rows,), jnp.bool_)])
    positions = length + jnp.arange(all_rows, dtype=jnp.int32)
    rotated = rotary(queries[0].astype(jnp.float32).reshape(all_rows, HQ, HD), positions).astype(
        jnp.bfloat16
    )
    grouped = rotated.reshape(all_rows, KVH, group_size, HD)
    scores = (
        jnp.einsum("nkgd,mkd->nkgm", grouped, local_keys, preferred_element_type=jnp.float32)
        * score_scale
    )
    usable = (live_keys[None, :] & (key_pos[None, :] <= positions[:, None]))[:, None, None, :]
    scores = jnp.where(usable, scores, MASKED)
    part_high = jnp.max(scores, axis=-1)
    weights = jnp.where(usable, jnp.exp(scores - part_high[..., None]), 0.0)
    part_total = jnp.sum(weights, axis=-1)
    part_blend = jnp.einsum(
        "nkgm,mkd->nkgd",
        weights.astype(jnp.bfloat16),
        local_values,
        preferred_element_type=jnp.float32,
    )
    partials = (
        part_high.reshape(all_rows, HQ),
        part_total.reshape(all_rows, HQ),
        part_blend.reshape(all_rows, HQ * HD),
    )
    highest, row_total, blended = merged(partials, "kv", combine_parts)
    attn_out = (
        (blended.reshape(all_rows, HQ, HD) / row_total[..., None])
        .reshape(1, all_rows, HQ * HD)
        .astype(jnp.bfloat16)
    )
    ep_count = lax.axis_size("ep")
    share_count = ep_count // EXPERTS
    tok_rows = moe_rows.shape[0]
    slot_total = ep_count * CAP
    flat_ids = expert_ids.reshape(-1)
    one_hot = (flat_ids[:, None] == jnp.arange(EXPERTS, dtype=jnp.int32)[None, :]).astype(jnp.int32)
    earlier = jnp.cumsum(one_hot, axis=0) - one_hot
    slot_rank = jnp.sum(earlier * one_hot, axis=1)
    slot_index = jnp.arange(slot_total, dtype=jnp.int32)
    dest_expert = slot_index // CAP // share_count
    dest_slot = slot_index % CAP
    matched = (flat_ids[None, :] == dest_expert[:, None]) & (
        slot_rank[None, :] == dest_slot[:, None]
    )
    select = jnp.sum(matched.astype(jnp.float32).reshape(slot_total, tok_rows, TOP), axis=2).astype(
        jnp.bfloat16
    )
    weight_map = jnp.sum(
        jnp.where(matched, gate_probs.reshape(-1)[None, :], 0.0).reshape(slot_total, tok_rows, TOP),
        axis=2,
    )
    outgoing = (
        jnp.dot(select, moe_rows, preferred_element_type=jnp.float32)
        .astype(jnp.bfloat16)
        .reshape(ep_count, CAP, -1)
    )
    arrived = lax.all_to_all(outgoing, "ep", split_axis=0, concat_axis=0, tiled=True).reshape(
        slot_total, -1
    )
    gate_proj = jnp.dot(arrived, w_gate[0], preferred_element_type=jnp.float32)
    up_proj = jnp.dot(arrived, w_up[0], preferred_element_type=jnp.float32)
    hidden = (jax.nn.silu(gate_proj) * up_proj).astype(jnp.bfloat16)
    out_width = w_down.shape[2] // kv_count
    down_split = w_down[0].reshape(w_down.shape[1], kv_count, out_width)
    down_cols = lax.all_to_all(down_split, "kv", split_axis=1, concat_axis=0, tiled=True).reshape(
        -1, out_width
    )
    summed = jnp.dot(
        lax.all_gather(hidden, "kv", axis=1, tiled=True),
        down_cols,
        preferred_element_type=jnp.float32,
    )
    returned = (
        lax.all_to_all(
            summed.reshape(ep_count, CAP, -1).astype(jnp.bfloat16),
            "ep",
            split_axis=0,
            concat_axis=0,
            tiled=True,
        )
        .astype(jnp.float32)
        .reshape(slot_total, -1)
    )
    moe_out = jnp.dot(
        weight_map.T, returned, precision=lax.Precision.HIGHEST, preferred_element_type=jnp.float32
    ).astype(jnp.bfloat16)
    return (attn_out, moe_out)


def solution(mesh):
    return jax.shard_map(
        on_device,
        mesh=mesh,
        in_specs=(
            P("ep", None, None),
            P("ep", None, None),
            P("ep", None, None),
            P("ep", "kv", None, None),
            P("ep", "kv", None, None),
            P("ep", None),
            P("ep"),
            P("ep", None),
            P("ep", None),
            P("ep", None),
            P("ep", None, "kv"),
            P("ep", None, "kv"),
            P("ep", "kv", None),
        ),
        out_specs=(P("ep", None, None), P("ep", "kv")),
        check_vma=False,
    )
```

profile of v0, /device:TPU:1, one launch (start us, length us, event | category | flops | bytes accessed | tf_op | source)
XLA Modules:
  0.0 284.0 jit_solution(5398753687239622973)
XLA Ops:
  9.6 2.2 convolution_convert_fusion
  11.8 102.2 %all_to_all.25 = bf16[32,16,4096]{2,1,0:T(8,128)(2,1)S(1)} all-to-all(bf16[32,16,4096]{2,1,0:T(8,128)(2,1)S(1)} %bitcast.135), channel_id=1, replica_groups=mesh['kv'=16,'ep'=32] {'ep'}, dimensions={0} | all-to-all | bytes 8388608 | tf_op jit(solution)/shard_map/all_to_all | solution.py:169
  113.9 1.3 fusion.14
  115.2 1.9 fusion.12
  124.2 1.0 all_gather_reshape.11
  125.5 1.3 copy.58
  126.8 15.6 %all-to-all-start.1 = ((bf16[128,16,256]{2,0,1:T(8,128)(2,1)}), bf16[128,16,256]{2,0,1:T(8,128)(2,1)S(1)}, u32[]{:S(2)}, u32[]{:S(2)}) async-start(bf16[128,16,256]{2,0,1:T(8,128)(2,1)} %copy.58), calls=%async_computation.1 | async-start | bytes 2097152 | tf_op jit(solution)/shard_map/all_to_all | solution.py:177
  142.3 2.6 fusion.5
  145.0 28.9 %all-to-all-done.1 = bf16[128,16,256]{2,0,1:T(8,128)(2,1)S(1)} async-done(((bf16[128,16,256]{2,0,1:T(8,128)(2,1)}), bf16[128,16,256]{2,0,1:T(8,128)(2,1)S(1)}, u32[]{:S(2)}, u32[]{:S(2)}) %all-to-all-start.1) | async-done | bytes 1048608 | tf_op jit(solution)/shard_map/all_to_all | solution.py:177
  173.9 6.0 %all-gather.5.cloned.1.call-done = bf16[512,2048]{1,0:T(8,128)(2,1)} async-done(((bf16[512,128]{1,0:T(8,128)(2,1)}), bf16[512,2048]{1,0:T(8,128)(2,1)}) %all-gather.5.cloned.1.call-update) | async-done | bytes 2097168 | tf_op jit(solution)/shard_map/all_gather | solution.py:181
  179.9 3.0 %convolution_convert_fusion.1 = bf16[32,16,256]{2,1,0:T(8,128)(2,1)} fusion(bf16[32,16,2048]{2,1,0:T(8,128)(2,1)} %bitcast.146, bf16[2048,256,1]{1,0,2:T(8,128)(2,1)S(1)} %bitcast.140), kind=kOutput, calls=%fused_computation.18 | convolution fusion | flops 537001984 | bytes 3407872 | tf_op jit(solution)/shard_map/dot_general | solution.py:180
  182.9 10.4 %all-to-all-start.2 = ((bf16[32,16,256]{2,1,0:T(8,128)(2,1)}), bf16[32,16,256]{2,1,0:T(8,128)(2,1)S(1)}, u32[]{:S(2)}, u32[]{:S(2)}) async-start(bf16[32,16,256]{2,1,0:T(8,128)(2,1)} %convolution_convert_fusion.1), calls=%async_computation.2 | async-start | bytes 524288 | tf_op jit(solution)/shard_map/all_to_all | solution.py:186
  193.4 18.7 %all_gather.12 = f32[16,64,16]{1,2,0:T(8,128)S(1)} all-gather(f32[1,64,16]{1,2,0:T(8,128)S(1)} %bitcast.144), channel_id=1, replica_groups=mesh['kv'=16,'ep'=32] {'kv'}, dimensions={0}, use_global_device_ids=true | all-gather | bytes 69632 | tf_op jit(solution)/shard_map/all_gather | solution.py:23
  212.1 15.8 %all_gather.13 = f32[16,64,16]{1,2,0:T(8,128)S(1)} all-gather(f32[1,64,16]{1,2,0:T(8,128)S(1)} %bitcast.145), channel_id=1, replica_groups=mesh['kv'=16,'ep'=32] {'kv'}, dimensions={0}, use_global_device_ids=true | all-gather | bytes 69632 | tf_op jit(solution)/shard_map/all_gather | solution.py:23
  228.8 13.1 %all-gather.3.cloned.1.call-done = f32[16,64,2048]{2,1,0:T(8,128)} async-done(((f32[1,64,2048]{2,1,0:T(8,128)}), f32[16,64,2048]{2,1,0:T(8,128)}) %all-gather.3.cloned.1.call-update) | async-done | bytes 8388624 | tf_op jit(solution)/shard_map/all_gather | solution.py:23
  241.8 1.1 slice_bitcast_fusion
  242.9 33.0 %while.19 = (s32[]{:T(128)}, f32[64,16]{0,1:T(8,128)S(1)}, f32[64,16]{0,1:T(8,128)S(1)}, f32[64,2048]{1,0:T(8,128)S(1)}, f32[16,64,16]{1,2,0:T(8,128)S(1)}, /*in...) while((s32[]{:T(128)}, f32[64,16]{0,1:T(8,128)S(1)}, ...), condition=%wide.region_4.5_spmd, body=%wide.region_3.4_spmd.sunk | while | flops 399365 | bytes 3727511 | solution.py:28
  243.5 1.6 fusion.62
  245.7 1.6 fusion.62
  247.9 1.6 fusion.62
  250.1 1.6 fusion.62
  252.3 1.6 fusion.62
  254.5 1.6 fusion.62
  256.7 1.6 fusion.62
  258.9 1.6 fusion.62
  261.1 1.6 fusion.62
  263.3 1.6 fusion.62
  265.5 1.6 fusion.62
  267.7 1.6 fusion.62
  269.9 1.6 fusion.62
  272.1 1.6 fusion.62
  274.3 1.6 fusion.62
  (140 shorter events, 19.4 us)
Async XLA Ops:
  7.2 106.8 %copy-start = (bf16[1,4096,128]{2,1,0:T(8,128)(2,1)S(1)}, bf16[1,4096,128]{2,1,0:T(8,128)(2,1)}, u32[]{:S(2)}) copy-start(bf16[1,4096,128]{2,1,0:T(8,128)(2,1)} %param.25) | copy-start | bytes 3145732
  7.2 172.8 %all-gather.5.cloned.1.call-start = ((), (), s32[]{:S(2)}) async-start(), calls=%async_computation.4 | async-start | bytes 2228224 | tf_op jit(solution)/shard_map/all_gather | solution.py:181
  113.9 1.3 copy-start.7
  115.2 2.7 copy-start.6
  115.2 2.9 %copy-start.3 = (bf16[1,4,128,512]{3,2,1,0:T(8,128)(2,1)S(1)}, bf16[1,4,128,512]{3,2,1,0:T(8,128)(2,1)}, u32[]{:S(2)}) copy-start(bf16[1,4,128,512]{3,2,1,0:T(8,128)(2,1)} %param.18) | copy-start | bytes 1572868
  117.1 1.9 copy-start.4
  117.2 124.7 %all-gather.3.cloned.1.call-start = ((), (), s32[]{:S(2)}) async-start(), calls=%async_computation.3 | async-start | bytes 8912896 | tf_op jit(solution)/shard_map/all_gather | solution.py:23
  118.0 1.3 copy-start.8
  119.2 2.3 copy-start.5
  122.3 1.6 copy-start.1
  123.8 1.4 copy-start.2
  126.8 47.1 %all-to-all-start.1 = ((bf16[128,16,256]{2,0,1:T(8,128)(2,1)}), bf16[128,16,256]{2,0,1:T(8,128)(2,1)S(1)}, u32[]{:S(2)}, u32[]{:S(2)}) async-start(bf16[128,16,256]{2,0,1:T(8,128)(2,1)} %copy.58), calls=%async_computation.1 | async-start | bytes 2097152 | tf_op jit(solution)/shard_map/all_to_all | solution.py:177
  182.9 45.0 %all-to-all-start.2 = ((bf16[32,16,256]{2,1,0:T(8,128)(2,1)}), bf16[32,16,256]{2,1,0:T(8,128)(2,1)S(1)}, u32[]{:S(2)}, u32[]{:S(2)}) async-start(bf16[32,16,256]{2,1,0:T(8,128)(2,1)} %convolution_convert_fusion.1), calls=%async_computation.2 | async-start | bytes 524288 | tf_op jit(solution)/shard_map/all_to_all | solution.py:186
Sparse Core Ops, SparseCore 0:
  117.3 62.6 all-gather.4
  182.1 59.7 all-gather.2
where the time goes:
time: 285 us; the launch traced here: 284 us
  blocking collectives  137 us (48%)
  waiting for transfers between devices  48.1 us (17%)
  other arithmetic  30.8 us (11%)
  starting transfers between devices  26.1 us (9%)
  local copies, waits for them, and re-layouts  16 us (6%)
  between operations  15 us (5%)
  matrix products  10.8 us (4%)
    all_to_all x1, blocking collectives, on_device(): lax.all_to_all(outgoing, 'ep', split_axis=0, concat_axis=0, tiled=True)  102 us
    all_gather x2, blocking collectives, merged(): gathered = jax.tree.map(lambda a: lax.all_gather(a, axis), part)  34.5 us
    all_to_all x1, waiting for transfers between devices, on_device(): lax.all_to_all(down_split, 'kv', split_axis=1, concat_axis=0, tiled=True)  28.9 us
    add x15, other arithmetic, combine_parts(): blend_first.reshape(row_count, head_count, -1) * factor_first[..., None]  23.9 us
    all_to_all x1, starting transfers between devices, on_device(): lax.all_to_all(down_split, 'kv', split_axis=1, concat_axis=0, tiled=True)  15.6 us
    all_gather x1, waiting for transfers between devices, merged(): gathered = jax.tree.map(lambda a: lax.all_gather(a, axis), part)  13.1 us
    all_to_all x1, starting transfers between devices, on_device(): lax.all_to_all(summed.reshape(ep_count, CAP, -1).astype(jnp.bfloat16), 'e...  10.4 us
    all_gather x1, waiting for transfers between devices, on_device(): lax.all_gather(hidden, 'kv', axis=1, tiled=True)  6.04 us
  transfers between devices with their start and end apart: 4, of which 3 were waited for; matrix products, arithmetic and copies ran while one was open for 5% of the time, Pallas kernels for 0%

commit v1 on v0

--- a/solution.py
+++ b/solution.py
@@ -19,17 +19,6 @@
 MASKED = -1e30
 
 
-def merged(part, axis, combine):
-    gathered = jax.tree.map(lambda a: lax.all_gather(a, axis), part)
-
-    def take(source):
-        return jax.tree.map(lambda a: lax.dynamic_index_in_dim(a, source, 0, False), gathered)
-
-    return lax.fori_loop(
-        1, lax.axis_size(axis), lambda source, state: combine(state, take(source)), take(0)
-    )
-
-
 def rotary(values, positions):
     half_width = values.shape[-1] // 2
     indices = jnp.arange(half_width, dtype=jnp.float32)
@@ -45,24 +34,6 @@
             upper_half * cosine + lower_half * sine_part,
         ],
         axis=-1,
-    )
-
-
-def combine_parts(first, second):
-    high_first, total_first, blend_first = first
-    high_second, total_second, blend_second = second
-    highest = jnp.maximum(high_first, high_second)
-    factor_first = jnp.exp(high_first - highest)
-    factor_second = jnp.exp(high_second - highest)
-    row_count, head_count = highest.shape
-    blended = (
-        blend_first.reshape(row_count, head_count, -1) * factor_first[..., None]
-        + blend_second.reshape(row_count, head_count, -1) * factor_second[..., None]
-    )
-    return (
-        highest,
-        total_first * factor_first + total_second * factor_second,
-        blended.reshape(blend_first.shape),
     )
 
 
@@ -121,7 +92,8 @@
     usable = (live_keys[None, :] & (key_pos[None, :] <= positions[:, None]))[:, None, None, :]
     scores = jnp.where(usable, scores, MASKED)
     part_high = jnp.max(scores, axis=-1)
-    weights = jnp.where(usable, jnp.exp(scores - part_high[..., None]), 0.0)
+    highest = lax.pmax(part_high, "kv")
+    weights = jnp.where(usable, jnp.exp(scores - highest[..., None]), 0.0)
     part_total = jnp.sum(weights, axis=-1)
     part_blend = jnp.einsum(
         "nkgm,mkd->nkgd",
@@ -129,14 +101,14 @@
         local_values,
         preferred_element_type=jnp.float32,
     )
-    partials = (
-        part_high.reshape(all_rows, HQ),
-        part_total.reshape(all_rows, HQ),
-        part_blend.reshape(all_rows, HQ * HD),
+    total_row = jnp.pad(part_total.reshape(1, -1), ((0, 0), (0, HQ * HD - all_rows * HQ)))
+    packed = lax.psum(
+        jnp.concatenate([part_blend.reshape(all_rows, HQ * HD), total_row], axis=0), "kv"
     )
-    highest, row_total, blended = merged(partials, "kv", combine_parts)
+    row_total = packed[all_rows, : all_rows * HQ].reshape(all_rows, HQ)
+    blended = packed[:all_rows].reshape(all_rows, HQ, HD)
     attn_out = (
-        (blended.reshape(all_rows, HQ, HD) / row_total[..., None])
+        (blended / row_total[..., None])
         .reshape(1, all_rows, HQ * HD)
         .astype(jnp.bfloat16)
     )
@@ -161,14 +133,17 @@
         jnp.where(matched, gate_probs.reshape(-1)[None, :], 0.0).reshape(slot_total, tok_rows, TOP),
         axis=2,
     )
+    col_width = moe_rows.shape[1] // kv_count
+    rows_cols = lax.dynamic_slice_in_dim(moe_rows, kv_index * col_width, col_width, 1)
     outgoing = (
-        jnp.dot(select, moe_rows, preferred_element_type=jnp.float32)
+        jnp.dot(select, rows_cols, preferred_element_type=jnp.float32)
         .astype(jnp.bfloat16)
         .reshape(ep_count, CAP, -1)
     )
-    arrived = lax.all_to_all(outgoing, "ep", split_axis=0, concat_axis=0, tiled=True).reshape(
+    arrived_cols = lax.all_to_all(outgoing, "ep", split_axis=0, concat_axis=0, tiled=True).reshape(
         slot_total, -1
     )
+    arrived = lax.all_gather(arrived_cols, "kv", axis=1, tiled=True)
     gate_proj = jnp.dot(arrived, w_gate[0], preferred_element_type=jnp.float32)
     up_proj = jnp.dot(arrived, w_up[0], preferred_element_type=jnp.float32)
     hidden = (jax.nn.silu(gate_proj) * up_proj).astype(jnp.bfloat16)

time: 285 us -> 278 us (0.975)
  waiting for transfers between devices: 48.1 us -> 162 us
  blocking collectives: 137 us -> 44.1 us
  other arithmetic: 30.8 us -> 8.52 us
  local copies, waits for them, and re-layouts: 16 us -> 9.25 us
  matrix products: 10.8 us -> 15.1 us
    psum x0 -> x1, waiting for transfers between devices: none -> 105 us  [on_device(): lax.psum(jnp.concatenate([part_blend.reshape(all_rows, HQ * HD), total_ro...]
    all_to_all x1, blocking collectives: 102 us -> 20.1 us  [on_device(): lax.all_to_all(outgoing, 'ep', split_axis=0, concat_axis=0, tiled=True)]
    all_gather x1, waiting for transfers between devices: 13.1 us -> 54.6 us  [on_device(): arrived = lax.all_gather(arrived_cols, 'kv', axis=1, tiled=True)]
    all_gather x2 -> x0, blocking collectives: 34.5 us -> none  [merged(): gathered = jax.tree.map(lambda a: lax.all_gather(a, axis), part)]
    all_to_all x1, waiting for transfers between devices: 28.9 us -> 0.01 us  [on_device(): lax.all_to_all(down_split, 'kv', split_axis=1, concat_axis=0, tiled=True)]
    add x30 -> x0, other arithmetic: 24.1 us -> none  [the longest x15 23.9 us: combine_parts(): blend_first.reshape(row_count, head_count, -1) * factor_first[..., None]]
    pmax x0 -> x1, blocking collectives: none -> 24 us  [on_device(): highest = lax.pmax(part_high, 'kv')]
    mul x30 -> x0, local copies, waits for them, and re-layouts: 5.76 us -> none  [the longest x15 2.92 us: combine_parts(): blend_first.reshape(row_count, head_count, -1) * factor_first[..., None]]
  transfers between devices with their start and end apart: 4 -> 5, of which waited for: 3 -> 3; matrix products, arithmetic and copies ran while one was open for 5% -> 10% of each run, Pallas kernels for 0% -> 0%
where the time goes in v1:
time: 278 us; the launch traced here: 277 us
  waiting for transfers between devices  162 us (58%)
  blocking collectives  44.1 us (16%)
  starting transfers between devices  23.6 us (8%)
  matrix products  15.1 us (5%)
  between operations  14.7 us (5%)
  local copies, waits for them, and re-layouts  9.25 us (3%)
  other arithmetic  8.52 us (3%)
    psum x1, waiting for transfers between devices, on_device(): lax.psum(jnp.concatenate([part_blend.reshape(all_rows, HQ * HD), total_ro...  105 us
    all_gather x1, waiting for transfers between devices, on_device(): arrived = lax.all_gather(arrived_cols, 'kv', axis=1, tiled=True)  54.6 us
    pmax x1, blocking collectives, on_device(): highest = lax.pmax(part_high, 'kv')  24 us
    all_to_all x1, blocking collectives, on_device(): lax.all_to_all(outgoing, 'ep', split_axis=0, concat_axis=0, tiled=True)  20.1 us
    all_to_all x1, starting transfers between devices, on_device(): lax.all_to_all(down_split, 'kv', split_axis=1, concat_axis=0, tiled=True)  14.2 us
    all_to_all x1, starting transfers between devices, on_device(): lax.all_to_all(summed.reshape(ep_count, CAP, -1).astype(jnp.bfloat16), 'e...  9.28 us
  transfers between devices with their start and end apart: 5, of which 3 were waited for; matrix products, arithmetic and copies ran while one was open for 10% of the time, Pallas kernels for 0%

profile of v1, /device:TPU:1, one launch (start us, length us, event | category | flops | bytes accessed | tf_op | source)
XLA Modules:
  0.0 277.3 jit_solution(767339811898479776)
XLA Ops:
  7.2 0.8 copy.46
  8.7 0.8 convert_reduce_fusion
  9.6 1.0 convolution_convert_fusion
  10.5 20.1 %all_to_all.25 = bf16[32,16,256]{2,1,0:T(8,128)(2,1)} all-to-all(bf16[32,16,256]{2,1,0:T(8,128)(2,1)S(1)} %bitcast.94), channel_id=1, replica_groups=mesh['kv'=16,'ep'=32] {'ep'}, dimensions={0} | all-to-all | bytes 524288 | tf_op jit(solution)/shard_map/all_to_all | solution.py:143
  30.6 1.5 copy.55
  32.1 1.3 copy.48
  33.5 14.2 %all-to-all-start.1 = ((bf16[128,16,256]{2,0,1:T(8,128)(2,1)}), bf16[128,16,256]{2,0,1:T(8,128)(2,1)S(1)}, u32[]{:S(2)}, u32[]{:S(2)}) async-start(bf16[128,16,256]{2,0,1:T(8,128)(2,1)} %copy.48), calls=%async_computation.1 | async-start | bytes 2097152 | tf_op jit(solution)/shard_map/all_to_all | solution.py:152
  48.5 1.2 reshape_squeeze.10
  49.7 0.9 copy.41
  50.7 54.6 %all-gather.3.cloned.1.call-done = bf16[512,4096]{1,0:T(8,128)(2,1)} async-done(((bf16[512,256]{1,0:T(8,128)(2,1)}), bf16[512,4096]{1,0:T(8,128)(2,1)}) %all-gather.3.cloned.1.call-update) | async-done | bytes 4194320 | tf_op jit(solution)/shard_map/all_gather | solution.py:146
  105.4 3.6 %fusion.11 = f32[512,128]{1,0:T(8,128)S(1)} fusion(bf16[512,4096]{1,0:T(8,128)(2,1)} %all-gather.3.cloned.1.call-done, bf16[1,4096,128]{2,1,0:T(8,128)(2,1)S(1)} %copy-done), kind=kOutput, calls=%fused_computation.14 | convolution fusion | flops 536870912 | bytes 5505024 | tf_op jit(solution)/shard_map/dot_general | solution.py:147
  109.1 1.9 fusion.9
  111.3 0.7 bitcast_convert_fusion
  112.2 0.2 multiply_cosine_fusion
  112.5 0.2 fusion.48
  112.7 0.3 subtract_convert_fusion
  113.1 2.2 fusion
  115.3 24.0 %pmax.7 = f32[64,4,4]{0,2,1:T(4,128)S(1)} all-reduce(f32[64,4,4]{0,2,1:T(4,128)S(1)} %get-tuple-element.14), channel_id=1, replica_groups=mesh['kv'=16,'ep'=32] {'kv'}, use_global_device_ids=true, to_apply=%region_2.3 | all-reduce | flops 1024 | bytes 8192 | tf_op jit(solution)/shard_map/pmax | solution.py:95
  139.3 2.6 fusion.1
  142.5 0.7 dynamic-slice_bitcast_fusion
  143.2 2.5 fusion.6
  145.7 0.3 copy.44
  146.1 0.2 reshape.298
  146.3 0.9 select_maximum_fusion
  147.2 2.6 all-gather.5.cloned.1.call-done
  149.8 3.0 %convolution_convert_fusion.1 = bf16[32,16,256]{2,1,0:T(8,128)(2,1)} fusion(bf16[32,16,2048]{2,1,0:T(8,128)(2,1)} %bitcast.97, bf16[2048,256,1]{1,0,2:T(8,128)(2,1)S(1)} %bitcast.91), kind=kOutput, calls=%fused_computation.9 | convolution fusion | flops 537001984 | bytes 3407872 | tf_op jit(solution)/shard_map/dot_general | solution.py:155
  152.8 9.3 %all-to-all-start.2 = ((bf16[32,16,256]{2,1,0:T(8,128)(2,1)}), bf16[32,16,256]{2,1,0:T(8,128)(2,1)S(1)}, u32[]{:S(2)}, u32[]{:S(2)}) async-start(bf16[32,16,256]{2,1,0:T(8,128)(2,1)} %convolution_convert_fusion.1), calls=%async_computation.2 | async-start | bytes 524288 | tf_op jit(solution)/shard_map/all_to_all | solution.py:161
  162.1 104.8 %all-reduce.4.cloned.1.call-done = f32[65,2048]{1,0:T(8,128)} async-done(((f32[65,2048]{1,0:T(8,128)}), f32[65,2048]{1,0:T(8,128)}) %all-reduce.4.cloned.1.call-update) | async-done | bytes 532496 | tf_op jit(solution)/shard_map/psum | solution.py:105
  266.9 0.8 slice_reduce_fusion
  267.8 0.2 div.46
  268.0 1.9 fusion.24
  269.9 0.9 convolution_convert_fusion.2
  (49 shorter events, 2.4 us)
Async XLA Ops:
  7.2 98.2 %copy-start = (bf16[1,4096,128]{2,1,0:T(8,128)(2,1)S(1)}, bf16[1,4096,128]{2,1,0:T(8,128)(2,1)}, u32[]{:S(2)}) copy-start(bf16[1,4096,128]{2,1,0:T(8,128)(2,1)} %param.23) | copy-start | bytes 3145732
  7.2 98.2 %all-gather.3.cloned.1.call-start = ((), (), s32[]{:S(2)}) async-start(), calls=%async_computation.4 | async-start | bytes 4456448 | tf_op jit(solution)/shard_map/all_gather | solution.py:146
  32.1 16.2 %copy-start.4 = (bf16[1,64,2048]{2,1,0:T(8,128)(2,1)S(1)}, bf16[1,64,2048]{2,1,0:T(8,128)(2,1)}, u32[]{:S(2)}) copy-start(bf16[1,64,2048]{2,1,0:T(8,128)(2,1)} %param.13) | copy-start | bytes 786436
  33.5 17.1 %copy-start.6 = (s32[1,64]{1,0:T(1,128)S(1)}, s32[1,64]{1,0:T(1,128)}, u32[]{:S(2)}) copy-start(s32[1,64]{1,0:T(1,128)} %param.18) | copy-start | bytes 772
  33.5 113.7 %all-to-all-start.1 = ((bf16[128,16,256]{2,0,1:T(8,128)(2,1)}), bf16[128,16,256]{2,0,1:T(8,128)(2,1)S(1)}, u32[]{:S(2)}, u32[]{:S(2)}) async-start(bf16[128,16,256]{2,0,1:T(8,128)(2,1)} %copy.48), calls=%async_computation.1 | async-start | bytes 2097152 | tf_op jit(solution)/shard_map/all_to_all | solution.py:152
  47.6 102.2 %all-gather.5.cloned.1.call-start = ((), (), s32[]{:S(2)}) async-start(), calls=%async_computation.5 | async-start | bytes 2228224 | tf_op jit(solution)/shard_map/all_gather | solution.py:156
  105.4 3.6 %copy-start.1 = (bf16[512,4096]{1,0:T(8,128)(2,1)S(1)}, bf16[512,4096]{1,0:T(8,128)(2,1)}, u32[]{:S(2)}) copy-start(bf16[512,4096]{1,0:T(8,128)(2,1)} %all-gather.3.cloned.1.call-done) | copy-start | bytes 12582916
  105.4 3.7 %copy-start.5 = (bf16[1,4096,128]{2,1,0:T(8,128)(2,1)S(1)}, bf16[1,4096,128]{2,1,0:T(8,128)(2,1)}, u32[]{:S(2)}) copy-start(bf16[1,4096,128]{2,1,0:T(8,128)(2,1)} %param.24) | copy-start | bytes 3145732
  111.0 2.0 copy-start.3
  111.0 155.9 %all-reduce.4.cloned.1.call-start = ((), (), s32[]{:S(2)}) async-start(), calls=%async_computation.3 | async-start | bytes 1179648 | tf_op jit(solution)/shard_map/psum | solution.py:105
  113.1 29.2 %copy-start.2 = (bf16[1,4,128,512]{3,2,1,0:T(8,128)(2,1)S(1)}, bf16[1,4,128,512]{3,2,1,0:T(8,128)(2,1)}, u32[]{:S(2)}) copy-start(bf16[1,4,128,512]{3,2,1,0:T(8,128)(2,1)} %param.17) | copy-start | bytes 1572868
  152.8 117.1 %all-to-all-start.2 = ((bf16[32,16,256]{2,1,0:T(8,128)(2,1)}), bf16[32,16,256]{2,1,0:T(8,128)(2,1)S(1)}, u32[]{:S(2)}, u32[]{:S(2)}) async-start(bf16[32,16,256]{2,1,0:T(8,128)(2,1)} %convolution_convert_fusion.1), calls=%async_computation.2 | async-start | bytes 524288 | tf_op jit(solution)/shard_map/all_to_all | solution.py:161
Sparse Core Ops, SparseCore 0:
  30.8 74.5 all-gather.2
  111.2 38.6 all-gather.4
  152.2 114.6 all-reduce.3

commit v2 on v1

--- a/solution.py
+++ b/solution.py
@@ -92,8 +92,7 @@
     usable = (live_keys[None, :] & (key_pos[None, :] <= positions[:, None]))[:, None, None, :]
     scores = jnp.where(usable, scores, MASKED)
     part_high = jnp.max(scores, axis=-1)
-    highest = lax.pmax(part_high, "kv")
-    weights = jnp.where(usable, jnp.exp(scores - highest[..., None]), 0.0)
+    weights = jnp.where(usable, jnp.exp(scores - part_high[..., None]), 0.0)
     part_total = jnp.sum(weights, axis=-1)
     part_blend = jnp.einsum(
         "nkgm,mkd->nkgd",
@@ -101,17 +100,26 @@
         local_values,
         preferred_element_type=jnp.float32,
     )
-    total_row = jnp.pad(part_total.reshape(1, -1), ((0, 0), (0, HQ * HD - all_rows * HQ)))
-    packed = lax.psum(
-        jnp.concatenate([part_blend.reshape(all_rows, HQ * HD), total_row], axis=0), "kv"
-    )
-    row_total = packed[all_rows, : all_rows * HQ].reshape(all_rows, HQ)
-    blended = packed[:all_rows].reshape(all_rows, HQ, HD)
-    attn_out = (
-        (blended / row_total[..., None])
-        .reshape(1, all_rows, HQ * HD)
-        .astype(jnp.bfloat16)
-    )
+    packed = jnp.concatenate(
+        [
+            part_blend.reshape(all_rows, HQ * HD),
+            part_high.reshape(all_rows, HQ),
+            part_total.reshape(all_rows, HQ),
+        ],
+        axis=1,
+    ).reshape(kv_count, block_rows, -1)
+    parts = lax.all_to_all(packed, "kv", split_axis=0, concat_axis=0, tiled=True).reshape(
+        kv_count, block_rows, -1
+    )
+    parts_blend = parts[..., : HQ * HD].reshape(kv_count, block_rows, HQ, HD)
+    parts_high = parts[..., HQ * HD : HQ * HD + HQ]
+    parts_total = parts[..., HQ * HD + HQ :]
+    highest = jnp.max(parts_high, axis=0)
+    factor = jnp.exp(parts_high - highest[None])
+    row_total = jnp.sum(parts_total * factor, axis=0)
+    blended = jnp.sum(parts_blend * factor[..., None], axis=0)
+    own_out = (blended / row_total[..., None]).reshape(block_rows, HQ * HD).astype(jnp.bfloat16)
+    attn_out = lax.all_gather(own_out, "kv", axis=0, tiled=True).reshape(1, all_rows, HQ * HD)
     ep_count = lax.axis_size("ep")
     share_count = ep_count // EXPERTS
     tok_rows = moe_rows.shape[0]

time: 278 us -> 198 us (0.71)
  waiting for transfers between devices: 162 us -> 97.5 us
  blocking collectives: 44.1 us -> 35.7 us
  starting transfers between devices: 23.6 us -> 18.6 us
    psum x1 -> x0, waiting for transfers between devices: 105 us -> none  [on_device(): lax.psum(jnp.concatenate([part_blend.reshape(all_rows, HQ * HD), total_ro...]
    all_to_all x1, waiting for transfers between devices: 0.01 us -> 26.9 us  [on_device(): lax.all_to_all(down_split, 'kv', split_axis=1, concat_axis=0, tiled=True)]
    pmax x1 -> x0, blocking collectives: 24 us -> none  [on_device(): highest = lax.pmax(part_high, 'kv')]
    all_to_all x0 -> x1, waiting for transfers between devices: none -> 19.1 us  [on_device(): lax.all_to_all(packed, 'kv', split_axis=0, concat_axis=0, tiled=True)]
    all_gather x0 -> x1, blocking collectives: none -> 15.6 us  [on_device(): lax.all_gather(own_out, 'kv', axis=0, tiled=True)]
    all_to_all x1, starting transfers between devices: 14.2 us -> 4.23 us  [on_device(): lax.all_to_all(down_split, 'kv', split_axis=1, concat_axis=0, tiled=True)]
    all_to_all x0 -> x1, starting transfers between devices: none -> 4.24 us  [on_device(): lax.all_to_all(packed, 'kv', split_axis=0, concat_axis=0, tiled=True)]
    all_gather x1, waiting for transfers between devices: 54.6 us -> 51.5 us  [on_device(): arrived = lax.all_gather(arrived_cols, 'kv', axis=1, tiled=True)]
  transfers between devices with their start and end apart: 5 -> 5, of which waited for: 3 -> 3; matrix products, arithmetic and copies ran while one was open for 10% -> 8% of each run, Pallas kernels for 0% -> 0%
where the time goes in v2:
time: 198 us; the launch traced here: 197 us
  waiting for transfers between devices  97.5 us (49%)
  blocking collectives  35.7 us (18%)
  starting transfers between devices  18.6 us (9%)
  matrix products  15.3 us (8%)
  between operations  15 us (8%)
  local copies, waits for them, and re-layouts  7.82 us (4%)
  other arithmetic  7.1 us (4%)
    all_gather x1, waiting for transfers between devices, on_device(): arrived = lax.all_gather(arrived_cols, 'kv', axis=1, tiled=True)  51.5 us
    all_to_all x1, waiting for transfers between devices, on_device(): lax.all_to_all(down_split, 'kv', split_axis=1, concat_axis=0, tiled=True)  26.9 us
    all_to_all x1, blocking collectives, on_device(): lax.all_to_all(outgoing, 'ep', split_axis=0, concat_axis=0, tiled=True)  20.1 us
    all_to_all x1, waiting for transfers between devices, on_device(): lax.all_to_all(packed, 'kv', split_axis=0, concat_axis=0, tiled=True)  19.1 us
    all_gather x1, blocking collectives, on_device(): lax.all_gather(own_out, 'kv', axis=0, tiled=True)  15.6 us
    all_to_all x1, starting transfers between devices, on_device(): lax.all_to_all(summed.reshape(ep_count, CAP, -1).astype(jnp.bfloat16), 'e...  10.1 us
    all_to_all x1, starting transfers between devices, on_device(): lax.all_to_all(packed, 'kv', split_axis=0, concat_axis=0, tiled=True)  4.24 us
    all_to_all x1, starting transfers between devices, on_device(): lax.all_to_all(down_split, 'kv', split_axis=1, concat_axis=0, tiled=True)  4.23 us
  transfers between devices with their start and end apart: 5, of which 3 were waited for; matrix products, arithmetic and copies ran while one was open for 8% of the time, Pallas kernels for 0%

profile of v2, /device:TPU:1, one launch (start us, length us, event | category | flops | bytes accessed | tf_op | source)
XLA Modules:
  0.0 197.0 jit_solution(15429339823385699277)
XLA Ops:
  7.3 0.8 copy.51
  8.7 0.8 convert_reduce_fusion
  9.6 1.0 convolution_convert_fusion
  10.5 20.1 %all_to_all.30 = bf16[32,16,256]{2,1,0:T(8,128)(2,1)} all-to-all(bf16[32,16,256]{2,1,0:T(8,128)(2,1)S(1)} %bitcast.99), channel_id=1, replica_groups=mesh['kv'=16,'ep'=32] {'ep'}, dimensions={0} | all-to-all | bytes 524288 | tf_op jit(solution)/shard_map/all_to_all | solution.py:151
  31.3 1.0 convert_bitcast_fusion
  32.9 0.7 bitcast_convert_fusion
  33.8 0.2 multiply_cosine_fusion
  34.0 0.2 fusion.50
  34.2 0.3 subtract_convert_fusion
  34.5 51.5 %all-gather.4.cloned.1.call-done = bf16[512,4096]{1,0:T(8,128)(2,1)} async-done(((bf16[512,256]{1,0:T(8,128)(2,1)}), bf16[512,4096]{1,0:T(8,128)(2,1)}) %all-gather.4.cloned.1.call-update) | async-done | bytes 4194320 | tf_op jit(solution)/shard_map/all_gather | solution.py:154
  86.0 3.6 %fusion.11 = f32[512,128]{1,0:T(8,128)S(1)} fusion(bf16[512,4096]{1,0:T(8,128)(2,1)} %all-gather.4.cloned.1.call-done, bf16[1,4096,128]{2,1,0:T(8,128)(2,1)S(1)} %copy-done), kind=kOutput, calls=%fused_computation.14 | convolution fusion | flops 536870912 | bytes 5505024 | tf_op jit(solution)/shard_map/dot_general | solution.py:155
  89.8 1.9 fusion.9
  92.0 0.7 copy-done.4
  92.9 2.2 %fusion = (f32[64,4,4]{0,2,1:T(4,128)S(1)}, f32[4,516,64,4]{1,2,3,0:T(8,128)}) fusion(pred[64,516]{1,0:T(8,128)(4,1)S(1)} %compare_and_fusion, bf16[64,4,4,64]{3,0,2,1:T(8,128)(2,1)S(1)} %bitcast.101, bf16[64,4,4,64]{3,0,2,1:T(8,128)(2,1)S(1)} %bitcast.100, bf16[4,4,64]{2,0,1:T(4,128)(2,1)S(1)} %get-tuple-element.11, ...), kind=kOutput, calls=%fused_computation.2 | convolution fusion | flops 138959872 | bytes 2941184 | tf_op jit(solution)/shard_map/nkgd,mkd->nkgm/dot_general | solution.py:89
  95.3 2.5 %fusion.6 = f32[64,4,4,128]{3,0,2,1:T(8,128)S(1)} fusion(f32[4,516,64,4]{1,2,3,0:T(8,128)} %get-tuple-element.17, f32[64,4,4]{0,2,1:T(4,128)S(1)} %get-tuple-element.16, pred[64,516]{1,0:T(8,128)(4,1)S(1)} %compare_and_fusion, bf16[4,4,128]{2,0,1:T(4,128)(2,1)S(1)} %get-tuple-element.23, bf16[512,4,128]{2,0,1:T(8,128)(2,1)S(1)} %copy.44), kind=kOutput, calls=%fused_computation.7 | convolution fusion | flops 138964992 | bytes 3203328 | tf_op jit(solution)/shard_map/nkgm,mkd->nkgd/dot_general | solution.py:97
  97.8 0.3 copy.48
  98.1 0.3 concatenate.43
  98.5 0.2 copy.49
  98.6 2.7 %fusion.1 = f32[64,4,4]{0,2,1:T(4,128)S(1)} fusion(f32[4,516,64,4]{1,2,3,0:T(8,128)} %get-tuple-element.17, f32[64,4,4]{0,2,1:T(4,128)S(1)} %get-tuple-element.16, pred[64,516]{1,0:T(8,128)(4,1)S(1)} %compare_and_fusion), kind=kLoop, calls=%fused_computation.3 | loop fusion | flops 2640896 | bytes 2154752 | tf_op jit(solution)/shard_map/reduce_sum | solution.py:96
  101.7 1.1 concatenate.46
  102.7 4.2 %all-to-all-start = ((f32[16,4,2080]{2,1,0:T(4,128)}), f32[16,4,2080]{2,1,0:T(4,128)S(1)}, u32[]{:S(2)}, u32[]{:S(2)}) async-start(f32[16,4,2080]{2,1,0:T(4,128)} %concatenate.46), calls=%async_computation | async-start | bytes 1114112 | tf_op jit(solution)/shard_map/all_to_all | solution.py:111
  107.0 0.2 copy.60
  107.2 1.4 copy.53
  108.6 19.1 %all-to-all-done = f32[16,4,2080]{2,1,0:T(4,128)S(1)} async-done(((f32[16,4,2080]{2,1,0:T(4,128)}), f32[16,4,2080]{2,1,0:T(4,128)S(1)}, u32[]{:S(2)}, u32[]{:S(2)}) %all-to-all-start) | async-done | bytes 532512 | tf_op jit(solution)/shard_map/all_to_all | solution.py:111
  127.6 4.2 %all-to-all-start.2 = ((bf16[128,16,256]{2,0,1:T(8,128)(2,1)}), bf16[128,16,256]{2,0,1:T(8,128)(2,1)}, u32[]{:S(2)}, u32[]{:S(2)}) async-start(bf16[128,16,256]{2,0,1:T(8,128)(2,1)} %copy.53), calls=%async_computation.2 | async-start | bytes 2097152 | tf_op jit(solution)/shard_map/all_to_all | solution.py:160
  132.0 0.2 mul.180
  132.6 26.9 %all-to-all-done.2 = bf16[128,16,256]{2,0,1:T(8,128)(2,1)} async-done(((bf16[128,16,256]{2,0,1:T(8,128)(2,1)}), bf16[128,16,256]{2,0,1:T(8,128)(2,1)}, u32[]{:S(2)}, u32[]{:S(2)}) %all-to-all-start.2) | async-done | bytes 1048608 | tf_op jit(solution)/shard_map/all_to_all | solution.py:160
  159.5 3.3 %convolution_convert_fusion.1 = bf16[32,16,256]{2,1,0:T(8,128)(2,1)} fusion(bf16[32,16,2048]{2,1,0:T(8,128)(2,1)} %bitcast.102, bf16[2048,256,1]{1,0,2:T(8,128)(2,1)} %bitcast.23), kind=kOutput, calls=%fused_computation.9 | convolution fusion | flops 537001984 | bytes 3407872 | tf_op jit(solution)/shard_map/dot_general | solution.py:163
  162.8 10.1 %all-to-all-start.3 = ((bf16[32,16,256]{2,1,0:T(8,128)(2,1)}), bf16[32,16,256]{2,1,0:T(8,128)(2,1)S(1)}, u32[]{:S(2)}, u32[]{:S(2)}) async-start(bf16[32,16,256]{2,1,0:T(8,128)(2,1)} %convolution_convert_fusion.1), calls=%async_computation.3 | async-start | bytes 524288 | tf_op jit(solution)/shard_map/all_to_all | solution.py:169
  172.9 15.6 %all-gather = bf16[16,4,2048]{2,1,0:T(4,128)(2,1)S(1)} all-gather(bf16[1,4,2048]{2,1,0:T(4,128)(2,1)S(1)} %fusion.29), channel_id=1, replica_groups=mesh['kv'=16,'ep'=32] {'kv'}, dimensions={0}, use_global_device_ids=true | all-gather | bytes 278528 | tf_op jit(solution)/shard_map/all_gather | solution.py:122
  188.6 0.8 reshape.309
  189.4 0.9 convolution_convert_fusion.2
  (53 shorter events, 3.0 us)
Async XLA Ops:
  7.2 78.9 %copy-start = (bf16[1,4096,128]{2,1,0:T(8,128)(2,1)S(1)}, bf16[1,4096,128]{2,1,0:T(8,128)(2,1)}, u32[]{:S(2)}) copy-start(bf16[1,4096,128]{2,1,0:T(8,128)(2,1)} %param.23) | copy-start | bytes 3145732
  7.2 25.3 %copy-start.6 = (s32[1,64]{1,0:T(1,128)S(1)}, s32[1,64]{1,0:T(1,128)}, u32[]{:S(2)}) copy-start(s32[1,64]{1,0:T(1,128)} %param.18) | copy-start | bytes 772
  7.2 78.9 %all-gather.4.cloned.1.call-start = ((), (), s32[]{:S(2)}) async-start(), calls=%async_computation.4 | async-start | bytes 4456448 | tf_op jit(solution)/shard_map/all_gather | solution.py:154
  30.6 128.9 %all-gather.6.cloned.1.call-start = ((), (), s32[]{:S(2)}) async-start(), calls=%async_computation.5 | async-start | bytes 2228224 | tf_op jit(solution)/shard_map/all_gather | solution.py:164
  86.0 3.6 %copy-start.1 = (bf16[512,4096]{1,0:T(8,128)(2,1)S(1)}, bf16[512,4096]{1,0:T(8,128)(2,1)}, u32[]{:S(2)}) copy-start(bf16[512,4096]{1,0:T(8,128)(2,1)} %all-gather.4.cloned.1.call-done) | copy-start | bytes 12582916
  86.0 3.7 %copy-start.5 = (bf16[1,4096,128]{2,1,0:T(8,128)(2,1)S(1)}, bf16[1,4096,128]{2,1,0:T(8,128)(2,1)}, u32[]{:S(2)}) copy-start(bf16[1,4096,128]{2,1,0:T(8,128)(2,1)} %param.24) | copy-start | bytes 3145732
  89.8 2.0 %copy-start.3 = (bf16[1,4,128,512]{3,2,1,0:T(8,128)(2,1)S(1)}, bf16[1,4,128,512]{3,2,1,0:T(8,128)(2,1)}, u32[]{:S(2)}) copy-start(bf16[1,4,128,512]{3,2,1,0:T(8,128)(2,1)} %param.16) | copy-start | bytes 1572868
  91.7 1.0 copy-start.4
  98.6 8.3 %copy-start.2 = (bf16[1,128,4096]{2,1,0:T(8,128)(2,1)S(1)}, bf16[1,128,4096]{2,1,0:T(8,128)(2,1)}, u32[]{:S(2)}) copy-start(bf16[1,128,4096]{2,1,0:T(8,128)(2,1)} %param.25) | copy-start | bytes 3145732
  102.7 24.9 %all-to-all-start = ((f32[16,4,2080]{2,1,0:T(4,128)}), f32[16,4,2080]{2,1,0:T(4,128)S(1)}, u32[]{:S(2)}, u32[]{:S(2)}) async-start(f32[16,4,2080]{2,1,0:T(4,128)} %concatenate.46), calls=%async_computation | async-start | bytes 1114112 | tf_op jit(solution)/shard_map/all_to_all | solution.py:111
  127.6 31.9 %all-to-all-start.2 = ((bf16[128,16,256]{2,0,1:T(8,128)(2,1)}), bf16[128,16,256]{2,0,1:T(8,128)(2,1)}, u32[]{:S(2)}, u32[]{:S(2)}) async-start(bf16[128,16,256]{2,0,1:T(8,128)(2,1)} %copy.53), calls=%async_computation.2 | async-start | bytes 2097152 | tf_op jit(solution)/shard_map/all_to_all | solution.py:160
  162.8 26.5 %all-to-all-start.3 = ((bf16[32,16,256]{2,1,0:T(8,128)(2,1)}), bf16[32,16,256]{2,1,0:T(8,128)(2,1)S(1)}, u32[]{:S(2)}, u32[]{:S(2)}) async-start(bf16[32,16,256]{2,1,0:T(8,128)(2,1)} %convolution_convert_fusion.1), calls=%async_computation.3 | async-start | bytes 524288 | tf_op jit(solution)/shard_map/all_to_all | solution.py:169
Sparse Core Ops, SparseCore 0:
  30.8 55.2 all-gather.3
  91.8 61.0 all-gather.5

commit v3 on v2

v3 whole, which is shorter than its diff:
```python
import math

import jax
import jax.numpy as jnp
from jax import lax
from jax.sharding import PartitionSpec as P

HD = 128
EXPERTS = 8
TOP = 2
HQ = 16
KVH = 4
PAGE = 128
POOL_DEV = 4
CAP = 16


ROPE_BASE = 10000.0
MASKED = -1e30


def rotary(values, positions):
    half_width = values.shape[-1] // 2
    indices = jnp.arange(half_width, dtype=jnp.float32)
    frequency = jnp.power(ROPE_BASE, -2.0 * indices / values.shape[-1])
    angles = positions.astype(jnp.float32)[:, None] * frequency[None, :]
    cosine = jnp.cos(angles)[:, None, :]
    sine_part = jnp.sin(angles)[:, None, :]
    lower_half = values[..., :half_width]
    upper_half = values[..., half_width:]
    return jnp.concatenate(
        [
            lower_half * cosine - upper_half * sine_part,
            upper_half * cosine + lower_half * sine_part,
        ],
        axis=-1,
    )


def on_device(
    queries,
    new_keys,
    new_values,
    cache_keys,
    cache_values,
    page_table,
    cached_len,
    moe_rows,
    expert_ids,
    gate_probs,
    w_gate,
    w_up,
    w_down,
):
    kv_index = lax.axis_index("kv")
    kv_count = lax.axis_size("kv")
    all_rows = queries.shape[1]
    block_rows = all_rows // kv_count
    length = cached_len[0]
    group_size = HQ // KVH
    score_scale = 1.0 / math.sqrt(HD)
    out_width = w_down.shape[2] // kv_count
    down_split = w_down[0].reshape(w_down.shape[1], kv_count, out_width)
    down_cols = lax.all_to_all(down_split, "kv", split_axis=1, concat_axis=0, tiled=True).reshape(
        -1, out_width
    )
    ep_count = lax.axis_size("ep")
    share_count = ep_count // EXPERTS
    tok_rows = moe_rows.shape[0]
    slot_total = ep_count * CAP
    flat_ids = expert_ids.reshape(-1)
    one_hot = (flat_ids[:, None] == jnp.arange(EXPERTS, dtype=jnp.int32)[None, :]).astype(jnp.int32)
    earlier = jnp.cumsum(one_hot, axis=0) - one_hot
    slot_rank = jnp.sum(earlier * one_hot, axis=1)
    slot_index = jnp.arange(slot_total, dtype=jnp.int32)
    dest_expert = slot_index // CAP // share_count
    dest_slot = slot_index % CAP
    matched = (flat_ids[None, :] == dest_expert[:, None]) & (
        slot_rank[None, :] == dest_slot[:, None]
    )
    select = jnp.sum(matched.astype(jnp.float32).reshape(slot_total, tok_rows, TOP), axis=2).astype(
        jnp.bfloat16
    )
    weight_map = jnp.sum(
        jnp.where(matched, gate_probs.reshape(-1)[None, :], 0.0).reshape(slot_total, tok_rows, TOP),
        axis=2,
    )
    col_width = moe_rows.shape[1] // kv_count
    rows_cols = lax.dynamic_slice_in_dim(moe_rows, kv_index * col_width, col_width, 1)
    outgoing = (
        jnp.dot(select, rows_cols, preferred_element_type=jnp.float32)
        .astype(jnp.bfloat16)
        .reshape(ep_count, CAP, -1)
    )
    arrived_cols = lax.all_to_all(outgoing, "ep", split_axis=0, concat_axis=0, tiled=True).reshape(
        slot_total, -1
    )
    arrived = lax.all_gather(arrived_cols, "kv", axis=1, tiled=True)
    arrived_cols, queries, new_keys, new_values, cache_keys, cache_values = lax.optimization_barrier(
        (arrived_cols, queries, new_keys, new_values, cache_keys, cache_values)
    )
    slot_ids = kv_index * POOL_DEV + jnp.arange(POOL_DEV, dtype=jnp.int32)
    matches = (page_table[0][:, None] == slot_ids[None, :]).astype(jnp.int32)
    page_index = jnp.sum(
        matches * jnp.arange(page_table.shape[1], dtype=jnp.int32)[:, None], axis=0
    )
    cached_pos = (page_index[:, None] * PAGE + jnp.arange(PAGE, dtype=jnp.int32)[None, :]).reshape(
        -1
    )
    block_start = kv_index * block_rows
    own_pos = length + block_start + jnp.arange(block_rows, dtype=jnp.int32)
    key_block = lax.dynamic_slice_in_dim(new_keys[0], block_start, block_rows, 0)
    value_block = lax.dynamic_slice_in_dim(new_values[0], block_start, block_rows, 0)
    own_keys = rotary(key_block.astype(jnp.float32).reshape(block_rows, KVH, HD), own_pos).astype(
        jnp.bfloat16
    )
    local_keys = jnp.concatenate([cache_keys[0].reshape(-1, KVH, HD), own_keys], axis=0)
    local_values = jnp.concatenate(
        [cache_values[0].reshape(-1, KVH, HD), value_block.reshape(block_rows, KVH, HD)], axis=0
    )
    key_pos = jnp.concatenate([cached_pos, own_pos])
    live_keys = jnp.concatenate([cached_pos < length, jnp.ones((block_rows,), jnp.bool_)])
    positions = length + jnp.arange(all_rows, dtype=jnp.int32)
    rotated = rotary(queries[0].astype(jnp.float32).reshape(all_rows, HQ, HD), positions).astype(
        jnp.bfloat16
    )
    grouped = rotated.reshape(all_rows, KVH, group_size, HD)
    scores = (
        jnp.einsum("nkgd,mkd->nkgm", grouped, local_keys, preferred_element_type=jnp.float32)
        * score_scale
    )
    usable = (live_keys[None, :] & (key_pos[None, :] <= positions[:, None]))[:, None, None, :]
    scores = jnp.where(usable, scores, MASKED)
    part_high = jnp.max(scores, axis=-1)
    weights = jnp.where(usable, jnp.exp(scores - part_high[..., None]), 0.0)
    part_total = jnp.sum(weights, axis=-1)
    part_blend = jnp.einsum(
        "nkgm,mkd->nkgd",
        weights.astype(jnp.bfloat16),
        local_values,
        preferred_element_type=jnp.float32,
    )
    packed = jnp.concatenate(
        [
            part_blend.reshape(all_rows, HQ * HD),
            part_high.reshape(all_rows, HQ),
            part_total.reshape(all_rows, HQ),
        ],
        axis=1,
    ).reshape(kv_count, block_rows, -1)
    parts = lax.all_to_all(packed, "kv", split_axis=0, concat_axis=0, tiled=True).reshape(
        kv_count, block_rows, -1
    )
    parts_blend = parts[..., : HQ * HD].reshape(kv_count, block_rows, HQ, HD)
    parts_high = parts[..., HQ * HD : HQ * HD + HQ]
    parts_total = parts[..., HQ * HD + HQ :]
    highest = jnp.max(parts_high, axis=0)
    factor = jnp.exp(parts_high - highest[None])
    row_total = jnp.sum(parts_total * factor, axis=0)
    blended = jnp.sum(parts_blend * factor[..., None], axis=0)
    own_out = (blended / row_total[..., None]).reshape(block_rows, HQ * HD).astype(jnp.bfloat16)
    attn_out = lax.all_gather(own_out, "kv", axis=0, tiled=True).reshape(1, all_rows, HQ * HD)
    arrived, attn_out, down_cols = lax.optimization_barrier((arrived, attn_out, down_cols))
    gate_proj = jnp.dot(arrived, w_gate[0], preferred_element_type=jnp.float32)
    up_proj = jnp.dot(arrived, w_up[0], preferred_element_type=jnp.float32)
    hidden = (jax.nn.silu(gate_proj) * up_proj).astype(jnp.bfloat16)
    summed = jnp.dot(
        lax.all_gather(hidden, "kv", axis=1, tiled=True),
        down_cols,
        preferred_element_type=jnp.float32,
    )
    returned = (
        lax.all_to_all(
            summed.reshape(ep_count, CAP, -1).astype(jnp.bfloat16),
            "ep",
            split_axis=0,
            concat_axis=0,
            tiled=True,
        )
        .astype(jnp.float32)
        .reshape(slot_total, -1)
    )
    moe_out = jnp.dot(
        weight_map.T, returned, precision=lax.Precision.HIGHEST, preferred_element_type=jnp.float32
    ).astype(jnp.bfloat16)
    return (attn_out, moe_out)

def solution(mesh):
    return jax.shard_map(
        on_device,
        mesh=mesh,
        in_specs=(
            P("ep", None, None),
            P("ep", None, None),
            P("ep", None, None),
            P("ep", "kv", None, None),
            P("ep", "kv", None, None),
            P("ep", None),
            P("ep"),
            P("ep", None),
            P("ep", None),
            P("ep", None),
            P("ep", None, "kv"),
            P("ep", None, "kv"),
            P("ep", "kv", None),
        ),
        out_specs=(P("ep", None, None), P("ep", "kv")),
        check_vma=False,
    )
```

time: 198 us -> 204 us (1.030)
  blocking collectives: 35.7 us -> 76.1 us
  waiting for transfers between devices: 97.5 us -> 59.9 us
  local copies, waits for them, and re-layouts: 7.82 us -> 10.9 us
    all_gather x1, waiting for transfers between devices: 51.5 us -> 0.02 us  [on_device(): arrived = lax.all_gather(arrived_cols, 'kv', axis=1, tiled=True)]
    all_gather x1, waiting for transfers between devices: 0.01 us -> 40.4 us  [on_device(): lax.all_gather(hidden, 'kv', axis=1, tiled=True)]
    all_to_all x1, waiting for transfers between devices: 26.9 us -> 0.01 us  [on_device(): lax.all_to_all(down_split, 'kv', split_axis=1, concat_axis=0, tiled=True)]
    all_gather x1, blocking collectives: 15.6 us -> 37 us  [on_device(): lax.all_gather(own_out, 'kv', axis=0, tiled=True)]
    all_to_all x0 -> x1, blocking collectives: none -> 19 us  [on_device(): lax.all_to_all(summed.reshape(ep_count, CAP, -1).astype(jnp.bfloat16), 'e...]
    all_to_all x1 -> x0, starting transfers between devices: 10.1 us -> none  [on_device(): lax.all_to_all(summed.reshape(ep_count, CAP, -1).astype(jnp.bfloat16), 'e...]
    all_to_all x1, starting transfers between devices: 4.24 us -> 14.2 us  [on_device(): lax.all_to_all(packed, 'kv', split_axis=0, concat_axis=0, tiled=True)]
  transfers between devices with their start and end apart: 5 -> 4, of which waited for: 3 -> 2; matrix products, arithmetic and copies ran while one was open for 8% -> 10% of each run, Pallas kernels for 0% -> 0%
where the time goes in v3:
time: 204 us; the launch traced here: 202 us
  blocking collectives  76.1 us (37%)
  waiting for transfers between devices  59.9 us (29%)
  starting transfers between devices  17.8 us (9%)
  between operations  15 us (7%)
  matrix products  14.3 us (7%)
  local copies, waits for them, and re-layouts  10.9 us (5%)
  other arithmetic  7.67 us (4%)
    all_gather x1, waiting for transfers between devices, on_device(): lax.all_gather(hidden, 'kv', axis=1, tiled=True)  40.4 us
    all_gather x1, blocking collectives, on_device(): lax.all_gather(own_out, 'kv', axis=0, tiled=True)  37 us
    all_to_all x1, blocking collectives, on_device(): lax.all_to_all(outgoing, 'ep', split_axis=0, concat_axis=0, tiled=True)  20.1 us
    all_to_all x1, waiting for transfers between devices, on_device(): lax.all_to_all(packed, 'kv', split_axis=0, concat_axis=0, tiled=True)  19.5 us
    all_to_all x1, blocking collectives, on_device(): lax.all_to_all(summed.reshape(ep_count, CAP, -1).astype(jnp.bfloat16), 'e...  19 us
    all_to_all x1, starting transfers between devices, on_device(): lax.all_to_all(packed, 'kv', split_axis=0, concat_axis=0, tiled=True)  14.2 us
  transfers between devices with their start and end apart: 4, of which 2 were waited for; matrix products, arithmetic and copies ran while one was open for 10% of the time, Pallas kernels for 0%

profile of v3, /device:TPU:1, one launch (start us, length us, event | category | flops | bytes accessed | tf_op | source)
XLA Modules:
  0.0 201.6 jit_solution(10481990579248270009)
XLA Ops:
  7.3 0.9 copy.55
  8.8 0.8 select_reduce_fusion
  9.6 1.0 convolution_convert_fusion
  10.6 20.1 %all_to_all.30 = bf16[32,16,256]{2,1,0:T(8,128)(2,1)} all-to-all(bf16[32,16,256]{2,1,0:T(8,128)(2,1)S(1)} %bitcast.94), channel_id=1, replica_groups=mesh['kv'=16,'ep'=32] {'ep'}, dimensions={0} | all-to-all | bytes 524288 | tf_op jit(solution)/shard_map/all_to_all | solution.py:95
  31.4 0.8 select_reduce_fusion.2
  32.6 0.2 multiply_cosine_fusion
  32.8 1.0 convert_bitcast_fusion
  34.1 0.7 bitcast_convert_fusion
  34.9 0.2 fusion.50
  35.1 0.3 subtract_convert_fusion
  35.5 2.2 %fusion = (f32[64,4,4]{0,2,1:T(4,128)S(1)}, f32[4,516,64,4]{1,2,3,0:T(8,128)}) fusion(pred[64,516]{1,0:T(8,128)(4,1)S(1)} %compare_and_fusion, bf16[64,4,4,64]{3,0,2,1:T(8,128)(2,1)S(1)} %bitcast.96, bf16[64,4,4,64]{3,0,2,1:T(8,128)(2,1)S(1)} %bitcast.95, bf16[4,4,64]{2,0,1:T(4,128)(2,1)S(1)} %get-tuple-element.27, ...), kind=kOutput, calls=%fused_computation.2 | convolution fusion | flops 138959872 | bytes 2941184 | tf_op jit(solution)/shard_map/nkgd,mkd->nkgm/dot_general | solution.py:129
  37.8 2.7 %fusion.1 = f32[64,4,4]{0,2,1:T(4,128)S(1)} fusion(f32[4,516,64,4]{1,2,3,0:T(8,128)} %get-tuple-element.33, f32[64,4,4]{0,2,1:T(4,128)S(1)} %get-tuple-element.32, pred[64,516]{1,0:T(8,128)(4,1)S(1)} %compare_and_fusion), kind=kLoop, calls=%fused_computation.3 | loop fusion | flops 2640896 | bytes 2154752 | tf_op jit(solution)/shard_map/reduce_sum | solution.py:136
  41.0 0.7 dynamic-slice_bitcast_fusion
  41.7 2.5 %fusion.6 = f32[64,4,4,128]{3,0,2,1:T(8,128)S(1)} fusion(f32[4,516,64,4]{1,2,3,0:T(8,128)} %get-tuple-element.33, f32[64,4,4]{0,2,1:T(4,128)S(1)} %get-tuple-element.32, pred[64,516]{1,0:T(8,128)(4,1)S(1)} %compare_and_fusion, bf16[4,4,128]{2,0,1:T(4,128)(2,1)S(1)} %dynamic-slice_bitcast_fusion, bf16[512,4,128]{2,0,1:T(8,128)(2,1)S(1)} %copy.57), kind=kOutput, calls=%fused_computation.7 | convolution fusion | flops 138964992 | bytes 3203328 | tf_op jit(solution)/shard_map/nkgm,mkd->nkgd/dot_general | solution.py:137
  44.2 0.3 copy.61
  44.5 0.3 concatenate.43
  45.0 1.1 concatenate.46
  46.1 14.2 %all-to-all-start.1 = ((f32[16,4,2080]{2,1,0:T(4,128)}), f32[16,4,2080]{2,1,0:T(4,128)S(1)}, u32[]{:S(2)}, u32[]{:S(2)}) async-start(f32[16,4,2080]{2,1,0:T(4,128)} %concatenate.46), calls=%async_computation.1 | async-start | bytes 1114112 | tf_op jit(solution)/shard_map/all_to_all | solution.py:151
  60.3 2.3 %copy.64 = bf16[1,128,4096]{1,2,0:T(8,128)(2,1)} copy(bf16[1,128,4096]{2,1,0:T(8,128)(2,1)} %param.25) | data formatting | bytes 2097152 | tf_op args[12]
  62.6 19.5 %all-to-all-done.1 = f32[16,4,2080]{2,1,0:T(4,128)S(1)} async-done(((f32[16,4,2080]{2,1,0:T(4,128)}), f32[16,4,2080]{2,1,0:T(4,128)S(1)}, u32[]{:S(2)}, u32[]{:S(2)}) %all-to-all-start.1) | async-done | bytes 532512 | tf_op jit(solution)/shard_map/all_to_all | solution.py:151
  82.1 3.6 %all-to-all-start.2 = ((bf16[128,16,256]{0,2,1:T(8,128)(2,1)}), bf16[128,16,256]{0,2,1:T(8,128)(2,1)S(1)}, u32[]{:S(2)}, u32[]{:S(2)}) async-start(bf16[128,16,256]{0,2,1:T(8,128)(2,1)} %bitcast.17), calls=%async_computation.2 | async-start | bytes 2097152 | tf_op jit(solution)/shard_map/all_to_all | solution.py:64
  85.8 1.0 mul.182
  86.8 1.2 mul.183
  88.3 37.0 %all-gather = bf16[16,4,2048]{2,1,0:T(4,128)(2,1)S(1)} all-gather(bf16[1,4,2048]{2,1,0:T(4,128)(2,1)S(1)} %fusion.29), channel_id=1, replica_groups=mesh['kv'=16,'ep'=32] {'kv'}, dimensions={0}, use_global_device_ids=true | all-gather | bytes 278528 | tf_op jit(solution)/shard_map/all_gather | solution.py:162
  125.3 0.8 reshape.311
  126.0 0.5 copy.65
  126.6 3.6 %fusion.11 = f32[512,128]{1,0:T(8,128)S(1)} fusion(bf16[512,4096]{1,0:T(8,128)(2,1)} %all-gather.4.cloned.1.call-done, bf16[1,4096,128]{2,1,0:T(8,128)(2,1)S(1)} %copy-done), kind=kOutput, calls=%fused_computation.14 | convolution fusion | flops 536870912 | bytes 5505024 | tf_op jit(solution)/shard_map/dot_general | solution.py:164
  130.4 1.9 fusion.9
  132.3 40.4 %all-gather.6.cloned.1.call-done = bf16[512,2048]{1,0:T(8,128)(2,1)} async-done(((bf16[512,128]{1,0:T(8,128)(2,1)}), bf16[512,2048]{1,0:T(8,128)(2,1)}) %all-gather.6.cloned.1.call-update) | async-done | bytes 2097168 | tf_op jit(solution)/shard_map/all_gather | solution.py:168
  172.6 2.3 %convolution_convert_fusion.1 = bf16[512,256]{1,0:T(8,128)(2,1)S(1)} fusion(bf16[512,2048]{1,0:T(8,128)(2,1)} %all-gather.6.cloned.1.call-done, bf16[2048,256]{1,0:T(8,128)(2,1)S(1)} %bitcast.91), kind=kOutput, calls=%fused_computation.9 | convolution fusion | flops 537001984 | bytes 3407872 | tf_op jit(solution)/shard_map/dot_general | solution.py:167
  174.9 19.0 %all_to_all.31 = bf16[32,16,256]{2,1,0:T(8,128)(2,1)S(1)} all-to-all(bf16[32,16,256]{2,1,0:T(8,128)(2,1)S(1)} %bitcast.97), channel_id=1, replica_groups=mesh['kv'=16,'ep'=32] {'ep'}, dimensions={0} | all-to-all | bytes 524288 | tf_op jit(solution)/shard_map/all_to_all | solution.py:173
  193.9 0.9 convolution_convert_fusion.2
  (49 shorter events, 2.8 us)
Async XLA Ops:
  7.2 119.4 %copy-start = (bf16[1,4096,128]{2,1,0:T(8,128)(2,1)S(1)}, bf16[1,4096,128]{2,1,0:T(8,128)(2,1)}, u32[]{:S(2)}) copy-start(bf16[1,4096,128]{2,1,0:T(8,128)(2,1)} %param.23) | copy-start | bytes 3145732
  7.2 26.7 %copy-start.2 = (bf16[1,4,128,512]{3,2,1,0:T(8,128)(2,1)S(1)}, bf16[1,4,128,512]{3,2,1,0:T(8,128)(2,1)}, u32[]{:S(2)}) copy-start(bf16[1,4,128,512]{3,2,1,0:T(8,128)(2,1)} %param.16) | copy-start | bytes 1572868
  7.2 119.4 %all-gather.4.cloned.1.call-start = ((), (), s32[]{:S(2)}) async-start(), calls=%async_computation.4 | async-start | bytes 4456448 | tf_op jit(solution)/shard_map/all_gather | solution.py:98
  37.7 3.1 %copy-start.3 = (bf16[1,4,128,512]{3,2,1,0:T(8,128)(2,1)S(1)}, bf16[1,4,128,512]{3,2,1,0:T(8,128)(2,1)}, u32[]{:S(2)}) copy-start(bf16[1,4,128,512]{3,2,1,0:T(8,128)(2,1)} %param.17) | copy-start | bytes 1572868
  46.1 36.0 %all-to-all-start.1 = ((f32[16,4,2080]{2,1,0:T(4,128)}), f32[16,4,2080]{2,1,0:T(4,128)S(1)}, u32[]{:S(2)}, u32[]{:S(2)}) async-start(f32[16,4,2080]{2,1,0:T(4,128)} %concatenate.46), calls=%async_computation.1 | async-start | bytes 1114112 | tf_op jit(solution)/shard_map/all_to_all | solution.py:151
  82.1 44.0 %all-to-all-start.2 = ((bf16[128,16,256]{0,2,1:T(8,128)(2,1)}), bf16[128,16,256]{0,2,1:T(8,128)(2,1)S(1)}, u32[]{:S(2)}, u32[]{:S(2)}) async-start(bf16[128,16,256]{0,2,1:T(8,128)(2,1)} %bitcast.17), calls=%async_computation.2 | async-start | bytes 2097152 | tf_op jit(solution)/shard_map/all_to_all | solution.py:64
  85.6 87.0 %all-gather.6.cloned.1.call-start = ((), (), s32[]{:S(2)}) async-start(), calls=%async_computation.5 | async-start | bytes 2228224 | tf_op jit(solution)/shard_map/all_gather | solution.py:168
  126.6 3.6 %copy-start.1 = (bf16[512,4096]{1,0:T(8,128)(2,1)S(1)}, bf16[512,4096]{1,0:T(8,128)(2,1)}, u32[]{:S(2)}) copy-start(bf16[512,4096]{1,0:T(8,128)(2,1)} %all-gather.4.cloned.1.call-done) | copy-start | bytes 12582916
  126.6 3.7 %copy-start.4 = (bf16[1,4096,128]{2,1,0:T(8,128)(2,1)S(1)}, bf16[1,4096,128]{2,1,0:T(8,128)(2,1)}, u32[]{:S(2)}) copy-start(bf16[1,4096,128]{2,1,0:T(8,128)(2,1)} %param.24) | copy-start | bytes 3145732
Sparse Core Ops, SparseCore 0:
  30.8 72.4 all-gather.3
  132.4 40.1 all-gather.5

commit v4 on v3

--- a/solution.py
+++ b/solution.py
@@ -95,7 +95,7 @@
     arrived_cols = lax.all_to_all(outgoing, "ep", split_axis=0, concat_axis=0, tiled=True).reshape(
         slot_total, -1
     )
-    arrived = lax.all_gather(arrived_cols, "kv", axis=1, tiled=True)
+    arrived = lax.all_gather(arrived_cols, "kv", axis=0, tiled=False)
     arrived_cols, queries, new_keys, new_values, cache_keys, cache_values = lax.optimization_barrier(
         (arrived_cols, queries, new_keys, new_values, cache_keys, cache_values)
     )
@@ -161,12 +161,15 @@
     own_out = (blended / row_total[..., None]).reshape(block_rows, HQ * HD).astype(jnp.bfloat16)
     attn_out = lax.all_gather(own_out, "kv", axis=0, tiled=True).reshape(1, all_rows, HQ * HD)
     arrived, attn_out, down_cols = lax.optimization_barrier((arrived, attn_out, down_cols))
-    gate_proj = jnp.dot(arrived, w_gate[0], preferred_element_type=jnp.float32)
-    up_proj = jnp.dot(arrived, w_up[0], preferred_element_type=jnp.float32)
+    gate_w = w_gate[0].reshape(kv_count, col_width, -1)
+    up_w = w_up[0].reshape(kv_count, col_width, -1)
+    gate_proj = jnp.einsum("ksc,kch->sh", arrived, gate_w, preferred_element_type=jnp.float32)
+    up_proj = jnp.einsum("ksc,kch->sh", arrived, up_w, preferred_element_type=jnp.float32)
     hidden = (jax.nn.silu(gate_proj) * up_proj).astype(jnp.bfloat16)
-    summed = jnp.dot(
-        lax.all_gather(hidden, "kv", axis=1, tiled=True),
-        down_cols,
+    summed = jnp.einsum(
+        "ksh,khc->sc",
+        lax.all_gather(hidden, "kv", axis=0, tiled=False),
+        down_cols.reshape(kv_count, -1, out_width),
         preferred_element_type=jnp.float32,
     )
     returned = (

time: 204 us -> 200 us (0.980)
  blocking collectives: 76.1 us -> 74 us
    all_gather x1, blocking collectives: 37 us -> 34.9 us  [on_device(): lax.all_gather(own_out, 'kv', axis=0, tiled=True)]
where the time goes in v4:
time: 200 us; the launch traced here: 198 us
  blocking collectives  74 us (37%)
  waiting for transfers between devices  58.9 us (29%)
  starting transfers between devices  18.3 us (9%)
  between operations  15 us (8%)
  matrix products  14.3 us (7%)
  local copies, waits for them, and re-layouts  10.2 us (5%)
  other arithmetic  7.03 us (4%)
    all_gather x1, waiting for transfers between devices, on_device(): lax.all_gather(hidden, 'kv', axis=0, tiled=False)  38.3 us
    all_gather x1, blocking collectives, on_device(): lax.all_gather(own_out, 'kv', axis=0, tiled=True)  34.9 us
    all_to_all x1, waiting for transfers between devices, on_device(): lax.all_to_all(packed, 'kv', split_axis=0, concat_axis=0, tiled=True)  20.5 us
    all_to_all x1, blocking collectives, on_device(): lax.all_to_all(outgoing, 'ep', split_axis=0, concat_axis=0, tiled=True)  20.1 us
    all_to_all x1, blocking collectives, on_device(): lax.all_to_all(summed.reshape(ep_count, CAP, -1).astype(jnp.bfloat16), 'e...  19 us
    all_to_all x1, starting transfers between devices, on_device(): lax.all_to_all(packed, 'kv', split_axis=0, concat_axis=0, tiled=True)  14.2 us
    all_to_all x1, starting transfers between devices, on_device(): lax.all_to_all(down_split, 'kv', split_axis=1, concat_axis=0, tiled=True)  4.03 us
  transfers between devices with their start and end apart: 4, of which 2 were waited for; matrix products, arithmetic and copies ran while one was open for 10% of the time, Pallas kernels for 0%

profile of v4, /device:TPU:1, one launch (start us, length us, event | category | flops | bytes accessed | tf_op | source)
XLA Modules:
  0.0 197.7 jit_solution(15654742241413323669)
XLA Ops:
  7.3 0.9 copy.61
  8.8 0.8 select_reduce_fusion
  9.6 1.0 convolution_convert_fusion
  10.6 20.1 %all_to_all.30 = bf16[32,16,256]{2,1,0:T(8,128)(2,1)} all-to-all(bf16[32,16,256]{2,1,0:T(8,128)(2,1)S(1)} %bitcast.117), channel_id=1, replica_groups=mesh['kv'=16,'ep'=32] {'ep'}, dimensions={0} | all-to-all | bytes 524288 | tf_op jit(solution)/shard_map/all_to_all | solution.py:95
  31.4 1.0 convert_bitcast_fusion
  32.7 0.2 select_reduce_fusion.2
  33.1 0.7 bitcast_convert_fusion
  34.1 0.2 multiply_cosine_fusion
  34.3 0.2 fusion.49
  34.5 0.3 subtract_convert_fusion
  34.9 2.2 %fusion = (f32[64,4,4]{0,2,1:T(4,128)S(1)}, f32[4,516,64,4]{1,2,3,0:T(8,128)}) fusion(pred[64,516]{1,0:T(8,128)(4,1)S(1)} %compare_and_fusion, bf16[64,4,4,64]{3,0,2,1:T(8,128)(2,1)S(1)} %bitcast.119, bf16[64,4,4,64]{3,0,2,1:T(8,128)(2,1)S(1)} %bitcast.118, bf16[4,4,64]{2,0,1:T(4,128)(2,1)S(1)} %get-tuple-element.27, ...), kind=kOutput, calls=%fused_computation.2 | convolution fusion | flops 138959872 | bytes 2941184 | tf_op jit(solution)/shard_map/nkgd,mkd->nkgm/dot_general | solution.py:129
  37.2 2.7 %fusion.1 = f32[64,4,4]{0,2,1:T(4,128)S(1)} fusion(f32[4,516,64,4]{1,2,3,0:T(8,128)} %get-tuple-element.33, f32[64,4,4]{0,2,1:T(4,128)S(1)} %get-tuple-element.32, pred[64,516]{1,0:T(8,128)(4,1)S(1)} %compare_and_fusion), kind=kLoop, calls=%fused_computation.3 | loop fusion | flops 2640896 | bytes 2154752 | tf_op jit(solution)/shard_map/reduce_sum | solution.py:136
  40.0 0.2 copy.69
  40.3 2.5 %fusion.6 = f32[64,4,4,128]{3,0,2,1:T(8,128)S(1)} fusion(f32[4,516,64,4]{1,2,3,0:T(8,128)} %get-tuple-element.33, f32[64,4,4]{0,2,1:T(4,128)S(1)} %get-tuple-element.32, pred[64,516]{1,0:T(8,128)(4,1)S(1)} %compare_and_fusion, bf16[4,4,128]{2,0,1:T(4,128)(2,1)S(1)} %get-tuple-element.41, bf16[512,4,128]{2,0,1:T(8,128)(2,1)S(1)} %copy.63), kind=kOutput, calls=%fused_computation.7 | convolution fusion | flops 138964992 | bytes 3203328 | tf_op jit(solution)/shard_map/nkgm,mkd->nkgd/dot_general | solution.py:137
  42.8 0.3 copy.67
  43.2 0.3 concatenate.43
  43.7 1.1 concatenate.46
  44.8 14.2 %all-to-all-start.1 = ((f32[16,4,2080]{2,1,0:T(4,128)}), f32[16,4,2080]{2,1,0:T(4,128)S(1)}, u32[]{:S(2)}, u32[]{:S(2)}) async-start(f32[16,4,2080]{2,1,0:T(4,128)} %concatenate.46), calls=%async_computation.1 | async-start | bytes 1114112 | tf_op jit(solution)/shard_map/all_to_all | solution.py:151
  59.0 2.3 %copy.70 = bf16[1,128,4096]{1,2,0:T(8,128)(2,1)} copy(bf16[1,128,4096]{2,1,0:T(8,128)(2,1)} %param.25) | data formatting | bytes 2097152 | tf_op args[12]
  61.3 20.5 %all-to-all-done.1 = f32[16,4,2080]{2,1,0:T(4,128)S(1)} async-done(((f32[16,4,2080]{2,1,0:T(4,128)}), f32[16,4,2080]{2,1,0:T(4,128)S(1)}, u32[]{:S(2)}, u32[]{:S(2)}) %all-to-all-start.1) | async-done | bytes 532512 | tf_op jit(solution)/shard_map/all_to_all | solution.py:151
  81.8 4.0 %all-to-all-start.2 = ((bf16[128,16,256]{0,2,1:T(8,128)(2,1)}), bf16[128,16,256]{0,2,1:T(8,128)(2,1)S(1)}, u32[]{:S(2)}, u32[]{:S(2)}) async-start(bf16[128,16,256]{0,2,1:T(8,128)(2,1)} %bitcast.17), calls=%async_computation.2 | async-start | bytes 2097152 | tf_op jit(solution)/shard_map/all_to_all | solution.py:64
  86.0 1.0 mul.182
  87.0 1.2 mul.183
  88.5 34.9 %all-gather.1 = bf16[16,4,2048]{2,1,0:T(4,128)(2,1)S(1)} all-gather(bf16[1,4,2048]{2,1,0:T(4,128)(2,1)S(1)} %fusion.28), channel_id=1, replica_groups=mesh['kv'=16,'ep'=32] {'kv'}, dimensions={0}, use_global_device_ids=true | all-gather | bytes 278528 | tf_op jit(solution)/shard_map/all_gather | solution.py:162
  123.4 0.8 reshape.311
  124.2 0.5 copy.71
  124.8 3.6 %convolution_bitcast_fusion.2 = f32[512,128]{1,0:T(8,128)S(1)} fusion(bf16[16,512,256]{2,1,0:T(8,128)(2,1)} %all-gather.5.cloned.1.call-done, bf16[16,256,128]{2,1,0:T(8,128)(2,1)S(1)} %bitcast.111), kind=kOutput, calls=%fused_computation.12 | convolution fusion | flops 536870912 | bytes 5505024 | tf_op jit(solution)/shard_map/ksc,kch->sh/dot_general | solution.py:166
  128.5 1.9 fusion.11
  130.4 38.3 %all-gather.7.cloned.1.call-done = bf16[8192,128]{1,0:T(8,128)(2,1)} async-done(((bf16[512,128]{1,0:T(8,128)(2,1)}), bf16[8192,128]{1,0:T(8,128)(2,1)}) %all-gather.7.cloned.1.call-update) | async-done | bytes 2097168 | tf_op jit(solution)/shard_map/all_gather | solution.py:171
  168.7 2.3 %fusion.9 = bf16[32,16,256]{2,1,0:T(8,128)(2,1)S(1)} fusion(bf16[32,16,128,16]{2,1,0,3:T(8,128)(2,1)} %bitcast.120, bf16[16,128,256,1]{2,1,3,0:T(8,128)(2,1)S(1)} %bitcast.114), kind=kOutput, calls=%fused_computation.10 | convolution fusion | flops 537001984 | bytes 3407872 | tf_op jit(solution)/shard_map/ksh,khc->sc/dot_general | solution.py:169
  171.0 19.0 %all_to_all.31 = bf16[32,16,256]{2,1,0:T(8,128)(2,1)S(1)} all-to-all(bf16[32,16,256]{2,1,0:T(8,128)(2,1)S(1)} %fusion.9), channel_id=1, replica_groups=mesh['kv'=16,'ep'=32] {'ep'}, dimensions={0} | all-to-all | bytes 524288 | tf_op jit(solution)/shard_map/all_to_all | solution.py:176
  190.0 0.9 convolution_convert_fusion.1
  (50 shorter events, 2.7 us)
Async XLA Ops:
  7.2 117.6 %copy-start = (bf16[1,4096,128]{2,1,0:T(8,128)(2,1)S(1)}, bf16[1,4096,128]{2,1,0:T(8,128)(2,1)}, u32[]{:S(2)}) copy-start(bf16[1,4096,128]{2,1,0:T(8,128)(2,1)} %param.23) | copy-start | bytes 3145732
  7.2 25.3 %copy-start.2 = (bf16[1,4,128,512]{3,2,1,0:T(8,128)(2,1)S(1)}, bf16[1,4,128,512]{3,2,1,0:T(8,128)(2,1)}, u32[]{:S(2)}) copy-start(bf16[1,4,128,512]{3,2,1,0:T(8,128)(2,1)} %param.16) | copy-start | bytes 1572868
  7.2 117.5 %all-gather.5.cloned.1.call-start = ((), (), s32[]{:S(2)}) async-start(), calls=%async_computation.4 | async-start | bytes 4456448 | tf_op jit(solution)/shard_map/all_gather | solution.py:98
  8.4 24.3 %copy-start.5 = (s32[1,64]{1,0:T(1,128)S(1)}, s32[1,64]{1,0:T(1,128)}, u32[]{:S(2)}) copy-start(s32[1,64]{1,0:T(1,128)} %param.18) | copy-start | bytes 772
  37.1 3.1 %copy-start.3 = (bf16[1,4,128,512]{3,2,1,0:T(8,128)(2,1)S(1)}, bf16[1,4,128,512]{3,2,1,0:T(8,128)(2,1)}, u32[]{:S(2)}) copy-start(bf16[1,4,128,512]{3,2,1,0:T(8,128)(2,1)} %param.17) | copy-start | bytes 1572868
  44.8 37.0 %all-to-all-start.1 = ((f32[16,4,2080]{2,1,0:T(4,128)}), f32[16,4,2080]{2,1,0:T(4,128)S(1)}, u32[]{:S(2)}, u32[]{:S(2)}) async-start(f32[16,4,2080]{2,1,0:T(4,128)} %concatenate.46), calls=%async_computation.1 | async-start | bytes 1114112 | tf_op jit(solution)/shard_map/all_to_all | solution.py:151
  81.8 42.4 %all-to-all-start.2 = ((bf16[128,16,256]{0,2,1:T(8,128)(2,1)}), bf16[128,16,256]{0,2,1:T(8,128)(2,1)S(1)}, u32[]{:S(2)}, u32[]{:S(2)}) async-start(bf16[128,16,256]{0,2,1:T(8,128)(2,1)} %bitcast.17), calls=%async_computation.2 | async-start | bytes 2097152 | tf_op jit(solution)/shard_map/all_to_all | solution.py:64
  85.8 82.9 %all-gather.7.cloned.1.call-start = ((), (), s32[]{:S(2)}) async-start(), calls=%async_computation.5 | async-start | bytes 2228224 | tf_op jit(solution)/shard_map/all_gather | solution.py:171
  124.7 3.6 %copy-start.1 = (bf16[16,512,256]{2,1,0:T(8,128)(2,1)S(1)}, bf16[16,512,256]{2,1,0:T(8,128)(2,1)}, u32[]{:S(2)}) copy-start(bf16[16,512,256]{2,1,0:T(8,128)(2,1)} %all-gather.5.cloned.1.call-done) | copy-start | bytes 12582916
  124.7 3.7 %copy-start.4 = (bf16[1,4096,128]{2,1,0:T(8,128)(2,1)S(1)}, bf16[1,4096,128]{2,1,0:T(8,128)(2,1)}, u32[]{:S(2)}) copy-start(bf16[1,4096,128]{2,1,0:T(8,128)(2,1)} %param.24) | copy-start | bytes 3145732
Sparse Core Ops, SparseCore 0:
  30.8 57.8 all-gather.4
  130.5 38.1 all-gather.6

commit v5 on v4

--- a/solution.py
+++ b/solution.py
@@ -159,16 +159,20 @@
     row_total = jnp.sum(parts_total * factor, axis=0)
     blended = jnp.sum(parts_blend * factor[..., None], axis=0)
     own_out = (blended / row_total[..., None]).reshape(block_rows, HQ * HD).astype(jnp.bfloat16)
-    attn_out = lax.all_gather(own_out, "kv", axis=0, tiled=True).reshape(1, all_rows, HQ * HD)
-    arrived, attn_out, down_cols = lax.optimization_barrier((arrived, attn_out, down_cols))
+    arrived, own_out, down_cols = lax.optimization_barrier((arrived, own_out, down_cols))
     gate_w = w_gate[0].reshape(kv_count, col_width, -1)
     up_w = w_up[0].reshape(kv_count, col_width, -1)
     gate_proj = jnp.einsum("ksc,kch->sh", arrived, gate_w, preferred_element_type=jnp.float32)
     up_proj = jnp.einsum("ksc,kch->sh", arrived, up_w, preferred_element_type=jnp.float32)
     hidden = (jax.nn.silu(gate_proj) * up_proj).astype(jnp.bfloat16)
+    hidden_width = hidden.shape[1]
+    joined = lax.all_gather(
+        jnp.concatenate([hidden, own_out.reshape(-1, hidden_width)], axis=0), "kv", axis=0, tiled=False
+    )
+    attn_out = joined[:, slot_total:].reshape(1, all_rows, HQ * HD)
     summed = jnp.einsum(
         "ksh,khc->sc",
-        lax.all_gather(hidden, "kv", axis=0, tiled=False),
+        joined[:, :slot_total],
         down_cols.reshape(kv_count, -1, out_width),
         preferred_element_type=jnp.float32,
     )

time: 200 us -> 189 us (0.945)
  blocking collectives: 74 us -> 20.1 us
  waiting for transfers between devices: 58.9 us -> 90.1 us
  starting transfers between devices: 18.3 us -> 27.5 us
  local copies, waits for them, and re-layouts: 10.2 us -> 13 us
    all_gather x1 -> x0, blocking collectives: 34.9 us -> none  [on_device(): lax.all_gather(own_out, 'kv', axis=0, tiled=True)]
    all_to_all x1, waiting for transfers between devices: 0.01 us -> 25.4 us  [on_device(): lax.all_to_all(down_split, 'kv', split_axis=1, concat_axis=0, tiled=True)]
    all_to_all x1 -> x0, blocking collectives: 19 us -> none  [on_device(): lax.all_to_all(summed.reshape(ep_count, CAP, -1).astype(jnp.bfloat16), 'e...]
    all_to_all x0 -> x1, starting transfers between devices: none -> 9.24 us  [on_device(): lax.all_to_all(summed.reshape(ep_count, CAP, -1).astype(jnp.bfloat16), 'e...]
    all_to_all x0 -> x1, waiting for transfers between devices: none -> 8.15 us  [on_device(): lax.all_to_all(summed.reshape(ep_count, CAP, -1).astype(jnp.bfloat16), 'e...]
    slice x0 -> x2, local copies, waits for them, and re-layouts: none -> 2.72 us  [the longest x1 1.75 us: on_device(): joined[:, :slot_total]]
    all_gather x1, waiting for transfers between devices: 38.3 us -> 36 us  [on_device(): lax.all_gather(jnp.concatenate([hidden, own_out.reshape(-1, hidden_width)...]
  transfers between devices with their start and end apart: 4 -> 5, of which waited for: 2 -> 4; matrix products, arithmetic and copies ran while one was open for 10% -> 11% of each run, Pallas kernels for 0% -> 0%
where the time goes in v5:
time: 189 us; the launch traced here: 186 us
  waiting for transfers between devices  90.1 us (48%)
  starting transfers between devices  27.5 us (15%)
  blocking collectives  20.1 us (11%)
  between operations  15 us (8%)
  local copies, waits for them, and re-layouts  13 us (7%)
  matrix products  12.8 us (7%)
  other arithmetic  7.7 us (4%)
    all_gather x1, waiting for transfers between devices, on_device(): lax.all_gather(jnp.concatenate([hidden, own_out.reshape(-1, hidden_width)...  36 us
    all_to_all x1, waiting for transfers between devices, on_device(): lax.all_to_all(down_split, 'kv', split_axis=1, concat_axis=0, tiled=True)  25.4 us
    all_to_all x1, waiting for transfers between devices, on_device(): lax.all_to_all(packed, 'kv', split_axis=0, concat_axis=0, tiled=True)  20.5 us
    all_to_all x1, blocking collectives, on_device(): lax.all_to_all(outgoing, 'ep', split_axis=0, concat_axis=0, tiled=True)  20.1 us
    all_to_all x1, starting transfers between devices, on_device(): lax.all_to_all(packed, 'kv', split_axis=0, concat_axis=0, tiled=True)  14.2 us
    all_to_all x1, starting transfers between devices, on_device(): lax.all_to_all(summed.reshape(ep_count, CAP, -1).astype(jnp.bfloat16), 'e...  9.24 us
    all_to_all x1, waiting for transfers between devices, on_device(): lax.all_to_all(summed.reshape(ep_count, CAP, -1).astype(jnp.bfloat16), 'e...  8.15 us
    all_to_all x1, starting transfers between devices, on_device(): lax.all_to_all(down_split, 'kv', split_axis=1, concat_axis=0, tiled=True)  4 us
  transfers between devices with their start and end apart: 5, of which 4 were waited for; matrix products, arithmetic and copies ran while one was open for 11% of the time, Pallas kernels for 0%

profile of v5, /device:TPU:1, one launch (start us, length us, event | category | flops | bytes accessed | tf_op | source)
XLA Modules:
  0.0 186.1 jit_solution(15813547133113623740)
XLA Ops:
  7.3 0.9 copy.61
  8.8 0.8 select_reduce_fusion
  9.6 1.0 convolution_convert_fusion
  10.6 20.1 %all_to_all.30 = bf16[32,16,256]{2,1,0:T(8,128)(2,1)} all-to-all(bf16[32,16,256]{2,1,0:T(8,128)(2,1)S(1)} %bitcast.116), channel_id=1, replica_groups=mesh['kv'=16,'ep'=32] {'ep'}, dimensions={0} | all-to-all | bytes 524288 | tf_op jit(solution)/shard_map/all_to_all | solution.py:95
  31.4 1.0 convert_bitcast_fusion
  33.1 0.7 bitcast_convert_fusion
  34.5 0.3 subtract_convert_fusion
  34.9 2.2 %fusion = (f32[64,4,4]{0,2,1:T(4,128)S(1)}, f32[4,516,64,4]{1,2,3,0:T(8,128)}) fusion(pred[64,516]{1,0:T(8,128)(4,1)S(1)} %compare_and_fusion, bf16[64,4,4,64]{3,0,2,1:T(8,128)(2,1)S(1)} %bitcast.118, bf16[64,4,4,64]{3,0,2,1:T(8,128)(2,1)S(1)} %bitcast.117, bf16[4,4,64]{2,0,1:T(4,128)(2,1)S(1)} %get-tuple-element.27, ...), kind=kOutput, calls=%fused_computation.2 | convolution fusion | flops 138959872 | bytes 2941184 | tf_op jit(solution)/shard_map/nkgd,mkd->nkgm/dot_general | solution.py:129
  37.2 2.7 %fusion.1 = f32[64,4,4]{0,2,1:T(4,128)S(1)} fusion(f32[4,516,64,4]{1,2,3,0:T(8,128)} %get-tuple-element.33, f32[64,4,4]{0,2,1:T(4,128)S(1)} %get-tuple-element.32, pred[64,516]{1,0:T(8,128)(4,1)S(1)} %compare_and_fusion), kind=kLoop, calls=%fused_computation.3 | loop fusion | flops 2640896 | bytes 2154752 | tf_op jit(solution)/shard_map/reduce_sum | solution.py:136
  40.3 2.5 %fusion.6 = f32[64,4,4,128]{3,0,2,1:T(8,128)S(1)} fusion(f32[4,516,64,4]{1,2,3,0:T(8,128)} %get-tuple-element.33, f32[64,4,4]{0,2,1:T(4,128)S(1)} %get-tuple-element.32, pred[64,516]{1,0:T(8,128)(4,1)S(1)} %compare_and_fusion, bf16[4,4,128]{2,0,1:T(4,128)(2,1)S(1)} %get-tuple-element.41, bf16[512,4,128]{2,0,1:T(8,128)(2,1)S(1)} %copy.63), kind=kOutput, calls=%fused_computation.7 | convolution fusion | flops 138964992 | bytes 3203328 | tf_op jit(solution)/shard_map/nkgm,mkd->nkgd/dot_general | solution.py:137
  42.8 0.3 copy.67
  43.2 0.3 concatenate.46
  43.7 1.1 concatenate.49
  44.8 14.2 %all-to-all-start.1 = ((f32[16,4,2080]{2,1,0:T(4,128)}), f32[16,4,2080]{2,1,0:T(4,128)S(1)}, u32[]{:S(2)}, u32[]{:S(2)}) async-start(f32[16,4,2080]{2,1,0:T(4,128)} %concatenate.49), calls=%async_computation.1 | async-start | bytes 1114112 | tf_op jit(solution)/shard_map/all_to_all | solution.py:151
  59.0 2.3 %copy.70 = bf16[1,128,4096]{1,2,0:T(8,128)(2,1)} copy(bf16[1,128,4096]{2,1,0:T(8,128)(2,1)} %param.25) | data formatting | bytes 2097152 | tf_op args[12]
  61.3 20.5 %all-to-all-done.1 = f32[16,4,2080]{2,1,0:T(4,128)S(1)} async-done(((f32[16,4,2080]{2,1,0:T(4,128)}), f32[16,4,2080]{2,1,0:T(4,128)S(1)}, u32[]{:S(2)}, u32[]{:S(2)}) %all-to-all-start.1) | async-done | bytes 532512 | tf_op jit(solution)/shard_map/all_to_all | solution.py:151
  81.8 4.0 %all-to-all-start.2 = ((bf16[128,16,256]{0,2,1:T(8,128)(2,1)}), bf16[128,16,256]{0,2,1:T(8,128)(2,1)S(1)}, u32[]{:S(2)}, u32[]{:S(2)}) async-start(bf16[128,16,256]{0,2,1:T(8,128)(2,1)} %bitcast.16), calls=%async_computation.2 | async-start | bytes 2097152 | tf_op jit(solution)/shard_map/all_to_all | solution.py:64
  86.0 1.0 mul.182
  87.0 1.2 mul.183
  88.4 25.4 %all-to-all-done.2 = bf16[128,16,256]{0,2,1:T(8,128)(2,1)S(1)} async-done(((bf16[128,16,256]{0,2,1:T(8,128)(2,1)}), bf16[128,16,256]{0,2,1:T(8,128)(2,1)S(1)}, u32[]{:S(2)}, u32[]{:S(2)}) %all-to-all-start.2) | async-done | bytes 1048608 | tf_op jit(solution)/shard_map/all_to_all | solution.py:64
  113.8 0.5 copy.71
  114.4 3.6 %convolution_bitcast_fusion.2 = f32[512,128]{1,0:T(8,128)S(1)} fusion(bf16[16,512,256]{2,1,0:T(8,128)(2,1)} %all-gather.4.cloned.1.call-done, bf16[16,256,128]{2,1,0:T(8,128)(2,1)S(1)} %bitcast.107), kind=kOutput, calls=%fused_computation.12 | convolution fusion | flops 536870912 | bytes 5505024 | tf_op jit(solution)/shard_map/ksc,kch->sh/dot_general | solution.py:165
  118.1 1.2 fusion.11
  119.4 0.7 pad_maximum_fusion
  120.1 36.0 %all-gather.6.cloned.1.call-done = bf16[9216,128]{1,0:T(8,128)(2,1)} async-done(((bf16[576,128]{1,0:T(8,128)(2,1)}), bf16[9216,128]{1,0:T(8,128)(2,1)}) %all-gather.6.cloned.1.call-update) | async-done | bytes 2359312 | tf_op jit(solution)/shard_map/all_gather | solution.py:169
  156.1 1.7 slice.44
  157.8 1.4 fusion.9
  159.2 9.2 %all-to-all-start.3 = ((bf16[32,16,256]{2,1,0:T(8,128)(2,1)}), bf16[32,16,256]{2,1,0:T(8,128)(2,1)S(1)}, u32[]{:S(2)}, u32[]{:S(2)}) async-start(bf16[32,16,256]{2,1,0:T(8,128)(2,1)} %fusion.9), calls=%async_computation.3 | async-start | bytes 524288 | tf_op jit(solution)/shard_map/all_to_all | solution.py:180
  168.5 1.0 slice.43
  169.5 0.8 reshape.316
  170.3 8.1 %all-to-all-done.3 = bf16[32,16,256]{2,1,0:T(8,128)(2,1)S(1)} async-done(((bf16[32,16,256]{2,1,0:T(8,128)(2,1)}), bf16[32,16,256]{2,1,0:T(8,128)(2,1)S(1)}, u32[]{:S(2)}, u32[]{:S(2)}) %all-to-all-start.3) | async-done | bytes 262176 | tf_op jit(solution)/shard_map/all_to_all | solution.py:180
  178.4 0.9 convolution_convert_fusion.1
  (54 shorter events, 3.4 us)
Async XLA Ops:
  7.2 107.2 %copy-start = (bf16[1,4096,128]{2,1,0:T(8,128)(2,1)S(1)}, bf16[1,4096,128]{2,1,0:T(8,128)(2,1)}, u32[]{:S(2)}) copy-start(bf16[1,4096,128]{2,1,0:T(8,128)(2,1)} %param.23) | copy-start | bytes 3145732
  7.2 25.3 %copy-start.2 = (bf16[1,4,128,512]{3,2,1,0:T(8,128)(2,1)S(1)}, bf16[1,4,128,512]{3,2,1,0:T(8,128)(2,1)}, u32[]{:S(2)}) copy-start(bf16[1,4,128,512]{3,2,1,0:T(8,128)(2,1)} %param.16) | copy-start | bytes 1572868
  7.2 107.1 %all-gather.4.cloned.1.call-start = ((), (), s32[]{:S(2)}) async-start(), calls=%async_computation.4 | async-start | bytes 4456448 | tf_op jit(solution)/shard_map/all_gather | solution.py:98
  8.4 24.3 %copy-start.5 = (s32[1,64]{1,0:T(1,128)S(1)}, s32[1,64]{1,0:T(1,128)}, u32[]{:S(2)}) copy-start(s32[1,64]{1,0:T(1,128)} %param.18) | copy-start | bytes 772
  37.0 3.1 %copy-start.3 = (bf16[1,4,128,512]{3,2,1,0:T(8,128)(2,1)S(1)}, bf16[1,4,128,512]{3,2,1,0:T(8,128)(2,1)}, u32[]{:S(2)}) copy-start(bf16[1,4,128,512]{3,2,1,0:T(8,128)(2,1)} %param.17) | copy-start | bytes 1572868
  44.8 37.0 %all-to-all-start.1 = ((f32[16,4,2080]{2,1,0:T(4,128)}), f32[16,4,2080]{2,1,0:T(4,128)S(1)}, u32[]{:S(2)}, u32[]{:S(2)}) async-start(f32[16,4,2080]{2,1,0:T(4,128)} %concatenate.49), calls=%async_computation.1 | async-start | bytes 1114112 | tf_op jit(solution)/shard_map/all_to_all | solution.py:151
  81.8 32.0 %all-to-all-start.2 = ((bf16[128,16,256]{0,2,1:T(8,128)(2,1)}), bf16[128,16,256]{0,2,1:T(8,128)(2,1)S(1)}, u32[]{:S(2)}, u32[]{:S(2)}) async-start(bf16[128,16,256]{0,2,1:T(8,128)(2,1)} %bitcast.16), calls=%async_computation.2 | async-start | bytes 2097152 | tf_op jit(solution)/shard_map/all_to_all | solution.py:64
  85.8 70.3 %all-gather.6.cloned.1.call-start = ((), (), s32[]{:S(2)}) async-start(), calls=%async_computation.5 | async-start | bytes 2506752 | tf_op jit(solution)/shard_map/all_gather | solution.py:169
  114.4 3.6 %copy-start.1 = (bf16[16,512,256]{2,1,0:T(8,128)(2,1)S(1)}, bf16[16,512,256]{2,1,0:T(8,128)(2,1)}, u32[]{:S(2)}) copy-start(bf16[16,512,256]{2,1,0:T(8,128)(2,1)} %all-gather.4.cloned.1.call-done) | copy-start | bytes 12582916
  114.4 3.7 %copy-start.4 = (bf16[1,4096,128]{2,1,0:T(8,128)(2,1)S(1)}, bf16[1,4096,128]{2,1,0:T(8,128)(2,1)}, u32[]{:S(2)}) copy-start(bf16[1,4096,128]{2,1,0:T(8,128)(2,1)} %param.24) | copy-start | bytes 3145732
  159.2 19.2 %all-to-all-start.3 = ((bf16[32,16,256]{2,1,0:T(8,128)(2,1)}), bf16[32,16,256]{2,1,0:T(8,128)(2,1)S(1)}, u32[]{:S(2)}, u32[]{:S(2)}) async-start(bf16[32,16,256]{2,1,0:T(8,128)(2,1)} %fusion.9), calls=%async_computation.3 | async-start | bytes 524288 | tf_op jit(solution)/shard_map/all_to_all | solution.py:180
Sparse Core Ops, SparseCore 0:
  30.8 57.8 all-gather.3
  120.2 35.8 all-gather.5

commit v6 on v5

--- a/solution.py
+++ b/solution.py
@@ -35,6 +35,23 @@
         ],
         axis=-1,
     )
+
+
+def bf16_pieces(values, count):
+    pieces = []
+    rest = values
+    for _ in range(count):
+        rounded = lax.reduce_precision(rest, exponent_bits=8, mantissa_bits=7)
+        pieces.append(rounded.astype(jnp.bfloat16))
+        rest = rest - rounded
+    return jnp.stack(pieces, axis=1)
+
+
+def from_pieces(pieces):
+    total = pieces[:, 0].astype(jnp.float32)
+    for index in range(1, pieces.shape[1]):
+        total = total + pieces[:, index].astype(jnp.float32)
+    return total
 
 
 def on_device(
@@ -61,9 +78,7 @@
     score_scale = 1.0 / math.sqrt(HD)
     out_width = w_down.shape[2] // kv_count
     down_split = w_down[0].reshape(w_down.shape[1], kv_count, out_width)
-    down_cols = lax.all_to_all(down_split, "kv", split_axis=1, concat_axis=0, tiled=True).reshape(
-        -1, out_width
-    )
+    down_out = jnp.transpose(down_split, (1, 0, 2)).reshape(kv_count, -1)
     ep_count = lax.axis_size("ep")
     share_count = ep_count // EXPERTS
     tok_rows = moe_rows.shape[0]
@@ -140,20 +155,25 @@
         local_values,
         preferred_element_type=jnp.float32,
     )
-    packed = jnp.concatenate(
-        [
-            part_blend.reshape(all_rows, HQ * HD),
-            part_high.reshape(all_rows, HQ),
-            part_total.reshape(all_rows, HQ),
-        ],
-        axis=1,
+    sums_out = jnp.concatenate(
+        [part_blend.reshape(all_rows, HQ * HD), part_total.reshape(all_rows, HQ)], axis=1
     ).reshape(kv_count, block_rows, -1)
-    parts = lax.all_to_all(packed, "kv", split_axis=0, concat_axis=0, tiled=True).reshape(
-        kv_count, block_rows, -1
-    )
-    parts_blend = parts[..., : HQ * HD].reshape(kv_count, block_rows, HQ, HD)
-    parts_high = parts[..., HQ * HD : HQ * HD + HQ]
-    parts_total = parts[..., HQ * HD + HQ :]
+    high_out = part_high.reshape(kv_count, block_rows, HQ)
+    sums_pieces = bf16_pieces(sums_out, 2)
+    high_pieces = bf16_pieces(high_out, 3)
+    sums_len = 2 * sums_out[0].size
+    high_len = 3 * high_out[0].size
+    outbound = jnp.concatenate(
+        [sums_pieces.reshape(kv_count, -1), high_pieces.reshape(kv_count, -1), down_out], axis=1
+    )
+    inbound = lax.all_to_all(outbound, "kv", split_axis=0, concat_axis=0, tiled=True)
+    parts_sums = from_pieces(inbound[:, :sums_len].reshape((kv_count, 2) + sums_out.shape[1:]))
+    parts_high = from_pieces(
+        inbound[:, sums_len : sums_len + high_len].reshape((kv_count, 3) + high_out.shape[1:])
+    )
+    down_cols = inbound[:, sums_len + high_len :].reshape(-1, out_width)
+    parts_blend = parts_sums[..., : HQ * HD].reshape(kv_count, block_rows, HQ, HD)
+    parts_total = parts_sums[..., HQ * HD :]
     highest = jnp.max(parts_high, axis=0)
     factor = jnp.exp(parts_high - highest[None])
     row_total = jnp.sum(parts_total * factor, axis=0)

time: 189 us -> 215 us (1.14)
  waiting for transfers between devices: 90.1 us -> 49.3 us
  blocking collectives: 20.1 us -> 58 us
  local copies, waits for them, and re-layouts: 13 us -> 40.9 us
  starting transfers between devices: 27.5 us -> 19.8 us
  other arithmetic: 7.7 us -> 14.4 us
    all_to_all x2 -> x1, waiting for transfers between devices: 45.9 us -> 0.01 us  [on_device(): lax.all_to_all(outgoing, 'ep', split_axis=0, concat_axis=0, tiled=True)]
    all_to_all x1, blocking collectives: 20.1 us -> 58 us  [on_device(): lax.all_to_all(outbound, 'kv', split_axis=0, concat_axis=0, tiled=True)]
    unnamed x16 -> x24, local copies, waits for them, and re-layouts: 3.51 us -> 22.2 us
    all_to_all x2 -> x1, starting transfers between devices: 18.2 us -> 10.5 us  [on_device(): lax.all_to_all(outgoing, 'ep', split_axis=0, concat_axis=0, tiled=True)]
    concatenate x6 -> x4, local copies, waits for them, and re-layouts: 1.97 us -> 7.66 us  [the longest x1 7.07 us: on_device(): jnp.concatenate([sums_pieces.reshape(kv_count, -1), high_pieces.reshape(k...]
    all_gather x1, waiting for transfers between devices: 36 us -> 41.1 us  [on_device(): lax.all_gather(jnp.concatenate([hidden, own_out.reshape(-1, hidden_width)...]
    all_to_all x0 -> x1, other arithmetic: none -> 3.95 us  [on_device(): lax.all_to_all(outbound, 'kv', split_axis=0, concat_axis=0, tiled=True)]
    reshape x0 -> x7, local copies, waits for them, and re-layouts: none -> 2.98 us  [the longest x1 1.33 us: on_device(): down_cols = inbound[:, sums_len + high_len:].reshape(-1, out_width)]
  transfers between devices with their start and end apart: 5 -> 4, of which waited for: 4 -> 2; matrix products, arithmetic and copies ran while one was open for 11% -> 26% of each run, Pallas kernels for 0% -> 0%
where the time goes in v6:
time: 215 us; the launch traced here: 211 us
  blocking collectives  58 us (27%)
  waiting for transfers between devices  49.3 us (23%)
  local copies, waits for them, and re-layouts  40.9 us (19%)
  starting transfers between devices  19.8 us (9%)
  between operations  15.1 us (7%)
  other arithmetic  14.4 us (7%)
  matrix products  13.5 us (6%)
    all_to_all x1, blocking collectives, on_device(): lax.all_to_all(outbound, 'kv', split_axis=0, concat_axis=0, tiled=True)  58 us
    all_gather x1, waiting for transfers between devices, on_device(): lax.all_gather(jnp.concatenate([hidden, own_out.reshape(-1, hidden_width)...  41.1 us
    unnamed x24, local copies, waits for them, and re-layouts  22.2 us
    all_to_all x1, starting transfers between devices, on_device(): lax.all_to_all(outgoing, 'ep', split_axis=0, concat_axis=0, tiled=True)  10.5 us
    all_to_all x1, starting transfers between devices, on_device(): lax.all_to_all(summed.reshape(ep_count, CAP, -1).astype(jnp.bfloat16), 'e...  9.21 us
    all_to_all x1, waiting for transfers between devices, on_device(): lax.all_to_all(summed.reshape(ep_count, CAP, -1).astype(jnp.bfloat16), 'e...  8.15 us
    concatenate x1, local copies, waits for them, and re-layouts, on_device(): jnp.concatenate([sums_pieces.reshape(kv_count, -1), high_pieces.reshape(k...  7.07 us
  transfers between devices with their start and end apart: 4, of which 2 were waited for; matrix products, arithmetic and copies ran while one was open for 26% of the time, Pallas kernels for 0%

profile of v6, /device:TPU:1, one launch (start us, length us, event | category | flops | bytes accessed | tf_op | source)
XLA Modules:
  0.0 211.1 jit_solution(8739350294593692694)
XLA Ops:
  7.2 0.9 copy.109
  9.6 1.7 convolution_convert_fusion
  11.2 10.5 %all-to-all-start = ((bf16[32,16,256]{2,1,0:T(8,128)(2,1)}), bf16[32,16,256]{2,1,0:T(8,128)(2,1)S(1)}, u32[]{:S(2)}, u32[]{:S(2)}) async-start(bf16[32,16,256]{2,1,0:T(8,128)(2,1)} %bitcast), calls=%async_computation | async-start | bytes 524288 | tf_op jit(solution)/shard_map/all_to_all | solution.py:110
  22.5 0.8 select_reduce_fusion.2
  23.5 1.0 convert_bitcast_fusion
  24.9 0.8 multiply_cosine_fusion
  26.9 1.1 subtract_convert_fusion
  28.0 2.2 %fusion = (f32[64,4,4]{0,2,1:T(4,128)S(1)}, f32[4,516,64,4]{1,2,3,0:T(8,128)}) fusion(pred[64,516]{1,0:T(8,128)(4,1)S(1)} %compare_and_fusion, bf16[64,4,4,64]{3,0,2,1:T(8,128)(2,1)S(1)} %bitcast.145, bf16[64,4,4,64]{3,0,2,1:T(8,128)(2,1)S(1)} %bitcast.144, bf16[4,4,64]{2,0,1:T(4,128)(2,1)S(1)} %get-tuple-element.32, ...), kind=kOutput, calls=%fused_computation.2 | convolution fusion | flops 138959872 | bytes 2941184 | tf_op jit(solution)/shard_map/nkgd,mkd->nkgm/dot_general | solution.py:144
  30.7 2.5 %fusion.6 = f32[64,4,4,128]{3,0,2,1:T(8,128)S(1)} fusion(f32[4,516,64,4]{1,2,3,0:T(8,128)} %get-tuple-element.38, f32[64,4,4]{0,2,1:T(4,128)S(1)} %get-tuple-element.37, pred[64,516]{1,0:T(8,128)(4,1)S(1)} %compare_and_fusion, bf16[4,4,128]{2,0,1:T(4,128)(2,1)S(1)} %get-tuple-element.46, bf16[512,4,128]{2,0,1:T(8,128)(2,1)S(1)} %copy.111), kind=kOutput, calls=%fused_computation.8 | convolution fusion | flops 138964992 | bytes 3203328 | tf_op jit(solution)/shard_map/nkgm,mkd->nkgd/dot_general | solution.py:152
  34.8 2.6 %fusion.1 = f32[64,4,4]{0,2,1:T(4,128)S(1)} fusion(f32[4,516,64,4]{1,2,3,0:T(8,128)} %get-tuple-element.38, f32[64,4,4]{0,2,1:T(4,128)S(1)} %get-tuple-element.37, pred[64,516]{1,0:T(8,128)(4,1)S(1)} %compare_and_fusion), kind=kLoop, calls=%fused_computation.3 | loop fusion | flops 2640896 | bytes 2154752 | tf_op jit(solution)/shard_map/reduce_sum | solution.py:151
  39.0 1.5 copy.138
  40.6 0.9 constant_dynamic-update-slice_fusion
  41.4 1.3 dynamic-update-slice.1
  42.8 7.1 %dynamic-update-slice.2 = bf16[16,49472]{1,0:T(8,128)(2,1)} dynamic-update-slice(bf16[16,49472]{1,0:T(8,128)(2,1)} %dynamic-update-slice.1, bf16[16,32768]{1,0:T(8,128)(2,1)S(1)} %bitcast.134, s32[]{} %constant.97, s32[]{} %constant.99) | dynamic-update-slice | bytes 2097156 | tf_op jit(solution)/shard_map/concatenate | solution.py:166
  50.3 4.0 %reduce.2 = bf16[16,49472]{1,0:T(8,128)(2,1)} reduce(bf16[16,1,49472]{2,0,1:T(8,128)(2,1)} %bitcast.136, bf16[]{:T(256)} %broadcast.263), dimensions={1}, to_apply=%copy.122.reduce_sub_computation | reduce | bytes 3166210 | tf_op jit(solution)/shard_map/all_to_all | solution.py:169
  54.3 2.6 %reshape.507 = bf16[16,2,24736]{2,1,0:T(2,128)(2,1)S(1)} reshape(bf16[16,49472]{1,0:T(8,128)(2,1)} %reduce.2) | data formatting | bytes 3166208
  56.9 58.0 %all_to_all.22 = bf16[16,2,24736]{2,1,0:T(2,128)(2,1)} all-to-all(bf16[16,2,24736]{2,1,0:T(2,128)(2,1)S(1)} %reshape.507), channel_id=1, replica_groups=mesh['kv'=16,'ep'=32] {'kv'}, dimensions={0} | all-to-all | bytes 3166208 | tf_op jit(solution)/shard_map/all_to_all | solution.py:169
  115.0 11.8 %reshape.508 = bf16[16,1,49472]{2,1,0:T(2,128)(2,1)} reshape(bf16[16,2,24736]{2,1,0:T(2,128)(2,1)} %all_to_all.22) | data formatting | bytes 3166208
  126.8 2.1 copy.150
  130.4 1.0 mul.182
  131.4 1.2 mul.183
  132.6 1.3 reshape.493
  134.2 3.6 %convolution_bitcast_fusion.2 = f32[512,128]{1,0:T(8,128)S(1)} fusion(bf16[16,512,256]{2,1,0:T(8,128)(2,1)} %all-gather.4.cloned.1.call-done, bf16[16,256,128]{2,1,0:T(8,128)(2,1)S(1)} %bitcast.129), kind=kOutput, calls=%fused_computation.13 | convolution fusion | flops 536870912 | bytes 5505024 | tf_op jit(solution)/shard_map/ksc,kch->sh/dot_general | solution.py:185
  137.9 1.2 fusion.11
  139.9 41.1 %all-gather.6.cloned.1.call-done = bf16[9216,128]{1,0:T(8,128)(2,1)} async-done(((bf16[576,128]{1,0:T(8,128)(2,1)}), bf16[9216,128]{1,0:T(8,128)(2,1)}) %all-gather.6.cloned.1.call-update) | async-done | bytes 2359312 | tf_op jit(solution)/shard_map/all_gather | solution.py:189
  181.0 1.7 slice.79
  182.8 1.4 fusion.9
  184.2 9.2 %all-to-all-start.2 = ((bf16[32,16,256]{2,1,0:T(8,128)(2,1)}), bf16[32,16,256]{2,1,0:T(8,128)(2,1)S(1)}, u32[]{:S(2)}, u32[]{:S(2)}) async-start(bf16[32,16,256]{2,1,0:T(8,128)(2,1)} %fusion.9), calls=%async_computation.2 | async-start | bytes 524288 | tf_op jit(solution)/shard_map/all_to_all | solution.py:200
  193.4 1.0 slice.78
  194.4 0.8 reshape.495
  195.2 8.1 %all-to-all-done.2 = bf16[32,16,256]{2,1,0:T(8,128)(2,1)S(1)} async-done(((bf16[32,16,256]{2,1,0:T(8,128)(2,1)}), bf16[32,16,256]{2,1,0:T(8,128)(2,1)S(1)}, u32[]{:S(2)}, u32[]{:S(2)}) %all-to-all-start.2) | async-done | bytes 262176 | tf_op jit(solution)/shard_map/all_to_all | solution.py:200
  203.4 0.9 convolution_convert_fusion.1
  (76 shorter events, 9.9 us)
Async XLA Ops:
  7.2 127.0 %copy-start = (bf16[1,4096,128]{2,1,0:T(8,128)(2,1)S(1)}, bf16[1,4096,128]{2,1,0:T(8,128)(2,1)}, u32[]{:S(2)}) copy-start(bf16[1,4096,128]{2,1,0:T(8,128)(2,1)} %param.23) | copy-start | bytes 3145732
  7.2 18.5 %copy-start.4 = (bf16[1,4,128,512]{3,2,1,0:T(8,128)(2,1)S(1)}, bf16[1,4,128,512]{3,2,1,0:T(8,128)(2,1)}, u32[]{:S(2)}) copy-start(bf16[1,4,128,512]{3,2,1,0:T(8,128)(2,1)} %param.16) | copy-start | bytes 1572868
  11.2 22.0 %all-to-all-start = ((bf16[32,16,256]{2,1,0:T(8,128)(2,1)}), bf16[32,16,256]{2,1,0:T(8,128)(2,1)S(1)}, u32[]{:S(2)}, u32[]{:S(2)}) async-start(bf16[32,16,256]{2,1,0:T(8,128)(2,1)} %bitcast), calls=%async_computation | async-start | bytes 524288 | tf_op jit(solution)/shard_map/all_to_all | solution.py:110
  21.7 112.4 %all-gather.4.cloned.1.call-start = ((), (), s32[]{:S(2)}) async-start(), calls=%async_computation.3 | async-start | bytes 4456448 | tf_op jit(solution)/shard_map/all_gather | solution.py:113
  28.0 2.5 %copy-start.5 = (bf16[1,4,128,512]{3,2,1,0:T(8,128)(2,1)S(1)}, bf16[1,4,128,512]{3,2,1,0:T(8,128)(2,1)}, u32[]{:S(2)}) copy-start(bf16[1,4,128,512]{3,2,1,0:T(8,128)(2,1)} %param.17) | copy-start | bytes 1572868
  33.2 0.7 copy-start.3
  34.0 147.1 %all-gather.6.cloned.1.call-start = ((), (), s32[]{:S(2)}) async-start(), calls=%async_computation.4 | async-start | bytes 2506752 | tf_op jit(solution)/shard_map/all_gather | solution.py:189
  134.2 3.6 %copy-start.1 = (bf16[16,512,256]{2,1,0:T(8,128)(2,1)S(1)}, bf16[16,512,256]{2,1,0:T(8,128)(2,1)}, u32[]{:S(2)}) copy-start(bf16[16,512,256]{2,1,0:T(8,128)(2,1)} %all-gather.4.cloned.1.call-done) | copy-start | bytes 12582916
  134.2 3.7 %copy-start.6 = (bf16[1,4096,128]{2,1,0:T(8,128)(2,1)S(1)}, bf16[1,4096,128]{2,1,0:T(8,128)(2,1)}, u32[]{:S(2)}) copy-start(bf16[1,4096,128]{2,1,0:T(8,128)(2,1)} %param.24) | copy-start | bytes 3145732
  139.2 43.6 %copy-start.2 = (bf16[2048,256]{1,0:T(8,128)(2,1)S(1)}, bf16[2048,256]{1,0:T(8,128)(2,1)}, u32[]{:S(2)}) copy-start(bf16[2048,256]{1,0:T(8,128)(2,1)} %reshape.493) | copy-start | bytes 3145732
  184.2 19.2 %all-to-all-start.2 = ((bf16[32,16,256]{2,1,0:T(8,128)(2,1)}), bf16[32,16,256]{2,1,0:T(8,128)(2,1)S(1)}, u32[]{:S(2)}, u32[]{:S(2)}) async-start(bf16[32,16,256]{2,1,0:T(8,128)(2,1)} %fusion.9), calls=%async_computation.2 | async-start | bytes 524288 | tf_op jit(solution)/shard_map/all_to_all | solution.py:200
Sparse Core Ops, SparseCore 0:
  34.1 65.9 all-gather.3
  140.0 40.9 all-gather.5

commit v7 on v5

--- a/solution.py
+++ b/solution.py
@@ -35,6 +35,34 @@
         ],
         axis=-1,
     )
+
+
+def ring_gather(piece, kv_index, kv_count):
+    z_count = kv_count // 2
+    z_here = kv_index // 2
+    core = kv_index % 2
+    ahead = [(2 * z + c, 2 * ((z + 1) % z_count) + c) for z in range(z_count) for c in range(2)]
+    behind = [(2 * z + c, 2 * ((z - 1) % z_count) + c) for z in range(z_count) for c in range(2)]
+    swap = [(2 * z + c, 2 * z + 1 - c) for z in range(z_count) for c in range(2)]
+    forward_steps = z_count // 2
+    backward_steps = z_count - 1 - forward_steps
+    plane = [piece]
+    sources = [z_here]
+    moving = piece
+    for step in range(1, forward_steps + 1):
+        moving = lax.ppermute(moving, "kv", ahead)
+        plane.append(moving)
+        sources.append((z_here - step) % z_count)
+    moving = piece
+    for step in range(1, backward_steps + 1):
+        moving = lax.ppermute(moving, "kv", behind)
+        plane.append(moving)
+        sources.append((z_here + step) % z_count)
+    own_plane = jnp.stack(plane)
+    other_plane = lax.ppermute(own_plane, "kv", swap)
+    source_z = jnp.stack(sources)
+    piece_ids = jnp.concatenate([2 * source_z + core, 2 * source_z + 1 - core])
+    return jnp.concatenate([own_plane, other_plane]), piece_ids
 
 
 def on_device(
@@ -95,7 +123,7 @@
     arrived_cols = lax.all_to_all(outgoing, "ep", split_axis=0, concat_axis=0, tiled=True).reshape(
         slot_total, -1
     )
-    arrived = lax.all_gather(arrived_cols, "kv", axis=0, tiled=False)
+    arrived, piece_ids = ring_gather(arrived_cols, kv_index, kv_count)
     arrived_cols, queries, new_keys, new_values, cache_keys, cache_values = lax.optimization_barrier(
         (arrived_cols, queries, new_keys, new_values, cache_keys, cache_values)
     )
@@ -160,8 +188,8 @@
     blended = jnp.sum(parts_blend * factor[..., None], axis=0)
     own_out = (blended / row_total[..., None]).reshape(block_rows, HQ * HD).astype(jnp.bfloat16)
     arrived, own_out, down_cols = lax.optimization_barrier((arrived, own_out, down_cols))
-    gate_w = w_gate[0].reshape(kv_count, col_width, -1)
-    up_w = w_up[0].reshape(kv_count, col_width, -1)
+    gate_w = w_gate[0].reshape(kv_count, col_width, -1)[piece_ids]
+    up_w = w_up[0].reshape(kv_count, col_width, -1)[piece_ids]
     gate_proj = jnp.einsum("ksc,kch->sh", arrived, gate_w, preferred_element_type=jnp.float32)
     up_proj = jnp.einsum("ksc,kch->sh", arrived, up_w, preferred_element_type=jnp.float32)
     hidden = (jax.nn.silu(gate_proj) * up_proj).astype(jnp.bfloat16)

time: 189 us -> 218 us (1.15)
  starting transfers between devices: 27.5 us -> 64.8 us
  local copies, waits for them, and re-layouts: 13 us -> 33.2 us
  blocking collectives: 20.1 us -> 0 us
  waiting for transfers between devices: 90.1 us -> 79.1 us
  other arithmetic: 7.7 us -> 12.1 us
  matrix products: 12.8 us -> 10.4 us
    ppermute x0 -> x8, starting transfers between devices: none -> 30.2 us  [the longest x3 17.6 us: ring_gather(): moving = lax.ppermute(moving, 'kv', behind)]
    all_to_all x1, waiting for transfers between devices: 20.5 us -> 0.01 us  [on_device(): lax.all_to_all(packed, 'kv', split_axis=0, concat_axis=0, tiled=True)]
    all_to_all x1 -> x0, blocking collectives: 20.1 us -> none  [on_device(): lax.all_to_all(outgoing, 'ep', split_axis=0, concat_axis=0, tiled=True)]
    ppermute x0 -> x8, waiting for transfers between devices: none -> 11.2 us  [the longest x4 11.2 us: ring_gather(): moving = lax.ppermute(moving, 'kv', ahead)]
    all_to_all x0 -> x1, starting transfers between devices: none -> 10.5 us  [on_device(): lax.all_to_all(outgoing, 'ep', split_axis=0, concat_axis=0, tiled=True)]
    unnamed x16 -> x27, local copies, waits for them, and re-layouts: 3.51 us -> 12.2 us
    all_to_all x1, waiting for transfers between devices: 25.4 us -> 17.8 us  [on_device(): lax.all_to_all(down_split, 'kv', split_axis=1, concat_axis=0, tiled=True)]
    all_to_all x0 -> x1, waiting for transfers between devices: none -> 6.37 us  [on_device(): lax.all_to_all(outgoing, 'ep', split_axis=0, concat_axis=0, tiled=True)]
  transfers between devices with their start and end apart: 5 -> 13, of which waited for: 4 -> 6; matrix products, arithmetic and copies ran while one was open for 11% -> 18% of each run, Pallas kernels for 0% -> 0%
where the time goes in v7:
time: 218 us; the launch traced here: 215 us
  waiting for transfers between devices  79.1 us (36%)
  starting transfers between devices  64.8 us (30%)
  local copies, waits for them, and re-layouts  33.2 us (15%)
  between operations  15.2 us (7%)
  other arithmetic  12.1 us (6%)
  matrix products  10.4 us (5%)
    all_gather x1, waiting for transfers between devices, on_device(): lax.all_gather(jnp.concatenate([hidden, own_out.reshape(-1, hidden_width)...  35.6 us
    all_to_all x1, waiting for transfers between devices, on_device(): lax.all_to_all(down_split, 'kv', split_axis=1, concat_axis=0, tiled=True)  17.8 us
    ppermute x3, starting transfers between devices, ring_gather(): moving = lax.ppermute(moving, 'kv', behind)  17.6 us
    unnamed x27, local copies, waits for them, and re-layouts  12.2 us
    ppermute x4, waiting for transfers between devices, ring_gather(): moving = lax.ppermute(moving, 'kv', ahead)  11.2 us
    all_to_all x1, starting transfers between devices, on_device(): lax.all_to_all(outgoing, 'ep', split_axis=0, concat_axis=0, tiled=True)  10.5 us
    all_to_all x1, starting transfers between devices, on_device(): lax.all_to_all(packed, 'kv', split_axis=0, concat_axis=0, tiled=True)  10.2 us
    ppermute x4, starting transfers between devices, ring_gather(): moving = lax.ppermute(moving, 'kv', ahead)  9.74 us
  transfers between devices with their start and end apart: 13, of which 6 were waited for; matrix products, arithmetic and copies ran while one was open for 18% of the time, Pallas kernels for 0%

profile of v7, /device:TPU:1, one launch (start us, length us, event | category | flops | bytes accessed | tf_op | source)
XLA Modules:
  0.0 214.8 jit_solution(16091327438351563031)
XLA Ops:
  9.5 1.7 convolution_convert_fusion
  11.2 10.5 %all-to-all-start = ((bf16[32,16,256]{2,1,0:T(8,128)(2,1)}), bf16[32,16,256]{2,1,0:T(8,128)(2,1)S(1)}, u32[]{:S(2)}, u32[]{:S(2)}) async-start(bf16[32,16,256]{2,1,0:T(8,128)(2,1)} %bitcast), calls=%async_computation | async-start | bytes 524288 | tf_op jit(solution)/shard_map/all_to_all | solution.py:123
  25.0 6.4 %all-to-all-done = bf16[32,16,256]{2,1,0:T(8,128)(2,1)S(1)} async-done(((bf16[32,16,256]{2,1,0:T(8,128)(2,1)}), bf16[32,16,256]{2,1,0:T(8,128)(2,1)S(1)}, u32[]{:S(2)}, u32[]{:S(2)}) %all-to-all-start) | async-done | bytes 262176 | tf_op jit(solution)/shard_map/all_to_all | solution.py:123
  31.4 4.0 %collective-permute-start = (bf16[512,256]{1,0:T(8,128)(2,1)S(1)}, bf16[512,256]{1,0:T(8,128)(2,1)}, u32[]{:S(2)}, u32[]{:S(2)}) collective-permute-start(bf16[512,256]{1,0:T(8,128)(2,1)S(1)} %bitcast.153), channel_id=1, source_target_pairs={{0,64},{32,96},{64,128},{96,160},{128,192},{160,224},{192,256},{22... | collective-permute-start | bytes 786440 | tf_op jit(solution)/shard_map/ppermute | solution.py:53
  35.4 8.6 %collective-permute-start.4 = (bf16[512,256]{1,0:T(8,128)(2,1)S(1)}, bf16[512,256]{1,0:T(8,128)(2,1)}, u32[]{:S(2)}, u32[]{:S(2)}) collective-permute-start(bf16[512,256]{1,0:T(8,128)(2,1)S(1)} %bitcast.154), channel_id=1, source_target_pairs={{0,448},{32,480},{64,0},{96,32},{128,64},{160,96},{192,128},{224,1... | collective-permute-start | bytes 786440 | tf_op jit(solution)/shard_map/ppermute | solution.py:58
  46.2 1.3 dynamic-slice_bitcast_fusion
  52.2 1.9 collective-permute-start.1
  55.0 4.6 %collective-permute-start.5 = (bf16[512,256]{1,0:T(8,128)(2,1)}, bf16[512,256]{1,0:T(8,128)(2,1)S(1)}, u32[]{:S(2)}, u32[]{:S(2)}) collective-permute-start(bf16[512,256]{1,0:T(8,128)(2,1)} %collective-permute-done.4), channel_id=1, source_target_pairs={{0,448},{32,480},{64,0},{96,32},{128,64},{160,96},{192,128},{224,1... | collective-permute-start | bytes 786440 | tf_op jit(solution)/shard_map/ppermute | solution.py:58
  60.7 1.9 collective-permute-start.2
  65.8 10.2 %all-to-all-start.1 = ((f32[16,4,2080]{2,1,0:T(4,128)}), f32[16,4,2080]{2,1,0:T(4,128)S(1)}, u32[]{:S(2)}, u32[]{:S(2)}) async-start(f32[16,4,2080]{2,1,0:T(4,128)} %concatenate.104), calls=%async_computation.1 | async-start | bytes 1114112 | tf_op jit(solution)/shard_map/all_to_all | solution.py:179
  76.0 1.9 bitcast_dynamic-update-slice_fusion.13
  77.8 4.5 %collective-permute-start.6 = (bf16[512,256]{1,0:T(8,128)(2,1)S(1)}, bf16[512,256]{1,0:T(8,128)(2,1)S(1)}, u32[]{:S(2)}, u32[]{:S(2)}) collective-permute-start(bf16[512,256]{1,0:T(8,128)(2,1)S(1)} %collective-permute-done.5), channel_id=1, source_target_pairs={{0,448},{32,480},{64,0},{96,32},{128,64},{160,96},{192,128},{224,1... | collective-permute-start | bytes 786440 | tf_op jit(solution)/shard_map/ppermute | solution.py:58
  82.3 1.9 collective-permute-start.3
  85.1 1.8 bitcast_dynamic-update-slice_fusion.9
  86.9 10.0 %collective-permute-done.3 = bf16[512,256]{1,0:T(8,128)(2,1)S(1)} collective-permute-done((bf16[512,256]{1,0:T(8,128)(2,1)}, bf16[512,256]{1,0:T(8,128)(2,1)S(1)}, u32[]{:S(2)}, u32[]{:S(2)}) %collective-permute-start.3) | collective-permute-done | bytes 262176 | tf_op jit(solution)/shard_map/ppermute | solution.py:53
  97.8 1.8 bitcast_dynamic-update-slice_fusion.5
  101.3 2.9 %collective-permute-start.7 = (bf16[8,512,256]{2,1,0:T(8,128)(2,1)}, bf16[8,512,256]{2,1,0:T(8,128)(2,1)}, u32[]{:S(2)}, u32[]{:S(2)}) collective-permute-start(bf16[8,512,256]{2,1,0:T(8,128)(2,1)} %get-tuple-element.26), channel_id=1, source_target_pairs={{0,32},{32,0},{64,96},{96,64},{128,160},{160,128},{192,224},{224,1... | collective-permute-start | bytes 6291464 | tf_op jit(solution)/shard_map/ppermute | solution.py:62
  104.2 1.4 copy.56
  106.4 4.7 %all-to-all-start.2 = ((bf16[128,16,256]{0,2,1:T(8,128)(2,1)}), bf16[128,16,256]{0,2,1:T(8,128)(2,1)S(1)}, u32[]{:S(2)}, u32[]{:S(2)}) async-start(bf16[128,16,256]{0,2,1:T(8,128)(2,1)} %bitcast.24), calls=%async_computation.2 | async-start | bytes 2097152 | tf_op jit(solution)/shard_map/all_to_all | solution.py:92
  111.4 1.7 gather_fusion.1
  113.1 2.0 gather_fusion
  117.7 2.0 mul.211
  119.7 1.3 fusion.19
  121.2 17.8 %all-to-all-done.2 = bf16[128,16,256]{0,2,1:T(8,128)(2,1)S(1)} async-done(((bf16[128,16,256]{0,2,1:T(8,128)(2,1)}), bf16[128,16,256]{0,2,1:T(8,128)(2,1)S(1)}, u32[]{:S(2)}, u32[]{:S(2)}) %all-to-all-start.2) | async-done | bytes 1048608 | tf_op jit(solution)/shard_map/all_to_all | solution.py:92
  139.0 1.3 copy.57
  140.4 3.1 %constant_dynamic-update-slice_fusion = bf16[16,512,256]{2,1,0:T(8,128)(2,1)} fusion(bf16[16,512,256]{2,1,0:T(8,128)(2,1)} %get-tuple-element.27, bf16[8,512,256]{2,1,0:T(8,128)(2,1)} %collective-permute-done.7), kind=kLoop, calls=%fused_computation.58 | loop fusion | bytes 4194304 | tf_op jit(solution)/shard_map/concatenate | solution.py:65
  143.5 3.6 %convolution_bitcast_fusion.2 = f32[512,128]{1,0:T(8,128)S(1)} fusion(bf16[16,512,256]{2,1,0:T(8,128)(2,1)} %constant_dynamic-update-slice_fusion, bf16[16,256,128]{2,1,0:T(8,128)(2,1)S(1)} %gather_fusion), kind=kOutput, calls=%fused_computation.14 | convolution fusion | flops 536870912 | bytes 5505024 | tf_op jit(solution)/shard_map/ksc,kch->sh/dot_general | solution.py:193
  149.1 35.6 %all-gather.3.cloned.1.call-done = bf16[9216,128]{1,0:T(8,128)(2,1)} async-done(((bf16[576,128]{1,0:T(8,128)(2,1)}), bf16[9216,128]{1,0:T(8,128)(2,1)}) %all-gather.3.cloned.1.call-update) | async-done | bytes 2359312 | tf_op jit(solution)/shard_map/all_gather | solution.py:197
  184.7 1.7 slice.48
  186.5 1.4 fusion.9
  187.9 9.2 %all-to-all-start.3 = ((bf16[32,16,256]{2,1,0:T(8,128)(2,1)}), bf16[32,16,256]{2,1,0:T(8,128)(2,1)S(1)}, u32[]{:S(2)}, u32[]{:S(2)}) async-start(bf16[32,16,256]{2,1,0:T(8,128)(2,1)} %fusion.9), calls=%async_computation.3 | async-start | bytes 524288 | tf_op jit(solution)/shard_map/all_to_all | solution.py:208
  198.9 8.1 %all-to-all-done.3 = bf16[32,16,256]{2,1,0:T(8,128)(2,1)S(1)} async-done(((bf16[32,16,256]{2,1,0:T(8,128)(2,1)}), bf16[32,16,256]{2,1,0:T(8,128)(2,1)S(1)}, u32[]{:S(2)}, u32[]{:S(2)}) %all-to-all-start.3) | async-done | bytes 262176 | tf_op jit(solution)/shard_map/all_to_all | solution.py:208
  (88 shorter events, 28.9 us)
Async XLA Ops:
  7.2 104.2 %copy-start = (bf16[1,4096,128]{2,1,0:T(8,128)(2,1)S(1)}, bf16[1,4096,128]{2,1,0:T(8,128)(2,1)}, u32[]{:S(2)}) copy-start(bf16[1,4096,128]{2,1,0:T(8,128)(2,1)} %param.24) | copy-start | bytes 3145732
  8.1 37.1 %copy-start.6 = (bf16[1,4,128,512]{3,2,1,0:T(8,128)(2,1)S(1)}, bf16[1,4,128,512]{3,2,1,0:T(8,128)(2,1)}, u32[]{:S(2)}) copy-start(bf16[1,4,128,512]{3,2,1,0:T(8,128)(2,1)} %param.16) | copy-start | bytes 1572868
  11.2 20.2 %all-to-all-start = ((bf16[32,16,256]{2,1,0:T(8,128)(2,1)}), bf16[32,16,256]{2,1,0:T(8,128)(2,1)S(1)}, u32[]{:S(2)}, u32[]{:S(2)}) async-start(bf16[32,16,256]{2,1,0:T(8,128)(2,1)} %bitcast), calls=%async_computation | async-start | bytes 524288 | tf_op jit(solution)/shard_map/all_to_all | solution.py:123
  31.4 20.8 %collective-permute-start = (bf16[512,256]{1,0:T(8,128)(2,1)S(1)}, bf16[512,256]{1,0:T(8,128)(2,1)}, u32[]{:S(2)}, u32[]{:S(2)}) collective-permute-start(bf16[512,256]{1,0:T(8,128)(2,1)S(1)} %bitcast.153), channel_id=1, source_target_pairs={{0,64},{32,96},{64,128},{96,160},{128,192},{160,224},{192,256},{22... | collective-permute-start | bytes 786440 | tf_op jit(solution)/shard_map/ppermute | solution.py:53
  35.4 19.6 %collective-permute-start.4 = (bf16[512,256]{1,0:T(8,128)(2,1)S(1)}, bf16[512,256]{1,0:T(8,128)(2,1)}, u32[]{:S(2)}, u32[]{:S(2)}) collective-permute-start(bf16[512,256]{1,0:T(8,128)(2,1)S(1)} %bitcast.154), channel_id=1, source_target_pairs={{0,448},{32,480},{64,0},{96,32},{128,64},{160,96},{192,128},{224,1... | collective-permute-start | bytes 786440 | tf_op jit(solution)/shard_map/ppermute | solution.py:58
  50.6 0.8 copy-start.7
  52.2 8.5 %collective-permute-start.1 = (bf16[512,256]{1,0:T(8,128)(2,1)}, bf16[512,256]{1,0:T(8,128)(2,1)S(1)}, u32[]{:S(2)}, u32[]{:S(2)}) collective-permute-start(bf16[512,256]{1,0:T(8,128)(2,1)} %collective-permute-done), channel_id=1, source_target_pairs={{0,64},{32,96},{64,128},{96,160},{128,192},{160,224},{192,256},{22... | collective-permute-start | bytes 786440 | tf_op jit(solution)/shard_map/ppermute | solution.py:53
  55.0 22.8 %collective-permute-start.5 = (bf16[512,256]{1,0:T(8,128)(2,1)}, bf16[512,256]{1,0:T(8,128)(2,1)S(1)}, u32[]{:S(2)}, u32[]{:S(2)}) collective-permute-start(bf16[512,256]{1,0:T(8,128)(2,1)} %collective-permute-done.4), channel_id=1, source_target_pairs={{0,448},{32,480},{64,0},{96,32},{128,64},{160,96},{192,128},{224,1... | collective-permute-start | bytes 786440 | tf_op jit(solution)/shard_map/ppermute | solution.py:58
  60.7 21.6 %collective-permute-start.2 = (bf16[512,256]{1,0:T(8,128)(2,1)S(1)}, bf16[512,256]{1,0:T(8,128)(2,1)}, u32[]{:S(2)}, u32[]{:S(2)}) collective-permute-start(bf16[512,256]{1,0:T(8,128)(2,1)S(1)} %collective-permute-done.1), channel_id=1, source_target_pairs={{0,64},{32,96},{64,128},{96,160},{128,192},{160,224},{192,256},{22... | collective-permute-start | bytes 786440 | tf_op jit(solution)/shard_map/ppermute | solution.py:53
  65.8 39.8 %all-to-all-start.1 = ((f32[16,4,2080]{2,1,0:T(4,128)}), f32[16,4,2080]{2,1,0:T(4,128)S(1)}, u32[]{:S(2)}, u32[]{:S(2)}) async-start(f32[16,4,2080]{2,1,0:T(4,128)} %concatenate.104), calls=%async_computation.1 | async-start | bytes 1114112 | tf_op jit(solution)/shard_map/all_to_all | solution.py:179
  76.0 28.2 %copy-start.4 = (bf16[1,128,4096]{2,1,0:T(8,128)(2,1)S(1)}, bf16[1,128,4096]{2,1,0:T(8,128)(2,1)}, u32[]{:S(2)}) copy-start(bf16[1,128,4096]{2,1,0:T(8,128)(2,1)} %param.25) | copy-start | bytes 3145732
  77.8 22.6 %collective-permute-start.6 = (bf16[512,256]{1,0:T(8,128)(2,1)S(1)}, bf16[512,256]{1,0:T(8,128)(2,1)S(1)}, u32[]{:S(2)}, u32[]{:S(2)}) collective-permute-start(bf16[512,256]{1,0:T(8,128)(2,1)S(1)} %collective-permute-done.5), channel_id=1, source_target_pairs={{0,448},{32,480},{64,0},{96,32},{128,64},{160,96},{192,128},{224,1... | collective-permute-start | bytes 786440 | tf_op jit(solution)/shard_map/ppermute | solution.py:58
  82.3 14.6 %collective-permute-start.3 = (bf16[512,256]{1,0:T(8,128)(2,1)}, bf16[512,256]{1,0:T(8,128)(2,1)S(1)}, u32[]{:S(2)}, u32[]{:S(2)}) collective-permute-start(bf16[512,256]{1,0:T(8,128)(2,1)} %collective-permute-done.2), channel_id=1, source_target_pairs={{0,64},{32,96},{64,128},{96,160},{128,192},{160,224},{192,256},{22... | collective-permute-start | bytes 786440 | tf_op jit(solution)/shard_map/ppermute | solution.py:53
  101.3 39.0 %collective-permute-start.7 = (bf16[8,512,256]{2,1,0:T(8,128)(2,1)}, bf16[8,512,256]{2,1,0:T(8,128)(2,1)}, u32[]{:S(2)}, u32[]{:S(2)}) collective-permute-start(bf16[8,512,256]{2,1,0:T(8,128)(2,1)} %get-tuple-element.26), channel_id=1, source_target_pairs={{0,32},{32,0},{64,96},{96,64},{128,160},{160,128},{192,224},{224,1... | collective-permute-start | bytes 6291464 | tf_op jit(solution)/shard_map/ppermute | solution.py:62
  105.6 0.8 copy-start.2
  106.4 32.6 %all-to-all-start.2 = ((bf16[128,16,256]{0,2,1:T(8,128)(2,1)}), bf16[128,16,256]{0,2,1:T(8,128)(2,1)S(1)}, u32[]{:S(2)}, u32[]{:S(2)}) async-start(bf16[128,16,256]{0,2,1:T(8,128)(2,1)} %bitcast.24), calls=%async_computation.2 | async-start | bytes 2097152 | tf_op jit(solution)/shard_map/all_to_all | solution.py:92
  111.0 73.7 %all-gather.3.cloned.1.call-start = ((), (), s32[]{:S(2)}) async-start(), calls=%async_computation.4 | async-start | bytes 2506752 | tf_op jit(solution)/shard_map/all_gather | solution.py:197
  143.4 3.6 %copy-start.1 = (bf16[16,512,256]{2,1,0:T(8,128)(2,1)S(1)}, bf16[16,512,256]{2,1,0:T(8,128)(2,1)}, u32[]{:S(2)}) copy-start(bf16[16,512,256]{2,1,0:T(8,128)(2,1)} %constant_dynamic-update-slice_fusion) | copy-start | bytes 12582916
  143.5 3.7 %copy-start.3 = (bf16[16,256,128]{2,1,0:T(8,128)(2,1)S(1)}, bf16[16,256,128]{2,1,0:T(8,128)(2,1)}, u32[]{:S(2)}) copy-start(bf16[16,256,128]{2,1,0:T(8,128)(2,1)} %gather_fusion.1) | copy-start | bytes 3145732
  148.4 38.0 %copy-start.5 = (bf16[16,128,1,256]{3,1,0,2:T(8,128)(2,1)S(1)}, bf16[16,128,1,256]{3,1,0,2:T(8,128)(2,1)}, u32[]{:S(2)}) copy-start(bf16[16,128,1,256]{3,1,0,2:T(8,128)(2,1)} %copy.57) | copy-start | bytes 3145732
  187.9 19.2 %all-to-all-start.3 = ((bf16[32,16,256]{2,1,0:T(8,128)(2,1)}), bf16[32,16,256]{2,1,0:T(8,128)(2,1)S(1)}, u32[]{:S(2)}, u32[]{:S(2)}) async-start(bf16[32,16,256]{2,1,0:T(8,128)(2,1)} %fusion.9), calls=%async_computation.3 | async-start | bytes 524288 | tf_op jit(solution)/shard_map/all_to_all | solution.py:208
Sparse Core Ops, SparseCore 0:
  149.3 35.3 all-gather.2

commit v8 on v5

--- a/solution.py
+++ b/solution.py
@@ -96,8 +96,10 @@
         slot_total, -1
     )
     arrived = lax.all_gather(arrived_cols, "kv", axis=0, tiled=False)
-    arrived_cols, queries, new_keys, new_values, cache_keys, cache_values = lax.optimization_barrier(
-        (arrived_cols, queries, new_keys, new_values, cache_keys, cache_values)
+    arrived_cols, down_cols, queries, new_keys, new_values, cache_keys, cache_values = (
+        lax.optimization_barrier(
+            (arrived_cols, down_cols, queries, new_keys, new_values, cache_keys, cache_values)
+        )
     )
     slot_ids = kv_index * POOL_DEV + jnp.arange(POOL_DEV, dtype=jnp.int32)
     matches = (page_table[0][:, None] == slot_ids[None, :]).astype(jnp.int32)

time: 189 us -> 193 us (1.021)
  blocking collectives: 20.1 us -> 43.3 us
  waiting for transfers between devices: 90.1 us -> 77.8 us
  starting transfers between devices: 27.5 us -> 23.5 us
    all_to_all x0 -> x1, blocking collectives: none -> 23.2 us  [on_device(): lax.all_to_all(packed, 'kv', split_axis=0, concat_axis=0, tiled=True)]
    all_to_all x1 -> x0, waiting for transfers between devices: 20.5 us -> none  [on_device(): lax.all_to_all(packed, 'kv', split_axis=0, concat_axis=0, tiled=True)]
    all_to_all x1 -> x0, starting transfers between devices: 14.2 us -> none  [on_device(): lax.all_to_all(packed, 'kv', split_axis=0, concat_axis=0, tiled=True)]
    all_to_all x1, waiting for transfers between devices: 25.4 us -> 35.8 us  [on_device(): lax.all_to_all(down_split, 'kv', split_axis=1, concat_axis=0, tiled=True)]
    all_to_all x1, starting transfers between devices: 4 us -> 14.2 us  [on_device(): lax.all_to_all(down_split, 'kv', split_axis=1, concat_axis=0, tiled=True)]
    all_gather x1, waiting for transfers between devices: 36 us -> 33.8 us  [on_device(): lax.all_gather(jnp.concatenate([hidden, own_out.reshape(-1, hidden_width)...]
  transfers between devices with their start and end apart: 5 -> 4, of which waited for: 4 -> 3; matrix products, arithmetic and copies ran while one was open for 11% -> 9% of each run, Pallas kernels for 0% -> 0%
where the time goes in v8:
time: 193 us; the launch traced here: 190 us
  waiting for transfers between devices  77.8 us (40%)
  blocking collectives  43.3 us (22%)
  starting transfers between devices  23.5 us (12%)
  between operations  15 us (8%)
  matrix products  12.8 us (7%)
  local copies, waits for them, and re-layouts  11.2 us (6%)
  other arithmetic  6.8 us (4%)
    all_to_all x1, waiting for transfers between devices, on_device(): lax.all_to_all(down_split, 'kv', split_axis=1, concat_axis=0, tiled=True)  35.8 us
    all_gather x1, waiting for transfers between devices, on_device(): lax.all_gather(jnp.concatenate([hidden, own_out.reshape(-1, hidden_width)...  33.8 us
    all_to_all x1, blocking collectives, on_device(): lax.all_to_all(packed, 'kv', split_axis=0, concat_axis=0, tiled=True)  23.2 us
    all_to_all x1, blocking collectives, on_device(): lax.all_to_all(outgoing, 'ep', split_axis=0, concat_axis=0, tiled=True)  20.1 us
    all_to_all x1, starting transfers between devices, on_device(): lax.all_to_all(down_split, 'kv', split_axis=1, concat_axis=0, tiled=True)  14.2 us
    all_to_all x1, starting transfers between devices, on_device(): lax.all_to_all(summed.reshape(ep_count, CAP, -1).astype(jnp.bfloat16), 'e...  9.23 us
    all_to_all x1, waiting for transfers between devices, on_device(): lax.all_to_all(summed.reshape(ep_count, CAP, -1).astype(jnp.bfloat16), 'e...  8.15 us
  transfers between devices with their start and end apart: 4, of which 3 were waited for; matrix products, arithmetic and copies ran while one was open for 9% of the time, Pallas kernels for 0%

profile of v8, /device:TPU:1, one launch (start us, length us, event | category | flops | bytes accessed | tf_op | source)
XLA Modules:
  0.0 190.4 jit_solution(2903136607906989065)
XLA Ops:
  7.2 0.8 copy.61
  8.7 0.8 select_reduce_fusion
  9.6 1.0 convolution_convert_fusion
  10.5 20.1 %all_to_all.30 = bf16[32,16,256]{2,1,0:T(8,128)(2,1)} all-to-all(bf16[32,16,256]{2,1,0:T(8,128)(2,1)S(1)} %bitcast.116), channel_id=1, replica_groups=mesh['kv'=16,'ep'=32] {'ep'}, dimensions={0} | all-to-all | bytes 524288 | tf_op jit(solution)/shard_map/all_to_all | solution.py:95
  30.6 2.3 %copy.63 = bf16[1,128,4096]{1,2,0:T(8,128)(2,1)} copy(bf16[1,128,4096]{2,1,0:T(8,128)(2,1)} %param.25) | data formatting | bytes 2097152 | tf_op args[12]
  32.9 14.2 %all-to-all-start.1 = ((bf16[128,16,256]{0,2,1:T(8,128)(2,1)}), bf16[128,16,256]{0,2,1:T(8,128)(2,1)S(1)}, u32[]{:S(2)}, u32[]{:S(2)}) async-start(bf16[128,16,256]{0,2,1:T(8,128)(2,1)} %bitcast.2), calls=%async_computation.1 | async-start | bytes 2097152 | tf_op jit(solution)/shard_map/all_to_all | solution.py:64
  47.8 0.2 select_reduce_fusion.2
  48.4 0.2 multiply_cosine_fusion
  48.6 35.8 %all-to-all-done.1 = bf16[128,16,256]{0,2,1:T(8,128)(2,1)S(1)} async-done(((bf16[128,16,256]{0,2,1:T(8,128)(2,1)}), bf16[128,16,256]{0,2,1:T(8,128)(2,1)S(1)}, u32[]{:S(2)}, u32[]{:S(2)}) %all-to-all-start.1) | async-done | bytes 1048608 | tf_op jit(solution)/shard_map/all_to_all | solution.py:64
  84.5 1.3 copy.64
  86.1 0.7 bitcast_convert_fusion
  86.9 0.2 fusion.48
  87.1 0.3 subtract_convert_fusion
  87.5 2.2 %fusion = (f32[64,4,4]{0,2,1:T(4,128)S(1)}, f32[4,516,64,4]{1,2,3,0:T(8,128)}) fusion(pred[64,516]{1,0:T(8,128)(4,1)S(1)} %compare_and_fusion, bf16[64,4,4,64]{3,0,2,1:T(8,128)(2,1)S(1)} %bitcast.118, bf16[64,4,4,64]{3,0,2,1:T(8,128)(2,1)S(1)} %bitcast.117, bf16[4,4,64]{2,0,1:T(4,128)(2,1)S(1)} %get-tuple-element.29, ...), kind=kOutput, calls=%fused_computation.2 | convolution fusion | flops 138959872 | bytes 2941184 | tf_op jit(solution)/shard_map/nkgd,mkd->nkgm/dot_general | solution.py:131
  89.8 2.7 %fusion.1 = f32[64,4,4]{0,2,1:T(4,128)S(1)} fusion(f32[4,516,64,4]{1,2,3,0:T(8,128)} %get-tuple-element.35, f32[64,4,4]{0,2,1:T(4,128)S(1)} %get-tuple-element.34, pred[64,516]{1,0:T(8,128)(4,1)S(1)} %compare_and_fusion), kind=kLoop, calls=%fused_computation.3 | loop fusion | flops 2640896 | bytes 2154752 | tf_op jit(solution)/shard_map/reduce_sum | solution.py:138
  93.0 2.5 %fusion.6 = f32[64,4,4,128]{3,0,2,1:T(8,128)S(1)} fusion(f32[4,516,64,4]{1,2,3,0:T(8,128)} %get-tuple-element.35, f32[64,4,4]{0,2,1:T(4,128)S(1)} %get-tuple-element.34, pred[64,516]{1,0:T(8,128)(4,1)S(1)} %compare_and_fusion, bf16[4,4,128]{2,0,1:T(4,128)(2,1)S(1)} %get-tuple-element.43, bf16[512,4,128]{2,0,1:T(8,128)(2,1)S(1)} %copy.65), kind=kOutput, calls=%fused_computation.7 | convolution fusion | flops 138964992 | bytes 3203328 | tf_op jit(solution)/shard_map/nkgm,mkd->nkgd/dot_general | solution.py:139
  95.5 0.3 copy.69
  95.9 0.3 concatenate.46
  96.4 0.4 concatenate.49
  96.8 23.2 %all_to_all.31 = f32[16,4,2080]{2,1,0:T(4,128)S(1)} all-to-all(f32[16,4,2080]{2,1,0:T(4,128)S(1)} %concatenate.49), channel_id=1, replica_groups=mesh['kv'=16,'ep'=32] {'kv'}, dimensions={0} | all-to-all | bytes 1064960 | tf_op jit(solution)/shard_map/all_to_all | solution.py:153
  120.1 0.2 mul.182
  120.9 3.6 %convolution_bitcast_fusion.2 = f32[512,128]{1,0:T(8,128)S(1)} fusion(bf16[16,512,256]{2,1,0:T(8,128)(2,1)} %all-gather.4.cloned.1.call-done, bf16[16,256,128]{2,1,0:T(8,128)(2,1)S(1)} %bitcast.107), kind=kOutput, calls=%fused_computation.12 | convolution fusion | flops 536870912 | bytes 5505024 | tf_op jit(solution)/shard_map/ksc,kch->sh/dot_general | solution.py:167
  124.6 1.2 fusion.11
  125.8 0.7 pad_maximum_fusion
  126.5 33.8 %all-gather.6.cloned.1.call-done = bf16[9216,128]{1,0:T(8,128)(2,1)} async-done(((bf16[576,128]{1,0:T(8,128)(2,1)}), bf16[9216,128]{1,0:T(8,128)(2,1)}) %all-gather.6.cloned.1.call-update) | async-done | bytes 2359312 | tf_op jit(solution)/shard_map/all_gather | solution.py:171
  160.3 1.7 slice.44
  162.1 1.4 fusion.9
  163.5 9.2 %all-to-all-start.3 = ((bf16[32,16,256]{2,1,0:T(8,128)(2,1)}), bf16[32,16,256]{2,1,0:T(8,128)(2,1)S(1)}, u32[]{:S(2)}, u32[]{:S(2)}) async-start(bf16[32,16,256]{2,1,0:T(8,128)(2,1)} %fusion.9), calls=%async_computation.3 | async-start | bytes 524288 | tf_op jit(solution)/shard_map/all_to_all | solution.py:182
  172.8 1.0 slice.43
  173.8 0.8 reshape.316
  174.6 8.1 %all-to-all-done.3 = bf16[32,16,256]{2,1,0:T(8,128)(2,1)S(1)} async-done(((bf16[32,16,256]{2,1,0:T(8,128)(2,1)}), bf16[32,16,256]{2,1,0:T(8,128)(2,1)S(1)}, u32[]{:S(2)}, u32[]{:S(2)}) %all-to-all-start.3) | async-done | bytes 262176 | tf_op jit(solution)/shard_map/all_to_all | solution.py:182
  182.7 0.9 convolution_convert_fusion.1
  (57 shorter events, 3.1 us)
Async XLA Ops:
  7.2 113.7 %copy-start = (bf16[1,4096,128]{2,1,0:T(8,128)(2,1)S(1)}, bf16[1,4096,128]{2,1,0:T(8,128)(2,1)}, u32[]{:S(2)}) copy-start(bf16[1,4096,128]{2,1,0:T(8,128)(2,1)} %param.23) | copy-start | bytes 3145732
  7.2 113.6 %all-gather.4.cloned.1.call-start = ((), (), s32[]{:S(2)}) async-start(), calls=%async_computation.4 | async-start | bytes 4456448 | tf_op jit(solution)/shard_map/all_gather | solution.py:98
  9.6 38.3 %copy-start.7 = (s32[1,64]{1,0:T(1,128)S(1)}, s32[1,64]{1,0:T(1,128)}, u32[]{:S(2)}) copy-start(s32[1,64]{1,0:T(1,128)} %param.18) | copy-start | bytes 772
  32.9 52.8 %copy-start.5 = (bf16[1,64,2048]{2,1,0:T(8,128)(2,1)S(1)}, bf16[1,64,2048]{2,1,0:T(8,128)(2,1)}, u32[]{:S(2)}) copy-start(bf16[1,64,2048]{2,1,0:T(8,128)(2,1)} %param.13) | copy-start | bytes 786436
  32.9 53.0 %copy-start.3 = (bf16[1,4,128,512]{3,2,1,0:T(8,128)(2,1)S(1)}, bf16[1,4,128,512]{3,2,1,0:T(8,128)(2,1)}, u32[]{:S(2)}) copy-start(bf16[1,4,128,512]{3,2,1,0:T(8,128)(2,1)} %param.16) | copy-start | bytes 1572868
  32.9 51.5 %all-to-all-start.1 = ((bf16[128,16,256]{0,2,1:T(8,128)(2,1)}), bf16[128,16,256]{0,2,1:T(8,128)(2,1)S(1)}, u32[]{:S(2)}, u32[]{:S(2)}) async-start(bf16[128,16,256]{0,2,1:T(8,128)(2,1)} %bitcast.2), calls=%async_computation.1 | async-start | bytes 2097152 | tf_op jit(solution)/shard_map/all_to_all | solution.py:64
  47.1 113.2 %all-gather.6.cloned.1.call-start = ((), (), s32[]{:S(2)}) async-start(), calls=%async_computation.5 | async-start | bytes 2506752 | tf_op jit(solution)/shard_map/all_gather | solution.py:171
  89.7 3.1 %copy-start.4 = (bf16[1,4,128,512]{3,2,1,0:T(8,128)(2,1)S(1)}, bf16[1,4,128,512]{3,2,1,0:T(8,128)(2,1)}, u32[]{:S(2)}) copy-start(bf16[1,4,128,512]{3,2,1,0:T(8,128)(2,1)} %param.17) | copy-start | bytes 1572868
  120.8 3.6 %copy-start.1 = (bf16[16,512,256]{2,1,0:T(8,128)(2,1)S(1)}, bf16[16,512,256]{2,1,0:T(8,128)(2,1)}, u32[]{:S(2)}) copy-start(bf16[16,512,256]{2,1,0:T(8,128)(2,1)} %all-gather.4.cloned.1.call-done) | copy-start | bytes 12582916
  120.8 3.7 %copy-start.6 = (bf16[1,4096,128]{2,1,0:T(8,128)(2,1)S(1)}, bf16[1,4096,128]{2,1,0:T(8,128)(2,1)}, u32[]{:S(2)}) copy-start(bf16[1,4096,128]{2,1,0:T(8,128)(2,1)} %param.24) | copy-start | bytes 3145732
  125.8 36.3 %copy-start.2 = (bf16[16,128,1,256]{3,1,0,2:T(8,128)(2,1)S(1)}, bf16[16,128,1,256]{3,1,0,2:T(8,128)(2,1)}, u32[]{:S(2)}) copy-start(bf16[16,128,1,256]{3,1,0,2:T(8,128)(2,1)} %copy.64) | copy-start | bytes 3145732
  163.5 19.2 %all-to-all-start.3 = ((bf16[32,16,256]{2,1,0:T(8,128)(2,1)}), bf16[32,16,256]{2,1,0:T(8,128)(2,1)S(1)}, u32[]{:S(2)}, u32[]{:S(2)}) async-start(bf16[32,16,256]{2,1,0:T(8,128)(2,1)} %fusion.9), calls=%async_computation.3 | async-start | bytes 524288 | tf_op jit(solution)/shard_map/all_to_all | solution.py:182
Sparse Core Ops, SparseCore 0:
  30.8 67.5 all-gather.3
  126.7 33.6 all-gather.5

commit v9 on v5

--- a/solution.py
+++ b/solution.py
@@ -35,6 +35,23 @@
         ],
         axis=-1,
     )
+
+
+def bf16_pieces(values, count):
+    pieces = []
+    rest = values
+    for _ in range(count):
+        rounded = lax.reduce_precision(rest, exponent_bits=8, mantissa_bits=7)
+        pieces.append(rounded.astype(jnp.bfloat16))
+        rest = rest - rounded
+    return jnp.concatenate(pieces, axis=-1)
+
+
+def from_pieces(pieces):
+    total = pieces[:, 0].astype(jnp.float32)
+    for index in range(1, pieces.shape[1]):
+        total = total + pieces[:, index].astype(jnp.float32)
+    return total
 
 
 def on_device(
@@ -140,20 +157,21 @@
         local_values,
         preferred_element_type=jnp.float32,
     )
+    small = jnp.concatenate(
+        [part_high.reshape(all_rows, HQ), part_total.reshape(all_rows, HQ)], axis=1
+    )
+    small_pieces = bf16_pieces(small, 3)
     packed = jnp.concatenate(
-        [
-            part_blend.reshape(all_rows, HQ * HD),
-            part_high.reshape(all_rows, HQ),
-            part_total.reshape(all_rows, HQ),
-        ],
-        axis=1,
+        [part_blend.reshape(all_rows, HQ * HD).astype(jnp.bfloat16), small_pieces], axis=1
     ).reshape(kv_count, block_rows, -1)
     parts = lax.all_to_all(packed, "kv", split_axis=0, concat_axis=0, tiled=True).reshape(
         kv_count, block_rows, -1
     )
-    parts_blend = parts[..., : HQ * HD].reshape(kv_count, block_rows, HQ, HD)
-    parts_high = parts[..., HQ * HD : HQ * HD + HQ]
-    parts_total = parts[..., HQ * HD + HQ :]
+    parts_blend = parts[..., : HQ * HD].astype(jnp.float32).reshape(kv_count, block_rows, HQ, HD)
+    parts_small = from_pieces(parts[..., HQ * HD :].reshape(kv_count * block_rows, 3, 2 * HQ))
+    parts_small = parts_small.reshape(kv_count, block_rows, 2 * HQ)
+    parts_high = parts_small[..., :HQ]
+    parts_total = parts_small[..., HQ:]
     highest = jnp.max(parts_high, axis=0)
     factor = jnp.exp(parts_high - highest[None])
     row_total = jnp.sum(parts_total * factor, axis=0)

time: 189 us -> 183 us (0.968)
  local copies, waits for them, and re-layouts: 13 us -> 9.83 us
  waiting for transfers between devices: 90.1 us -> 87.2 us
    all_to_all x1, waiting for transfers between devices: 20.5 us -> 13.4 us  [on_device(): lax.all_to_all(packed, 'kv', split_axis=0, concat_axis=0, tiled=True)]
    all_gather x1, waiting for transfers between devices: 36 us -> 39 us  [on_device(): lax.all_gather(jnp.concatenate([hidden, own_out.reshape(-1, hidden_width)...]
  transfers between devices with their start and end apart: 5 -> 5, of which waited for: 4 -> 4; matrix products, arithmetic and copies ran while one was open for 11% -> 10% of each run, Pallas kernels for 0% -> 0%
where the time goes in v9:
time: 183 us; the launch traced here: 180 us
  waiting for transfers between devices  87.2 us (48%)
  starting transfers between devices  27.1 us (15%)
  blocking collectives  20.1 us (11%)
  between operations  15.1 us (8%)
  matrix products  12.9 us (7%)
  local copies, waits for them, and re-layouts  9.83 us (5%)
  other arithmetic  7.86 us (4%)
    all_gather x1, waiting for transfers between devices, on_device(): lax.all_gather(jnp.concatenate([hidden, own_out.reshape(-1, hidden_width)...  39 us
    all_to_all x1, waiting for transfers between devices, on_device(): lax.all_to_all(down_split, 'kv', split_axis=1, concat_axis=0, tiled=True)  26.7 us
    all_to_all x1, blocking collectives, on_device(): lax.all_to_all(outgoing, 'ep', split_axis=0, concat_axis=0, tiled=True)  20.1 us
    all_to_all x1, starting transfers between devices, on_device(): lax.all_to_all(packed, 'kv', split_axis=0, concat_axis=0, tiled=True)  14 us
    all_to_all x1, waiting for transfers between devices, on_device(): lax.all_to_all(packed, 'kv', split_axis=0, concat_axis=0, tiled=True)  13.4 us
    all_to_all x1, starting transfers between devices, on_device(): lax.all_to_all(summed.reshape(ep_count, CAP, -1).astype(jnp.bfloat16), 'e...  9.22 us
    all_to_all x1, waiting for transfers between devices, on_device(): lax.all_to_all(summed.reshape(ep_count, CAP, -1).astype(jnp.bfloat16), 'e...  8.15 us
    all_to_all x1, starting transfers between devices, on_device(): lax.all_to_all(down_split, 'kv', split_axis=1, concat_axis=0, tiled=True)  3.8 us
  transfers between devices with their start and end apart: 5, of which 4 were waited for; matrix products, arithmetic and copies ran while one was open for 10% of the time, Pallas kernels for 0%

profile of v9, /device:TPU:1, one launch (start us, length us, event | category | flops | bytes accessed | tf_op | source)
XLA Modules:
  0.0 180.1 jit_solution(7106286894296346584)
XLA Ops:
  7.3 0.9 copy.76
  8.8 0.8 select_reduce_fusion
  9.6 1.0 convolution_convert_fusion
  10.6 20.1 %all_to_all.30 = bf16[32,16,256]{2,1,0:T(8,128)(2,1)} all-to-all(bf16[32,16,256]{2,1,0:T(8,128)(2,1)S(1)} %bitcast.119), channel_id=1, replica_groups=mesh['kv'=16,'ep'=32] {'ep'}, dimensions={0} | all-to-all | bytes 524288 | tf_op jit(solution)/shard_map/all_to_all | solution.py:112
  31.4 1.0 convert_bitcast_fusion
  33.1 0.7 bitcast_convert_fusion
  34.1 0.2 multiply_cosine_fusion
  34.3 0.2 fusion.54
  34.5 0.3 subtract_convert_fusion
  34.9 2.2 %fusion = (f32[64,4,4]{0,2,1:T(4,128)S(1)}, f32[4,516,64,4]{1,2,3,0:T(8,128)}) fusion(pred[64,516]{1,0:T(8,128)(4,1)S(1)} %compare_and_fusion, bf16[64,4,4,64]{3,0,2,1:T(8,128)(2,1)S(1)} %bitcast.123, bf16[64,4,4,64]{3,0,2,1:T(8,128)(2,1)S(1)} %bitcast.122, bf16[4,4,64]{2,0,1:T(4,128)(2,1)S(1)} %get-tuple-element.30, ...), kind=kOutput, calls=%fused_computation.2 | convolution fusion | flops 138959872 | bytes 2941184 | tf_op jit(solution)/shard_map/nkgd,mkd->nkgm/dot_general | solution.py:146
  37.2 2.7 %fusion.1 = f32[64,4,4]{0,2,1:T(4,128)S(1)} fusion(f32[4,516,64,4]{1,2,3,0:T(8,128)} %get-tuple-element.36, f32[64,4,4]{0,2,1:T(4,128)S(1)} %get-tuple-element.35, pred[64,516]{1,0:T(8,128)(4,1)S(1)} %compare_and_fusion), kind=kLoop, calls=%fused_computation.3 | loop fusion | flops 2640896 | bytes 2154752 | tf_op jit(solution)/shard_map/reduce_sum | solution.py:153
  40.7 2.6 %fusion.10 = bf16[64,4,4,128]{3,0,2,1:T(8,128)(2,1)S(1)} fusion(f32[4,516,64,4]{1,2,3,0:T(8,128)} %get-tuple-element.36, f32[64,4,4]{0,2,1:T(4,128)S(1)} %get-tuple-element.35, pred[64,516]{1,0:T(8,128)(4,1)S(1)} %compare_and_fusion, bf16[4,4,128]{2,0,1:T(4,128)(2,1)S(1)} %get-tuple-element.44, bf16[512,4,128]{2,0,1:T(8,128)(2,1)S(1)} %copy.78), kind=kOutput, calls=%fused_computation.11 | convolution fusion | flops 139096064 | bytes 2941184 | tf_op jit(solution)/shard_map/nkgm,mkd->nkgd/dot_general | solution.py:154
  43.3 0.2 copy.82
  43.6 1.0 concatenate.53
  44.6 14.0 %all-to-all-start.1 = ((bf16[16,4,2144]{2,1,0:T(4,128)(2,1)}), bf16[16,4,2144]{2,1,0:T(4,128)(2,1)S(1)}, u32[]{:S(2)}, u32[]{:S(2)}) async-start(bf16[16,4,2144]{2,1,0:T(4,128)(2,1)} %concatenate.53), calls=%async_computation.1 | async-start | bytes 557056 | tf_op jit(solution)/shard_map/all_to_all | solution.py:167
  58.6 1.3 copy.88
  60.0 13.4 %all-to-all-done.1 = bf16[16,4,2144]{2,1,0:T(4,128)(2,1)S(1)} async-done(((bf16[16,4,2144]{2,1,0:T(4,128)(2,1)}), bf16[16,4,2144]{2,1,0:T(4,128)(2,1)S(1)}, u32[]{:S(2)}, u32[]{:S(2)}) %all-to-all-start.1) | async-done | bytes 274464 | tf_op jit(solution)/shard_map/all_to_all | solution.py:167
  73.3 3.8 %all-to-all-start.2 = ((bf16[128,16,256]{0,2,1:T(8,128)(2,1)}), bf16[128,16,256]{0,2,1:T(8,128)(2,1)S(1)}, u32[]{:S(2)}, u32[]{:S(2)}) async-start(bf16[128,16,256]{0,2,1:T(8,128)(2,1)} %bitcast.17), calls=%async_computation.2 | async-start | bytes 2097152 | tf_op jit(solution)/shard_map/all_to_all | solution.py:81
  77.5 0.2 mul.182
  78.1 26.7 %all-to-all-done.2 = bf16[128,16,256]{0,2,1:T(8,128)(2,1)S(1)} async-done(((bf16[128,16,256]{0,2,1:T(8,128)(2,1)}), bf16[128,16,256]{0,2,1:T(8,128)(2,1)S(1)}, u32[]{:S(2)}, u32[]{:S(2)}) %all-to-all-start.2) | async-done | bytes 1048608 | tf_op jit(solution)/shard_map/all_to_all | solution.py:81
  104.8 0.5 copy.89
  105.4 3.6 %convolution_bitcast_fusion.2 = f32[512,128]{1,0:T(8,128)S(1)} fusion(bf16[16,512,256]{2,1,0:T(8,128)(2,1)} %all-gather.4.cloned.1.call-done, bf16[16,256,128]{2,1,0:T(8,128)(2,1)S(1)} %bitcast.110), kind=kOutput, calls=%fused_computation.13 | convolution fusion | flops 536870912 | bytes 5505024 | tf_op jit(solution)/shard_map/ksc,kch->sh/dot_general | solution.py:183
  109.1 1.2 fusion.14
  110.4 0.7 pad_maximum_fusion
  111.1 39.0 %all-gather.6.cloned.1.call-done = bf16[9216,128]{1,0:T(8,128)(2,1)} async-done(((bf16[576,128]{1,0:T(8,128)(2,1)}), bf16[9216,128]{1,0:T(8,128)(2,1)}) %all-gather.6.cloned.1.call-update) | async-done | bytes 2359312 | tf_op jit(solution)/shard_map/all_gather | solution.py:187
  150.1 1.7 slice.64
  151.8 1.4 fusion.6
  153.2 9.2 %all-to-all-start.3 = ((bf16[32,16,256]{2,1,0:T(8,128)(2,1)}), bf16[32,16,256]{2,1,0:T(8,128)(2,1)S(1)}, u32[]{:S(2)}, u32[]{:S(2)}) async-start(bf16[32,16,256]{2,1,0:T(8,128)(2,1)} %fusion.6), calls=%async_computation.3 | async-start | bytes 524288 | tf_op jit(solution)/shard_map/all_to_all | solution.py:198
  162.5 1.0 slice.63
  163.4 0.8 reshape.341
  164.3 8.1 %all-to-all-done.3 = bf16[32,16,256]{2,1,0:T(8,128)(2,1)S(1)} async-done(((bf16[32,16,256]{2,1,0:T(8,128)(2,1)}), bf16[32,16,256]{2,1,0:T(8,128)(2,1)S(1)}, u32[]{:S(2)}, u32[]{:S(2)}) %all-to-all-start.3) | async-done | bytes 262176 | tf_op jit(solution)/shard_map/all_to_all | solution.py:198
  172.4 0.9 convolution_convert_fusion.1
  (63 shorter events, 3.6 us)
Async XLA Ops:
  7.2 98.2 %copy-start = (bf16[1,4096,128]{2,1,0:T(8,128)(2,1)S(1)}, bf16[1,4096,128]{2,1,0:T(8,128)(2,1)}, u32[]{:S(2)}) copy-start(bf16[1,4096,128]{2,1,0:T(8,128)(2,1)} %param.23) | copy-start | bytes 3145732
  7.2 25.3 %copy-start.3 = (bf16[1,4,128,512]{3,2,1,0:T(8,128)(2,1)S(1)}, bf16[1,4,128,512]{3,2,1,0:T(8,128)(2,1)}, u32[]{:S(2)}) copy-start(bf16[1,4,128,512]{3,2,1,0:T(8,128)(2,1)} %param.16) | copy-start | bytes 1572868
  7.2 98.2 %all-gather.4.cloned.1.call-start = ((), (), s32[]{:S(2)}) async-start(), calls=%async_computation.4 | async-start | bytes 4456448 | tf_op jit(solution)/shard_map/all_gather | solution.py:115
  8.4 24.3 %copy-start.6 = (s32[1,64]{1,0:T(1,128)S(1)}, s32[1,64]{1,0:T(1,128)}, u32[]{:S(2)}) copy-start(s32[1,64]{1,0:T(1,128)} %param.18) | copy-start | bytes 772
  37.1 3.4 %copy-start.4 = (bf16[1,4,128,512]{3,2,1,0:T(8,128)(2,1)S(1)}, bf16[1,4,128,512]{3,2,1,0:T(8,128)(2,1)}, u32[]{:S(2)}) copy-start(bf16[1,4,128,512]{3,2,1,0:T(8,128)(2,1)} %param.17) | copy-start | bytes 1572868
  40.7 17.9 %copy-start.2 = (bf16[1,128,4096]{2,1,0:T(8,128)(2,1)S(1)}, bf16[1,128,4096]{2,1,0:T(8,128)(2,1)}, u32[]{:S(2)}) copy-start(bf16[1,128,4096]{2,1,0:T(8,128)(2,1)} %param.25) | copy-start | bytes 3145732
  44.6 28.8 %all-to-all-start.1 = ((bf16[16,4,2144]{2,1,0:T(4,128)(2,1)}), bf16[16,4,2144]{2,1,0:T(4,128)(2,1)S(1)}, u32[]{:S(2)}, u32[]{:S(2)}) async-start(bf16[16,4,2144]{2,1,0:T(4,128)(2,1)} %concatenate.53), calls=%async_computation.1 | async-start | bytes 557056 | tf_op jit(solution)/shard_map/all_to_all | solution.py:167
  73.3 31.5 %all-to-all-start.2 = ((bf16[128,16,256]{0,2,1:T(8,128)(2,1)}), bf16[128,16,256]{0,2,1:T(8,128)(2,1)S(1)}, u32[]{:S(2)}, u32[]{:S(2)}) async-start(bf16[128,16,256]{0,2,1:T(8,128)(2,1)} %bitcast.17), calls=%async_computation.2 | async-start | bytes 2097152 | tf_op jit(solution)/shard_map/all_to_all | solution.py:81
  77.1 72.9 %all-gather.6.cloned.1.call-start = ((), (), s32[]{:S(2)}) async-start(), calls=%async_computation.5 | async-start | bytes 2506752 | tf_op jit(solution)/shard_map/all_gather | solution.py:187
  105.4 3.6 %copy-start.1 = (bf16[16,512,256]{2,1,0:T(8,128)(2,1)S(1)}, bf16[16,512,256]{2,1,0:T(8,128)(2,1)}, u32[]{:S(2)}) copy-start(bf16[16,512,256]{2,1,0:T(8,128)(2,1)} %all-gather.4.cloned.1.call-done) | copy-start | bytes 12582916
  105.4 3.7 %copy-start.5 = (bf16[1,4096,128]{2,1,0:T(8,128)(2,1)S(1)}, bf16[1,4096,128]{2,1,0:T(8,128)(2,1)}, u32[]{:S(2)}) copy-start(bf16[1,4096,128]{2,1,0:T(8,128)(2,1)} %param.24) | copy-start | bytes 3145732
  153.2 19.2 %all-to-all-start.3 = ((bf16[32,16,256]{2,1,0:T(8,128)(2,1)}), bf16[32,16,256]{2,1,0:T(8,128)(2,1)S(1)}, u32[]{:S(2)}, u32[]{:S(2)}) async-start(bf16[32,16,256]{2,1,0:T(8,128)(2,1)} %fusion.6), calls=%async_computation.3 | async-start | bytes 524288 | tf_op jit(solution)/shard_map/all_to_all | solution.py:198
Sparse Core Ops, SparseCore 0:
  30.8 55.8 all-gather.3
  111.2 38.8 all-gather.5

commit v10 on v9

--- a/solution.py
+++ b/solution.py
@@ -177,7 +177,7 @@
     row_total = jnp.sum(parts_total * factor, axis=0)
     blended = jnp.sum(parts_blend * factor[..., None], axis=0)
     own_out = (blended / row_total[..., None]).reshape(block_rows, HQ * HD).astype(jnp.bfloat16)
-    arrived, own_out, down_cols = lax.optimization_barrier((arrived, own_out, down_cols))
+    arrived, own_out = lax.optimization_barrier((arrived, own_out))
     gate_w = w_gate[0].reshape(kv_count, col_width, -1)
     up_w = w_up[0].reshape(kv_count, col_width, -1)
     gate_proj = jnp.einsum("ksc,kch->sh", arrived, gate_w, preferred_element_type=jnp.float32)

time: 183 us -> 176 us (0.962)
  blocking collectives: 20.1 us -> 49 us
  waiting for transfers between devices: 87.2 us -> 62.8 us
  starting transfers between devices: 27.1 us -> 15 us
    all_to_all x0 -> x1, blocking collectives: none -> 28.9 us  [on_device(): lax.all_to_all(packed, 'kv', split_axis=0, concat_axis=0, tiled=True)]
    all_to_all x1, waiting for transfers between devices: 26.7 us -> 0.01 us  [on_device(): lax.all_to_all(down_split, 'kv', split_axis=1, concat_axis=0, tiled=True)]
    all_to_all x1 -> x0, starting transfers between devices: 14 us -> none  [on_device(): lax.all_to_all(packed, 'kv', split_axis=0, concat_axis=0, tiled=True)]
    all_to_all x1 -> x0, waiting for transfers between devices: 13.4 us -> none  [on_device(): lax.all_to_all(packed, 'kv', split_axis=0, concat_axis=0, tiled=True)]
    all_gather x1, waiting for transfers between devices: 0.02 us -> 9.72 us  [on_device(): arrived = lax.all_gather(arrived_cols, 'kv', axis=0, tiled=False)]
    all_gather x1, waiting for transfers between devices: 39 us -> 44.9 us  [on_device(): lax.all_gather(jnp.concatenate([hidden, own_out.reshape(-1, hidden_width)...]
  transfers between devices with their start and end apart: 5 -> 4, of which waited for: 4 -> 3; matrix products, arithmetic and copies ran while one was open for 10% -> 11% of each run, Pallas kernels for 0% -> 0%
where the time goes in v10:
time: 176 us; the launch traced here: 173 us
  waiting for transfers between devices  62.8 us (36%)
  blocking collectives  49 us (28%)
  between operations  15.1 us (9%)
  starting transfers between devices  15 us (9%)
  matrix products  14 us (8%)
  local copies, waits for them, and re-layouts  9.34 us (5%)
  other arithmetic  7.86 us (4%)
    all_gather x1, waiting for transfers between devices, on_device(): lax.all_gather(jnp.concatenate([hidden, own_out.reshape(-1, hidden_width)...  44.9 us
    all_to_all x1, blocking collectives, on_device(): lax.all_to_all(packed, 'kv', split_axis=0, concat_axis=0, tiled=True)  28.9 us
    all_to_all x1, blocking collectives, on_device(): lax.all_to_all(outgoing, 'ep', split_axis=0, concat_axis=0, tiled=True)  20.1 us
    all_to_all x1, starting transfers between devices, on_device(): lax.all_to_all(summed.reshape(ep_count, CAP, -1).astype(jnp.bfloat16), 'e...  10.5 us
    all_gather x1, waiting for transfers between devices, on_device(): arrived = lax.all_gather(arrived_cols, 'kv', axis=0, tiled=False)  9.72 us
    all_to_all x1, waiting for transfers between devices, on_device(): lax.all_to_all(summed.reshape(ep_count, CAP, -1).astype(jnp.bfloat16), 'e...  8.15 us
    all_to_all x1, starting transfers between devices, on_device(): lax.all_to_all(down_split, 'kv', split_axis=1, concat_axis=0, tiled=True)  4.34 us
    dot_general x1, matrix products, on_device(): jnp.einsum('ksc,kch->sh', arrived, gate_w, preferred_element_type=jnp.flo...  3.58 us
  transfers between devices with their start and end apart: 4, of which 3 were waited for; matrix products, arithmetic and copies ran while one was open for 11% of the time, Pallas kernels for 0%

profile of v10, /device:TPU:1, one launch (start us, length us, event | category | flops | bytes accessed | tf_op | source)
XLA Modules:
  0.0 173.0 jit_solution(17011047584477261563)
XLA Ops:
  7.3 0.9 copy.64
  8.8 0.8 select_reduce_fusion
  9.6 1.0 convolution_convert_fusion
  10.6 20.1 %all_to_all.30 = bf16[32,16,256]{2,1,0:T(8,128)(2,1)} all-to-all(bf16[32,16,256]{2,1,0:T(8,128)(2,1)S(1)} %bitcast.119), channel_id=1, replica_groups=mesh['kv'=16,'ep'=32] {'ep'}, dimensions={0} | all-to-all | bytes 524288 | tf_op jit(solution)/shard_map/all_to_all | solution.py:112
  31.4 1.0 convert_bitcast_fusion
  33.1 0.7 bitcast_convert_fusion
  34.2 0.2 multiply_cosine_fusion
  34.4 0.2 fusion.55
  34.6 0.3 subtract_convert_fusion
  34.9 2.2 %fusion = (f32[64,4,4]{0,2,1:T(4,128)S(1)}, f32[4,516,64,4]{1,2,3,0:T(8,128)}) fusion(pred[64,516]{1,0:T(8,128)(4,1)S(1)} %compare_and_fusion, bf16[64,4,4,64]{3,0,2,1:T(8,128)(2,1)S(1)} %bitcast.123, bf16[64,4,4,64]{3,0,2,1:T(8,128)(2,1)S(1)} %bitcast.122, bf16[4,4,64]{2,0,1:T(4,128)(2,1)S(1)} %get-tuple-element.28, ...), kind=kOutput, calls=%fused_computation.2 | convolution fusion | flops 138959872 | bytes 2941184 | tf_op jit(solution)/shard_map/nkgd,mkd->nkgm/dot_general | solution.py:146
  37.2 2.7 %fusion.1 = f32[64,4,4]{0,2,1:T(4,128)S(1)} fusion(f32[4,516,64,4]{1,2,3,0:T(8,128)} %get-tuple-element.34, f32[64,4,4]{0,2,1:T(4,128)S(1)} %get-tuple-element.33, pred[64,516]{1,0:T(8,128)(4,1)S(1)} %compare_and_fusion), kind=kLoop, calls=%fused_computation.3 | loop fusion | flops 2640896 | bytes 2154752 | tf_op jit(solution)/shard_map/reduce_sum | solution.py:153
  40.0 0.2 copy.72
  40.7 2.5 %fusion.10 = bf16[64,4,4,128]{3,0,2,1:T(8,128)(2,1)S(1)} fusion(f32[4,516,64,4]{1,2,3,0:T(8,128)} %get-tuple-element.34, f32[64,4,4]{0,2,1:T(4,128)S(1)} %get-tuple-element.33, pred[64,516]{1,0:T(8,128)(4,1)S(1)} %compare_and_fusion, bf16[4,4,128]{2,0,1:T(4,128)(2,1)S(1)} %get-tuple-element.42, bf16[512,4,128]{2,0,1:T(8,128)(2,1)S(1)} %copy.66), kind=kOutput, calls=%fused_computation.11 | convolution fusion | flops 139096064 | bytes 2941184 | tf_op jit(solution)/shard_map/nkgm,mkd->nkgd/dot_general | solution.py:154
  43.3 0.2 copy.70
  43.6 0.4 concatenate.53
  43.9 28.9 %all_to_all.31 = bf16[16,4,2144]{2,1,0:T(4,128)(2,1)S(1)} all-to-all(bf16[16,4,2144]{2,1,0:T(4,128)(2,1)S(1)} %concatenate.53), channel_id=1, replica_groups=mesh['kv'=16,'ep'=32] {'kv'}, dimensions={0} | all-to-all | bytes 548864 | tf_op jit(solution)/shard_map/all_to_all | solution.py:167
  73.1 0.2 mul.182
  73.8 9.7 %all-gather.4.cloned.1.call-done = bf16[16,512,256]{2,1,0:T(8,128)(2,1)} async-done(((bf16[1,512,256]{2,1,0:T(8,128)(2,1)}), bf16[16,512,256]{2,1,0:T(8,128)(2,1)}) %all-gather.4.cloned.1.call-update) | async-done | bytes 4194320 | tf_op jit(solution)/shard_map/all_gather | solution.py:115
  83.5 3.6 %convolution_bitcast_fusion.2 = f32[512,128]{1,0:T(8,128)S(1)} fusion(bf16[16,512,256]{2,1,0:T(8,128)(2,1)} %all-gather.4.cloned.1.call-done, bf16[16,256,128]{2,1,0:T(8,128)(2,1)S(1)} %bitcast.111), kind=kOutput, calls=%fused_computation.13 | convolution fusion | flops 536870912 | bytes 5505024 | tf_op jit(solution)/shard_map/ksc,kch->sh/dot_general | solution.py:183
  87.3 1.2 fusion.14
  88.5 0.7 pad_maximum_fusion
  89.2 0.7 copy.77
  89.9 1.3 copy.78
  91.2 4.3 %all-to-all-start.2 = ((bf16[128,16,256]{2,0,1:T(8,128)(2,1)}), bf16[128,16,256]{2,0,1:T(8,128)(2,1)}, u32[]{:S(2)}, u32[]{:S(2)}) async-start(bf16[128,16,256]{2,0,1:T(8,128)(2,1)} %copy.78), calls=%async_computation.2 | async-start | bytes 2097152 | tf_op jit(solution)/shard_map/all_to_all | solution.py:81
  95.6 44.9 %all-gather.6.cloned.1.call-done = bf16[9216,128]{1,0:T(8,128)(2,1)} async-done(((bf16[576,128]{1,0:T(8,128)(2,1)}), bf16[9216,128]{1,0:T(8,128)(2,1)}) %all-gather.6.cloned.1.call-update) | async-done | bytes 2359312 | tf_op jit(solution)/shard_map/all_gather | solution.py:187
  140.4 1.7 %slice.64 = bf16[16,512,128]{2,1,0:T(8,128)(2,1)S(1)} slice(bf16[16,576,128]{2,1,0:T(8,128)(2,1)} %bitcast.114), slice={[0:16], [0:512], [0:128]} | slice | bytes 4194304 | tf_op jit(solution)/shard_map/slice | solution.py:193
  142.2 2.6 %fusion.6 = bf16[32,16,256]{2,1,0:T(8,128)(2,1)} fusion(bf16[32,16,128,16]{2,1,0,3:T(8,128)(2,1)S(1)} %bitcast.116, bf16[128,16,256]{2,0,1:T(8,128)(2,1)} %all-to-all-done.2), kind=kOutput, calls=%fused_computation.9 | convolution fusion | flops 537001984 | bytes 3407872 | tf_op jit(solution)/shard_map/ksh,khc->sc/dot_general | solution.py:191
  144.8 10.5 %all-to-all-start.3 = ((bf16[32,16,256]{2,1,0:T(8,128)(2,1)}), bf16[32,16,256]{2,1,0:T(8,128)(2,1)S(1)}, u32[]{:S(2)}, u32[]{:S(2)}) async-start(bf16[32,16,256]{2,1,0:T(8,128)(2,1)} %fusion.6), calls=%async_computation.3 | async-start | bytes 524288 | tf_op jit(solution)/shard_map/all_to_all | solution.py:198
  155.4 1.0 slice.63
  156.4 0.8 reshape.334
  157.2 8.1 %all-to-all-done.3 = bf16[32,16,256]{2,1,0:T(8,128)(2,1)S(1)} async-done(((bf16[32,16,256]{2,1,0:T(8,128)(2,1)}), bf16[32,16,256]{2,1,0:T(8,128)(2,1)S(1)}, u32[]{:S(2)}, u32[]{:S(2)}) %all-to-all-start.3) | async-done | bytes 262176 | tf_op jit(solution)/shard_map/all_to_all | solution.py:198
  165.3 0.9 convolution_convert_fusion.1
  (62 shorter events, 3.4 us)
Async XLA Ops:
  7.2 76.3 %copy-start = (bf16[1,4096,128]{2,1,0:T(8,128)(2,1)S(1)}, bf16[1,4096,128]{2,1,0:T(8,128)(2,1)}, u32[]{:S(2)}) copy-start(bf16[1,4096,128]{2,1,0:T(8,128)(2,1)} %param.23) | copy-start | bytes 3145732
  7.2 25.3 %copy-start.3 = (bf16[1,4,128,512]{3,2,1,0:T(8,128)(2,1)S(1)}, bf16[1,4,128,512]{3,2,1,0:T(8,128)(2,1)}, u32[]{:S(2)}) copy-start(bf16[1,4,128,512]{3,2,1,0:T(8,128)(2,1)} %param.16) | copy-start | bytes 1572868
  7.2 76.3 %all-gather.4.cloned.1.call-start = ((), (), s32[]{:S(2)}) async-start(), calls=%async_computation.4 | async-start | bytes 4456448 | tf_op jit(solution)/shard_map/all_gather | solution.py:115
  8.4 24.3 %copy-start.6 = (s32[1,64]{1,0:T(1,128)S(1)}, s32[1,64]{1,0:T(1,128)}, u32[]{:S(2)}) copy-start(s32[1,64]{1,0:T(1,128)} %param.18) | copy-start | bytes 772
  30.7 109.7 %all-gather.6.cloned.1.call-start = ((), (), s32[]{:S(2)}) async-start(), calls=%async_computation.5 | async-start | bytes 2506752 | tf_op jit(solution)/shard_map/all_gather | solution.py:187
  37.1 3.4 %copy-start.4 = (bf16[1,4,128,512]{3,2,1,0:T(8,128)(2,1)S(1)}, bf16[1,4,128,512]{3,2,1,0:T(8,128)(2,1)}, u32[]{:S(2)}) copy-start(bf16[1,4,128,512]{3,2,1,0:T(8,128)(2,1)} %param.17) | copy-start | bytes 1572868
  83.5 3.6 %copy-start.1 = (bf16[16,512,256]{2,1,0:T(8,128)(2,1)S(1)}, bf16[16,512,256]{2,1,0:T(8,128)(2,1)}, u32[]{:S(2)}) copy-start(bf16[16,512,256]{2,1,0:T(8,128)(2,1)} %all-gather.4.cloned.1.call-done) | copy-start | bytes 12582916
  83.5 3.7 %copy-start.5 = (bf16[1,4096,128]{2,1,0:T(8,128)(2,1)S(1)}, bf16[1,4096,128]{2,1,0:T(8,128)(2,1)}, u32[]{:S(2)}) copy-start(bf16[1,4096,128]{2,1,0:T(8,128)(2,1)} %param.24) | copy-start | bytes 3145732
  87.3 2.0 %copy-start.2 = (bf16[1,128,4096]{2,1,0:T(8,128)(2,1)S(1)}, bf16[1,128,4096]{2,1,0:T(8,128)(2,1)}, u32[]{:S(2)}) copy-start(bf16[1,128,4096]{2,1,0:T(8,128)(2,1)} %param.25) | copy-start | bytes 3145732
  91.2 51.0 %all-to-all-start.2 = ((bf16[128,16,256]{2,0,1:T(8,128)(2,1)}), bf16[128,16,256]{2,0,1:T(8,128)(2,1)}, u32[]{:S(2)}, u32[]{:S(2)}) async-start(bf16[128,16,256]{2,0,1:T(8,128)(2,1)} %copy.78), calls=%async_computation.2 | async-start | bytes 2097152 | tf_op jit(solution)/shard_map/all_to_all | solution.py:81
  144.8 20.5 %all-to-all-start.3 = ((bf16[32,16,256]{2,1,0:T(8,128)(2,1)}), bf16[32,16,256]{2,1,0:T(8,128)(2,1)S(1)}, u32[]{:S(2)}, u32[]{:S(2)}) async-start(bf16[32,16,256]{2,1,0:T(8,128)(2,1)} %fusion.6), calls=%async_computation.3 | async-start | bytes 524288 | tf_op jit(solution)/shard_map/all_to_all | solution.py:198
Sparse Core Ops, SparseCore 0:
  30.8 52.6 all-gather.3
  89.3 51.0 all-gather.5

commit v11 on v10

--- a/solution.py
+++ b/solution.py
@@ -184,24 +184,38 @@
     up_proj = jnp.einsum("ksc,kch->sh", arrived, up_w, preferred_element_type=jnp.float32)
     hidden = (jax.nn.silu(gate_proj) * up_proj).astype(jnp.bfloat16)
     hidden_width = hidden.shape[1]
-    joined = lax.all_gather(
-        jnp.concatenate([hidden, own_out.reshape(-1, hidden_width)], axis=0), "kv", axis=0, tiled=False
-    )
-    attn_out = joined[:, slot_total:].reshape(1, all_rows, HQ * HD)
-    summed = jnp.einsum(
-        "ksh,khc->sc",
-        joined[:, :slot_total],
-        down_cols.reshape(kv_count, -1, out_width),
-        preferred_element_type=jnp.float32,
-    )
-    returned = (
-        lax.all_to_all(
-            summed.reshape(ep_count, CAP, -1).astype(jnp.bfloat16),
+    half_cap = CAP // 2
+    by_rank = hidden.reshape(ep_count, CAP, hidden_width)
+    half_slots = ep_count * half_cap
+    down_blocks = down_cols.reshape(kv_count, -1, out_width)
+    first = lax.all_gather(
+        jnp.concatenate(
+            [by_rank[:, :half_cap].reshape(half_slots, hidden_width), own_out.reshape(-1, hidden_width)],
+            axis=0,
+        ),
+        "kv",
+        axis=0,
+        tiled=False,
+    )
+    second = lax.all_gather(
+        by_rank[:, half_cap:].reshape(half_slots, hidden_width), "kv", axis=0, tiled=False
+    )
+    attn_out = first[:, half_slots:].reshape(1, all_rows, HQ * HD)
+
+    def project_back(gathered):
+        summed = jnp.einsum(
+            "ksh,khc->sc", gathered, down_blocks, preferred_element_type=jnp.float32
+        )
+        return lax.all_to_all(
+            summed.reshape(ep_count, half_cap, -1).astype(jnp.bfloat16),
             "ep",
             split_axis=0,
             concat_axis=0,
             tiled=True,
         )
+
+    returned = (
+        jnp.concatenate([project_back(first[:, :half_slots]), project_back(second)], axis=1)
         .astype(jnp.float32)
         .reshape(slot_total, -1)
     )

time: 176 us -> 205 us (1.16)
  blocking collectives: 49 us -> 85.3 us
  waiting for transfers between devices: 62.8 us -> 54.2 us
  starting transfers between devices: 15 us -> 18 us
    all_to_all x0 -> x1, blocking collectives: none -> 36.3 us  [on_device(): lax.all_to_all(down_split, 'kv', split_axis=1, concat_axis=0, tiled=True)]
    all_gather x1 -> x2, waiting for transfers between devices: 44.9 us -> 36.8 us  [the longest x1 30.7 us: on_device(): lax.all_gather(jnp.concatenate([by_rank[:, :half_cap].reshape(half_slots,...]
    all_to_all x2, starting transfers between devices: 14.9 us -> 17.9 us  [project_back(): lax.all_to_all(summed.reshape(ep_count, half_cap, -1).astype(jnp.bfloat16...]
    dot_general x1 -> x2, matrix products: 2.64 us -> 4.64 us  [project_back(): jnp.einsum('ksh,khc->sc', gathered, down_blocks, preferred_element_type=j...]
  transfers between devices with their start and end apart: 4 -> 5, of which waited for: 3 -> 4; matrix products, arithmetic and copies ran while one was open for 11% -> 11% of each run, Pallas kernels for 0% -> 0%
where the time goes in v11:
time: 205 us; the launch traced here: 204 us
  blocking collectives  85.3 us (42%)
  waiting for transfers between devices  54.2 us (26%)
  starting transfers between devices  18 us (9%)
  matrix products  16 us (8%)
  between operations  14.8 us (7%)
  other arithmetic  7.85 us (4%)
  local copies, waits for them, and re-layouts  7.46 us (4%)
    all_to_all x1, blocking collectives, on_device(): lax.all_to_all(down_split, 'kv', split_axis=1, concat_axis=0, tiled=True)  36.3 us
    all_gather x1, waiting for transfers between devices, on_device(): lax.all_gather(jnp.concatenate([by_rank[:, :half_cap].reshape(half_slots,...  30.7 us
    all_to_all x1, blocking collectives, on_device(): lax.all_to_all(packed, 'kv', split_axis=0, concat_axis=0, tiled=True)  28.9 us
    all_to_all x1, blocking collectives, on_device(): lax.all_to_all(outgoing, 'ep', split_axis=0, concat_axis=0, tiled=True)  20.1 us
    all_to_all x2, starting transfers between devices, project_back(): lax.all_to_all(summed.reshape(ep_count, half_cap, -1).astype(jnp.bfloat16...  17.9 us
    all_gather x1, waiting for transfers between devices, on_device(): arrived = lax.all_gather(arrived_cols, 'kv', axis=0, tiled=False)  9.96 us
    all_to_all x2, waiting for transfers between devices, project_back(): lax.all_to_all(summed.reshape(ep_count, half_cap, -1).astype(jnp.bfloat16...  7.36 us
    all_gather x1, waiting for transfers between devices, on_device(): lax.all_gather(by_rank[:, half_cap:].reshape(half_slots, hidden_width), '...  6.07 us
  transfers between devices with their start and end apart: 5, of which 4 were waited for; matrix products, arithmetic and copies ran while one was open for 11% of the time, Pallas kernels for 0%

profile of v11, /device:TPU:1, one launch (start us, length us, event | category | flops | bytes accessed | tf_op | source)
XLA Modules:
  0.0 203.7 jit_solution(3459130399514620270)
XLA Ops:
  7.3 0.9 copy.84
  8.8 0.8 select_reduce_fusion
  9.6 1.0 convolution_convert_fusion
  10.6 20.1 %all_to_all.35 = bf16[32,16,256]{2,1,0:T(8,128)(2,1)} all-to-all(bf16[32,16,256]{2,1,0:T(8,128)(2,1)S(1)} %bitcast.136), channel_id=1, replica_groups=mesh['kv'=16,'ep'=32] {'ep'}, dimensions={0} | all-to-all | bytes 524288 | tf_op jit(solution)/shard_map/all_to_all | solution.py:112
  31.4 1.0 convert_bitcast_fusion
  33.1 0.7 bitcast_convert_fusion
  34.4 0.2 fusion.58
  34.6 0.3 subtract_convert_fusion
  34.9 2.2 %fusion = (f32[64,4,4]{0,2,1:T(4,128)S(1)}, f32[4,516,64,4]{1,2,3,0:T(8,128)}) fusion(pred[64,516]{1,0:T(8,128)(4,1)S(1)} %compare_and_fusion, bf16[64,4,4,64]{3,0,2,1:T(8,128)(2,1)S(1)} %bitcast.140, bf16[64,4,4,64]{3,0,2,1:T(8,128)(2,1)S(1)} %bitcast.139, bf16[4,4,64]{2,0,1:T(4,128)(2,1)S(1)} %get-tuple-element.30, ...), kind=kOutput, calls=%fused_computation.2 | convolution fusion | flops 138959872 | bytes 2941184 | tf_op jit(solution)/shard_map/nkgd,mkd->nkgm/dot_general | solution.py:146
  37.2 2.7 %fusion.1 = f32[64,4,4]{0,2,1:T(4,128)S(1)} fusion(f32[4,516,64,4]{1,2,3,0:T(8,128)} %get-tuple-element.36, f32[64,4,4]{0,2,1:T(4,128)S(1)} %get-tuple-element.35, pred[64,516]{1,0:T(8,128)(4,1)S(1)} %compare_and_fusion), kind=kLoop, calls=%fused_computation.3 | loop fusion | flops 2640896 | bytes 2154752 | tf_op jit(solution)/shard_map/reduce_sum | solution.py:153
  40.8 2.5 %fusion.9 = bf16[64,4,4,128]{3,0,2,1:T(8,128)(2,1)S(1)} fusion(f32[4,516,64,4]{1,2,3,0:T(8,128)} %get-tuple-element.36, f32[64,4,4]{0,2,1:T(4,128)S(1)} %get-tuple-element.35, pred[64,516]{1,0:T(8,128)(4,1)S(1)} %compare_and_fusion, bf16[4,4,128]{2,0,1:T(4,128)(2,1)S(1)} %get-tuple-element.44, bf16[512,4,128]{2,0,1:T(8,128)(2,1)S(1)} %copy.86), kind=kOutput, calls=%fused_computation.9 | convolution fusion | flops 139096064 | bytes 2941184 | tf_op jit(solution)/shard_map/nkgm,mkd->nkgd/dot_general | solution.py:154
  43.3 0.2 copy.90
  43.6 0.4 concatenate.56
  43.9 28.9 %all_to_all.36 = bf16[16,4,2144]{2,1,0:T(4,128)(2,1)S(1)} all-to-all(bf16[16,4,2144]{2,1,0:T(4,128)(2,1)S(1)} %concatenate.56), channel_id=1, replica_groups=mesh['kv'=16,'ep'=32] {'kv'}, dimensions={0} | all-to-all | bytes 548864 | tf_op jit(solution)/shard_map/all_to_all | solution.py:167
  73.8 10.0 %all-gather.5.cloned.1.call-done = bf16[16,512,256]{2,1,0:T(8,128)(2,1)} async-done(((bf16[1,512,256]{2,1,0:T(8,128)(2,1)}), bf16[16,512,256]{2,1,0:T(8,128)(2,1)}) %all-gather.5.cloned.1.call-update) | async-done | bytes 4194320 | tf_op jit(solution)/shard_map/all_gather | solution.py:115
  83.8 3.6 %convolution_bitcast_fusion.1 = f32[512,128]{1,0:T(8,128)S(1)} fusion(bf16[16,512,256]{2,1,0:T(8,128)(2,1)} %all-gather.5.cloned.1.call-done, bf16[16,256,128]{2,1,0:T(8,128)(2,1)S(1)} %bitcast.131), kind=kOutput, calls=%fused_computation.11 | convolution fusion | flops 536870912 | bytes 5505024 | tf_op jit(solution)/shard_map/ksc,kch->sh/dot_general | solution.py:183
  87.5 1.2 fusion.15
  88.8 0.6 slice_bitcast_fusion.2
  89.5 0.6 pad_maximum_fusion.1
  90.2 0.7 copy.97
  90.8 0.5 copy.98
  91.4 36.3 %all_to_all.37 = bf16[128,16,256]{2,0,1:T(8,128)(2,1)S(1)} all-to-all(bf16[128,16,256]{2,0,1:T(8,128)(2,1)S(1)} %copy.98), channel_id=1, replica_groups=mesh['kv'=16,'ep'=32] {'kv'}, dimensions={1} | all-to-all | bytes 2097152 | tf_op jit(solution)/shard_map/all_to_all | solution.py:81
  127.7 6.1 %all-gather.7.cloned.1.call-done = bf16[16,256,128]{2,1,0:T(8,128)(2,1)} async-done(((bf16[1,256,128]{2,1,0:T(8,128)(2,1)}), bf16[16,256,128]{2,1,0:T(8,128)(2,1)}) %all-gather.7.cloned.1.call-update) | async-done | bytes 1048592 | tf_op jit(solution)/shard_map/all_gather | solution.py:200
  133.8 2.3 %fusion.14 = bf16[32,8,256]{2,1,0:T(8,128)(2,1)} fusion(bf16[128,16,256]{2,0,1:T(8,128)(2,1)S(1)} %all_to_all.37, bf16[16,256,128]{2,1,0:T(8,128)(2,1)} %all-gather.7.cloned.1.call-done), kind=kOutput, calls=%fused_computation.16 | convolution fusion | flops 268500992 | bytes 2228224 | tf_op jit(solution)/shard_map/ksh,khc->sc/dot_general | solution.py:206
  136.1 8.6 %all-to-all-start.4 = ((bf16[32,8,256]{2,1,0:T(8,128)(2,1)}), bf16[32,8,256]{2,1,0:T(8,128)(2,1)S(1)}, u32[]{:S(2)}, u32[]{:S(2)}) async-start(bf16[32,8,256]{2,1,0:T(8,128)(2,1)} %fusion.14), calls=%async_computation.4 | async-start | bytes 262144 | tf_op jit(solution)/shard_map/all_to_all | solution.py:209
  144.7 30.7 %all-gather.9.cloned.1.call-done = bf16[5120,128]{1,0:T(8,128)(2,1)} async-done(((bf16[320,128]{1,0:T(8,128)(2,1)}), bf16[5120,128]{1,0:T(8,128)(2,1)}) %all-gather.9.cloned.1.call-update) | async-done | bytes 1310736 | tf_op jit(solution)/shard_map/all_gather | solution.py:191
  175.4 2.3 %fusion.13 = bf16[32,8,256]{2,1,0:T(8,128)(2,1)} fusion(bf16[16,320,128]{2,1,0:T(8,128)(2,1)} %bitcast.142, bf16[128,16,256]{2,0,1:T(8,128)(2,1)S(1)} %all_to_all.37), kind=kOutput, calls=%fused_computation.15 | convolution fusion | flops 268500992 | bytes 2228224 | tf_op jit(solution)/shard_map/ksh,khc->sc/dot_general | solution.py:206
  177.8 9.3 %all-to-all-start.3 = ((bf16[32,8,256]{2,1,0:T(8,128)(2,1)}), bf16[32,8,256]{2,1,0:T(8,128)(2,1)S(1)}, u32[]{:S(2)}, u32[]{:S(2)}) async-start(bf16[32,8,256]{2,1,0:T(8,128)(2,1)} %fusion.13), calls=%async_computation.3 | async-start | bytes 262144 | tf_op jit(solution)/shard_map/all_to_all | solution.py:209
  187.1 1.0 slice.72
  188.1 0.8 reshape.344
  188.9 7.4 %all-to-all-done.3 = bf16[32,8,256]{2,1,0:T(8,128)(2,1)S(1)} async-done(((bf16[32,8,256]{2,1,0:T(8,128)(2,1)}), bf16[32,8,256]{2,1,0:T(8,128)(2,1)S(1)}, u32[]{:S(2)}, u32[]{:S(2)}) %all-to-all-start.3) | async-done | bytes 131104 | tf_op jit(solution)/shard_map/all_to_all | solution.py:209
  196.3 0.9 convolution_convert_fusion.1
  (68 shorter events, 4.0 us)
Async XLA Ops:
  7.2 76.6 %copy-start = (bf16[1,4096,128]{2,1,0:T(8,128)(2,1)S(1)}, bf16[1,4096,128]{2,1,0:T(8,128)(2,1)}, u32[]{:S(2)}) copy-start(bf16[1,4096,128]{2,1,0:T(8,128)(2,1)} %param.23) | copy-start | bytes 3145732
  7.2 25.3 %copy-start.3 = (bf16[1,4,128,512]{3,2,1,0:T(8,128)(2,1)S(1)}, bf16[1,4,128,512]{3,2,1,0:T(8,128)(2,1)}, u32[]{:S(2)}) copy-start(bf16[1,4,128,512]{3,2,1,0:T(8,128)(2,1)} %param.16) | copy-start | bytes 1572868
  7.2 76.6 %all-gather.5.cloned.1.call-start = ((), (), s32[]{:S(2)}) async-start(), calls=%async_computation.5 | async-start | bytes 4456448 | tf_op jit(solution)/shard_map/all_gather | solution.py:115
  8.4 24.3 %copy-start.6 = (s32[1,64]{1,0:T(1,128)S(1)}, s32[1,64]{1,0:T(1,128)}, u32[]{:S(2)}) copy-start(s32[1,64]{1,0:T(1,128)} %param.18) | copy-start | bytes 772
  30.7 103.1 %all-gather.7.cloned.1.call-start = ((), (), s32[]{:S(2)}) async-start(), calls=%async_computation.6 | async-start | bytes 1114112 | tf_op jit(solution)/shard_map/all_gather | solution.py:200
  37.1 3.4 %copy-start.4 = (bf16[1,4,128,512]{3,2,1,0:T(8,128)(2,1)S(1)}, bf16[1,4,128,512]{3,2,1,0:T(8,128)(2,1)}, u32[]{:S(2)}) copy-start(bf16[1,4,128,512]{3,2,1,0:T(8,128)(2,1)} %param.17) | copy-start | bytes 1572868
  83.8 3.6 %copy-start.1 = (bf16[16,512,256]{2,1,0:T(8,128)(2,1)S(1)}, bf16[16,512,256]{2,1,0:T(8,128)(2,1)}, u32[]{:S(2)}) copy-start(bf16[16,512,256]{2,1,0:T(8,128)(2,1)} %all-gather.5.cloned.1.call-done) | copy-start | bytes 12582916
  83.8 3.7 %copy-start.5 = (bf16[1,4096,128]{2,1,0:T(8,128)(2,1)S(1)}, bf16[1,4096,128]{2,1,0:T(8,128)(2,1)}, u32[]{:S(2)}) copy-start(bf16[1,4096,128]{2,1,0:T(8,128)(2,1)} %param.24) | copy-start | bytes 3145732
  87.5 2.7 %copy-start.2 = (bf16[1,128,4096]{2,1,0:T(8,128)(2,1)S(1)}, bf16[1,128,4096]{2,1,0:T(8,128)(2,1)}, u32[]{:S(2)}) copy-start(bf16[1,128,4096]{2,1,0:T(8,128)(2,1)} %param.25) | copy-start | bytes 3145732
  89.4 86.0 %all-gather.9.cloned.1.call-start = ((), (), s32[]{:S(2)}) async-start(), calls=%async_computation.7 | async-start | bytes 1392640 | tf_op jit(solution)/shard_map/all_gather | solution.py:191
  136.1 41.7 %all-to-all-start.4 = ((bf16[32,8,256]{2,1,0:T(8,128)(2,1)}), bf16[32,8,256]{2,1,0:T(8,128)(2,1)S(1)}, u32[]{:S(2)}, u32[]{:S(2)}) async-start(bf16[32,8,256]{2,1,0:T(8,128)(2,1)} %fusion.14), calls=%async_computation.4 | async-start | bytes 262144 | tf_op jit(solution)/shard_map/all_to_all | solution.py:209
  177.8 18.5 %all-to-all-start.3 = ((bf16[32,8,256]{2,1,0:T(8,128)(2,1)}), bf16[32,8,256]{2,1,0:T(8,128)(2,1)S(1)}, u32[]{:S(2)}, u32[]{:S(2)}) async-start(bf16[32,8,256]{2,1,0:T(8,128)(2,1)} %fusion.13), calls=%async_computation.3 | async-start | bytes 262144 | tf_op jit(solution)/shard_map/all_to_all | solution.py:209
Sparse Core Ops, SparseCore 0:
  30.8 52.8 all-gather.4
  89.5 44.1 all-gather.6
  135.9 39.4 all-gather.8
